TPU v7x, 512 devices: a whole 4x4x16 slice. The times are simulated.
512 devices in a mesh: seq: 64 (over x, z), head: 8 (over y, core).
Axes of the slice: x: 4, y: 4, z: 16, core: 2. Of those that a mesh axis runs over, the one named last changes fastest.
Arguments:
- queries: bfloat16 [8192, 4096], P('seq', 'head'), may hold values from -6 to 6
- keys: bfloat16 [8192, 4096], P('seq', 'head'), may hold values from -6 to 6
- values: bfloat16 [8192, 4096], P('seq', 'head'), may hold values from -6 to 6
- log_decay: float32 [8192, 32], P('seq', 'head'), may hold values from -0.75 to 0
- norm_gain: float32 [4096], P('head'), may hold values from 0.1 to 1.9
- out_weight: bfloat16 [4096, 4096], P('head'), may hold values from -0.125 to 0.125
- steer_ids: int32 [8192], P('seq'), may hold values from 0 to 15
- steer_table: bfloat16 [16, 4096], P(None, 'head'), may hold values from -3 to 3
Outputs:
- layer_out: bfloat16 [8192, 4096], P('seq', 'head')
All inputs are finite; a program needn't handle non-finite values.
Results may differ from a plain program's by a relative error of at most 0.0052.
Values sent between devices are 32-bit elements; how exact they have to be, the bound alone decides.
No kernel may reach another device: no remote copies, remote signals or barrier semaphores. Data moves between devices by JAX's collectives and lax.ppermute only.
A program may use at most 64 MiB of HBM per device.

v0:
```python
import jax
import jax.numpy as jnp
from jax import lax
from jax.sharding import PartitionSpec as P

SPAN = 128


def prefix(part, axis, combine, identity):
    place = lax.axis_index(axis)
    gathered = jax.tree.map(lambda a: lax.all_gather(a, axis), part)
    state = jax.tree.map(lambda a, e: jnp.zeros_like(a) + jnp.asarray(e, a.dtype), part, identity)

    def one(step, state):
        return combine(
            state, jax.tree.map(lambda a: lax.dynamic_index_in_dim(a, step, 0, False), gathered)
        )

    return lax.fori_loop(0, place, one, state)


def block_step(state, inputs):
    query, key_blk, value_blk, decay = inputs
    cum = jnp.cumsum(decay, axis=1)
    size = decay.shape[1]
    rows = lax.broadcasted_iota(jnp.int32, (size, size), 0)
    cols = lax.broadcasted_iota(jnp.int32, (size, size), 1)
    lower = (cols <= rows)[None]
    scores = jnp.einsum("hte,hse->hts", query, key_blk, preferred_element_type=jnp.float32)
    diffs = jnp.where(lower, cum[:, :, None] - cum[:, None, :], 0.0)
    block_weights = (jnp.where(lower, jnp.exp(diffs), 0.0) * scores).astype(jnp.bfloat16)
    intra = jnp.einsum("hts,hse->hte", block_weights, value_blk, preferred_element_type=jnp.float32)
    inter = jnp.exp(cum)[:, :, None] * jnp.einsum(
        "hte,hef->htf", query.astype(jnp.float32), state, precision=lax.Precision.HIGHEST
    )
    total = cum[:, -1]
    scaled_keys = key_blk.astype(jnp.float32) * jnp.exp(total[:, None] - cum)[:, :, None]
    update = jnp.einsum(
        "hse,hsf->hef", scaled_keys, value_blk.astype(jnp.float32), precision=lax.Precision.HIGHEST
    )
    new_state = jnp.exp(total)[:, None, None] * state + update
    return (new_state, intra + inter)


def join_memory(earlier, later):
    return (earlier[0] + later[0], jnp.exp(later[0])[:, None, None] * earlier[1] + later[1])


def shards(queries, keys, values, log_decay, norm_gain, out_weight, steer_ids, steer_table):
    tok_rows, features = queries.shape
    heads_here = log_decay.shape[1]
    head_size = features // heads_here
    count = tok_rows // SPAN

    def split(array):
        return array.reshape(count, SPAN, heads_here, head_size).transpose(0, 2, 1, 3)

    decays = log_decay.reshape(count, SPAN, heads_here).transpose(0, 2, 1)
    start = jnp.zeros((heads_here, head_size, head_size), jnp.float32)
    local_memory, blocks = lax.scan(
        block_step, start, (split(queries), split(keys), split(values), decays)
    )
    device_log = jnp.sum(log_decay, axis=0)
    identity = (jnp.zeros((heads_here,), jnp.float32), start)
    passed = prefix((device_log, local_memory), "seq", join_memory, identity)
    earlier_memory = passed[1]
    running = jnp.cumsum(log_decay, axis=0)
    query_heads = queries.reshape(tok_rows, heads_here, head_size).astype(jnp.float32)
    carried = jnp.exp(running)[:, :, None] * jnp.einsum(
        "the,hef->thf", query_heads, earlier_memory, precision=lax.Precision.HIGHEST
    )
    attended = blocks.transpose(0, 2, 1, 3).reshape(tok_rows, heads_here, head_size) + carried
    mean_sq = jnp.mean(attended * attended, axis=-1, keepdims=True)
    normed = (attended * lax.rsqrt(mean_sq + 1e-06)).reshape(tok_rows, features) * norm_gain
    normed = normed.astype(jnp.bfloat16)
    partial_term = jnp.dot(normed, out_weight, preferred_element_type=jnp.float32)
    onehot = (
        steer_ids[:, None] == jnp.arange(steer_table.shape[0], dtype=jnp.int32)[None, :]
    ).astype(jnp.bfloat16)
    steering = jnp.dot(onehot, steer_table, preferred_element_type=jnp.float32)
    whole_sum = lax.psum(partial_term, "head")
    column_width = steer_table.shape[1]
    summed = lax.dynamic_slice_in_dim(
        whole_sum, lax.axis_index("head") * column_width, column_width, 1
    )
    return (summed + steering).astype(jnp.bfloat16)


def solution(mesh):
    in_specs = (
        P("seq", "head"),
        P("seq", "head"),
        P("seq", "head"),
        P("seq", "head"),
        P("head"),
        P("head", None),
        P("seq"),
        P(None, "head"),
    )
    out_specs = P("seq", "head")
    return jax.shard_map(shards, mesh=mesh, in_specs=in_specs, out_specs=out_specs, check_vma=False)
```

profile of v0, /device:TPU:6, one launch (start us, length us, event | category | flops | bytes accessed | tf_op | source)
XLA Modules:
  0.0 363.2 jit_solution(9025703200872860775)
XLA Ops:
  13.4 1.3 dynamic-slice.5
  15.6 130.0 %all-reduce = f32[256]{0:T(256)S(1)} all-reduce(f32[256]{0:T(256)S(1)} %dynamic-update-slice), channel_id=2, replica_groups=mesh['seq'=64,'head'=8] {'seq'}, use_global_device_ids=true, to_apply=%add | all-reduce | flops 256 | bytes 2048
  146.7 60.6 %all-gather.4.cloned.1.call-done = f32[256,128,128]{2,1,0:T(8,128)} async-done(((f32[4,128,128]{2,1,0:T(8,128)}), f32[256,128,128]{2,1,0:T(8,128)}) %all-gather.4.cloned.1.call-update) | async-done | bytes 16777232 | tf_op jit(solution)/shard_map/all_gather | solution.py:11
  207.4 53.0 %while.3 = (s32[]{:T(128)}, f32[4,128,128]{2,1,0:T(8,128)S(1)}, s32[]{:T(128)}, f32[64,4]{1,0:T(8,128)S(1)}, f32[64,4,128,128]{3,2,1,0:T(8,128)}, /*index=5*/s32[]{:T(128)}, s32[]{:T(128)}, s32[]{:T(128)}) while((s32[]{:T(128)}, f32[4,128,128]{2,1,0:T(8,128)S(1)}, s32[]{:T(128)}, f32[64,4]{1,0:T(8,128)S(1)}, f32[64,4,128,128]{3,2,1,0:T(8,128)}, ...), condition=%wide.region_4.5_spmd, body=%wide.region_3.4_spmd.sunk | while | flops 131077 | bytes 786615 | solution.py:19
  209.6 1.1 bitcast_add_fusion.2
  210.7 1.1 bitcast_add_fusion.2
  211.8 1.1 bitcast_add_fusion.2
  212.9 1.1 bitcast_add_fusion.2
  216.2 1.1 bitcast_add_fusion.2
  217.3 1.1 bitcast_add_fusion.2
  218.5 1.1 bitcast_add_fusion.2
  219.6 1.1 bitcast_add_fusion.2
  222.9 1.1 bitcast_add_fusion.2
  224.0 1.1 bitcast_add_fusion.2
  225.1 1.1 bitcast_add_fusion.2
  226.2 1.1 bitcast_add_fusion.2
  230.6 1.1 bitcast_add_fusion.2
  231.7 1.1 bitcast_add_fusion.2
  232.8 1.1 bitcast_add_fusion.2
  233.9 1.1 bitcast_add_fusion.2
  237.2 1.1 bitcast_add_fusion.2
  261.0 4.2 %fusion.36 = f32[128,4096]{1,0:T(8,128)} fusion(bf16[128,512]{0,1:T(8,128)(2,1)S(1)} %fusion.8, bf16[512,4096]{1,0:T(8,128)(2,1)} %param.15), kind=kOutput, calls=%fused_computation.50 | convolution fusion | flops 536870912 | bytes 6422528 | tf_op jit(solution)/shard_map/dot_general | solution.py:76
  265.3 89.3 %all-reduce.3.cloned.1.call-done = f32[128,4096]{1,0:T(8,128)} async-done(((f32[128,4096]{1,0:T(8,128)}), f32[128,4096]{1,0:T(8,128)}) %all-reduce.3.cloned.1.call-update) | async-done | bytes 2097168 | tf_op jit(solution)/shard_map/psum | solution.py:81
  354.6 1.8 fusion.6
  (115 shorter events, 42.4 us)
Async XLA Ops:
  6.5 348.0 %copy-start = (bf16[16,512]{1,0:T(8,128)(2,1)S(1)}, bf16[16,512]{1,0:T(8,128)(2,1)}, u32[]{:S(2)}) copy-start(bf16[16,512]{1,0:T(8,128)(2,1)} %param.17) | copy-start | bytes 49156
  6.5 253.9 %copy-start.1 = (bf16[128,512]{1,0:T(8,128)(2,1)S(1)}, bf16[128,512]{1,0:T(8,128)(2,1)}, u32[]{:S(2)}) copy-start(bf16[128,512]{1,0:T(8,128)(2,1)} %param.10) | copy-start | bytes 393220
  6.5 200.8 %all-gather.4.cloned.1.call-start = ((), (), s32[]{:S(2)}) async-start(), calls=%async_computation.1 | async-start | bytes 17039360 | tf_op jit(solution)/shard_map/all_gather | solution.py:11
  10.8 250.1 %copy-start.2 = (f32[512]{0:T(512)S(1)}, f32[512]{0:T(512)}, u32[]{:S(2)}) copy-start(f32[512]{0:T(512)} %param.14) | copy-start | bytes 6148
  10.8 343.8 %all-reduce.3.cloned.1.call-start = ((), (), s32[]{:S(2)}) async-start(), calls=%async_computation | async-start | bytes 4194304 | tf_op jit(solution)/shard_map/psum | solution.py:81
  261.0 93.6 %copy-start.3 = (s32[128]{0:T(128)S(1)}, s32[128]{0:T(128)}, u32[]{:S(2)}) copy-start(s32[128]{0:T(128)} %param.16) | copy-start | bytes 1540
Sparse Core Ops, SparseCore 0:
  10.9 196.3 all-gather.3
  265.4 89.1 all-reduce.2
where the time goes:
time: 366 us; the launch traced here: 363 us
  waiting for transfers between devices  150 us (41%)
  blocking collectives  130 us (36%)
  other arithmetic  53.2 us (15%)
  between operations  14.2 us (4%)
  matrix products  8.18 us (2%)
  local copies, waits for them, and re-layouts  6.36 us (2%)
    unnamed x1, blocking collectives  130 us
    psum x1, waiting for transfers between devices, shards(): whole_sum = lax.psum(partial_term, 'head')  89.3 us
    all_gather x1, waiting for transfers between devices, prefix(): gathered = jax.tree.map(lambda a: lax.all_gather(a, axis), part)  60.6 us
    add x48, other arithmetic, join_memory(): jnp.exp(later[0])[:, None, None] * earlier[1] + later[1]  50.9 us
  transfers between devices with their start and end apart: 2, of which 2 were waited for; matrix products, arithmetic and copies ran while one was open for 1% of the time, Pallas kernels for 0%

commit v1 on v0

--- a/solution.py
+++ b/solution.py
@@ -1,22 +1,10 @@
 import jax
 import jax.numpy as jnp
+import numpy as np
 from jax import lax
 from jax.sharding import PartitionSpec as P
 
 SPAN = 128
-
-
-def prefix(part, axis, combine, identity):
-    place = lax.axis_index(axis)
-    gathered = jax.tree.map(lambda a: lax.all_gather(a, axis), part)
-    state = jax.tree.map(lambda a, e: jnp.zeros_like(a) + jnp.asarray(e, a.dtype), part, identity)
-
-    def one(step, state):
-        return combine(
-            state, jax.tree.map(lambda a: lax.dynamic_index_in_dim(a, step, 0, False), gathered)
-        )
-
-    return lax.fori_loop(0, place, one, state)
 
 
 def block_step(state, inputs):
@@ -46,7 +34,84 @@
     return (earlier[0] + later[0], jnp.exp(later[0])[:, None, None] * earlier[1] + later[1])
 
 
-def shards(queries, keys, values, log_decay, norm_gain, out_weight, steer_ids, steer_table):
+def scan_rounds(n):
+    top = 1
+    while top < n:
+        top *= 2
+    levels = top.bit_length() - 1
+    ups = []
+    for k in range(levels):
+        step = 1 << k
+        ups.append([(p - step, p) for p in range(2 * step - 1, n, 2 * step)])
+    downs = []
+    for k in range(levels - 1, -1, -1):
+        step = 1 << k
+        downs.append([(p - step, p) for p in range(3 * step - 1, n, 2 * step)])
+    rounds = ups[:-1]
+    tail = ups[-1] if ups else []
+    downs = [d for d in downs if d]
+    if tail and downs and all(s == tail[0][0] for s, _ in tail) and downs[0][0][0] == tail[0][0]:
+        rounds.append(tail + downs[0])
+        rounds.extend(downs[1:])
+    else:
+        if tail:
+            rounds.append(tail)
+        rounds.extend(downs)
+    return [r for r in rounds if r]
+
+
+def exclusive_scan(part, axis, n):
+    place = lax.axis_index(axis)
+    held = part
+    before = (jnp.zeros_like(part[0]), jnp.zeros_like(part[1]))
+    for pairs in scan_rounds(n):
+        table = np.zeros((n,), np.bool_)
+        for _, dst in pairs:
+            table[dst] = True
+        takes = jnp.asarray(table)[place]
+        groups = []
+        for pair in pairs:
+            for group in groups:
+                if all(pair[0] != other[0] for other in group):
+                    group.append(pair)
+                    break
+            else:
+                groups.append([pair])
+        got = None
+        for group in groups:
+            one = (lax.ppermute(held[0], axis, group), lax.ppermute(held[1], axis, group))
+            got = one if got is None else jax.tree.map(jnp.add, got, one)
+        new_held = join_memory(got, held)
+        new_before = join_memory(got, before)
+        held = jax.tree.map(lambda a, b: jnp.where(takes, a, b), new_held, held)
+        before = jax.tree.map(lambda a, b: jnp.where(takes, a, b), new_before, before)
+    return before
+
+
+def scatter_heads(partial, axis, n):
+    rows, total_cols = partial.shape
+    width = total_cols // n
+    place = lax.axis_index(axis)
+    if n % 2 == 0 and n > 2:
+        chips = n // 2
+        core = place % 2
+        chip = place // 2
+        blocks = partial.reshape(rows, chips, 2, width)
+        keep = jnp.where(core == 0, blocks[:, :, 0], blocks[:, :, 1])
+        away = jnp.where(core == 0, blocks[:, :, 1], blocks[:, :, 0])
+        pairs = [(h, h ^ 1) for h in range(n)]
+        mine = keep + lax.ppermute(away, axis, pairs)
+        out = lax.dynamic_index_in_dim(mine, chip, 1, False)
+        for shift in range(1, chips):
+            send = lax.dynamic_index_in_dim(mine, (chip + shift) % chips, 1, False)
+            pairs = [(2 * y + c, 2 * ((y + shift) % chips) + c) for y in range(chips) for c in range(2)]
+            out = out + lax.ppermute(send, axis, pairs)
+        return out
+    whole = lax.psum(partial, axis)
+    return lax.dynamic_slice_in_dim(whole, place * width, width, 1)
+
+
+def shards(queries, keys, values, log_decay, norm_gain, out_weight, steer_ids, steer_table, seq_n, head_n):
     tok_rows, features = queries.shape
     heads_here = log_decay.shape[1]
     head_size = features // heads_here
@@ -61,8 +126,7 @@
         block_step, start, (split(queries), split(keys), split(values), decays)
     )
     device_log = jnp.sum(log_decay, axis=0)
-    identity = (jnp.zeros((heads_here,), jnp.float32), start)
-    passed = prefix((device_log, local_memory), "seq", join_memory, identity)
+    passed = exclusive_scan((device_log, local_memory), "seq", seq_n)
     earlier_memory = passed[1]
     running = jnp.cumsum(log_decay, axis=0)
     query_heads = queries.reshape(tok_rows, heads_here, head_size).astype(jnp.float32)
@@ -78,11 +142,7 @@
         steer_ids[:, None] == jnp.arange(steer_table.shape[0], dtype=jnp.int32)[None, :]
     ).astype(jnp.bfloat16)
     steering = jnp.dot(onehot, steer_table, preferred_element_type=jnp.float32)
-    whole_sum = lax.psum(partial_term, "head")
-    column_width = steer_table.shape[1]
-    summed = lax.dynamic_slice_in_dim(
-        whole_sum, lax.axis_index("head") * column_width, column_width, 1
-    )
+    summed = scatter_heads(partial_term, "head", head_n)
     return (summed + steering).astype(jnp.bfloat16)
 
 
@@ -98,4 +158,10 @@
         P(None, "head"),
     )
     out_specs = P("seq", "head")
-    return jax.shard_map(shards, mesh=mesh, in_specs=in_specs, out_specs=out_specs, check_vma=False)
+    seq_n = mesh.shape["seq"]
+    head_n = mesh.shape["head"]
+
+    def body(*args):
+        return shards(*args, seq_n=seq_n, head_n=head_n)
+
+    return jax.shard_map(body, mesh=mesh, in_specs=in_specs, out_specs=out_specs, check_vma=False)

time: 366 us -> 188 us (0.51)
  the two profiles are of different devices: /device:TPU:6 before, /device:TPU:77 now
where the time goes in v1:
time: 188 us; the launch traced here: 187 us
  waiting for transfers between devices  91.6 us (49%)
  starting transfers between devices  42.4 us (23%)
  other arithmetic  24.7 us (13%)
  local copies, waits for them, and re-layouts  17.9 us (10%)
  matrix products  9.78 us (5%)
    ppermute x11, waiting for transfers between devices, exclusive_scan(): lax.ppermute(held[1], axis, group)  77.2 us
    ppermute x1, starting transfers between devices, scatter_heads(): mine = keep + lax.ppermute(away, axis, pairs)  14.4 us
    exp x11, other arithmetic, join_memory(): jnp.exp(later[0])[:, None, None] * earlier[1] + later[1]  13.3 us
    ppermute x11, starting transfers between devices, exclusive_scan(): lax.ppermute(held[1], axis, group)  10.9 us
    ppermute x3, waiting for transfers between devices, scatter_heads(): out = out + lax.ppermute(send, axis, pairs)  10.4 us
    ppermute x3, starting transfers between devices, scatter_heads(): out = out + lax.ppermute(send, axis, pairs)  9.8 us
    dynamic_slice x10, local copies, waits for them, and re-layouts, exclusive_scan(): takes = jnp.asarray(table)[place]  8.85 us
    ppermute x10, starting transfers between devices, exclusive_scan(): lax.ppermute(held[0], axis, group)  7.31 us
  transfers between devices with their start and end apart: 25, of which 5 were waited for; matrix products, arithmetic and copies ran while one was open for 17% of the time, Pallas kernels for 0%

profile of v1, /device:TPU:77, one launch (start us, length us, event | category | flops | bytes accessed | tf_op | source)
XLA Modules:
  0.0 187.1 jit_solution(3560461194743123411)
XLA Ops:
  0.0 1.0 reduce_window_sum.23
  1.3 1.0 copy.53
  3.7 3.6 %collective-permute-start.10 = (f32[4,128,128]{2,1,0:T(8,128)S(1)}, f32[4,128,128]{2,1,0:T(8,128)S(1)}, u32[]{:S(2)}, u32[]{:S(2)}) collective-permute-start(f32[4,128,128]{2,1,0:T(8,128)S(1)} %convolution_add_fusion), channel_id=1, source_target_pairs={{0,8},{16,24},{32,40},{48,56},{64,72},{80,88},{96,104},{112,120},{... | collective-permute-start | bytes 786440 | tf_op jit(solution)/shard_map/ppermute | solution.py:82
  8.0 1.3 collective-permute-start
  9.3 1.2 dynamic_slice.74
  10.6 1.7 collective-permute-done
  14.3 1.3 dynamic_slice.73
  17.0 1.3 dynamic_slice.72
  21.0 1.3 dynamic_slice.71
  39.8 6.5 %copy.57 = bf16[4096,512]{1,0:T(8,128)(2,1)} copy(bf16[4096,512]{0,1:T(8,128)(2,1)} %bitcast.109) | data formatting | bytes 8388608 | tf_op jit(solution)/shard_map/dot_general | solution.py:140
  51.6 5.7 %fusion.70 = (f32[4]{0:T(128)S(1)}, f32[4]{0:T(128)S(1)}, f32[4]{0:T(128)S(1)}, f32[4]{0:T(128)S(1)}, f32[4]{0:T(128)S(1)}, /*index=5*/f32[4]{0:T(128)S(1)}) fusion(f32[4]{0:T(128)S(1)} %collective-permute-done.9, pred[]{:T(512)} %bitcast.18, f32[4]{0:T(128)S(1)} %collective-permute-done.8, pred[]{:T(512)} %bitcast.19, f32[4]{0:T(128)S(1)} %collective-permute-done.7, ...), kind=kLoop, calls=%fused_computation.120 | loop fusion | flops 72 | bytes 265 | tf_op jit(solution)/shard_map/exp | solution.py:34
  58.0 1.3 collective-permute-start.20
  59.9 1.4 fusion.75
  61.3 77.2 %collective-permute-done.20 = f32[4,128,128]{2,1,0:T(8,128)S(1)} collective-permute-done((f32[4,128,128]{2,1,0:T(8,128)S(1)}, f32[4,128,128]{2,1,0:T(8,128)S(1)}, u32[]{:S(2)}, u32[]{:S(2)}) %collective-permute-start.20) | collective-permute-done | bytes 262176 | tf_op jit(solution)/shard_map/ppermute | solution.py:82
  138.5 7.1 %multiply_reduce_fusion = (f32[128,4]{0,1:T(4,128)S(1)}, f32[128,4,128]{0,2,1:T(8,128)S(1)}) fusion(f32[128,4,128]{0,2,1:T(8,128)S(1)} %fusion.4, f32[4,128,128]{2,1,0:T(8,128)S(1)} %collective-permute-done.10, f32[4,128,128]{2,1,0:T(8,128)S(1)} %collective-permute-done.11, f32[4,128,128]{2,1,0:T(8,128)S(1)} %collective-permute-done.12, ...), kind=kOutput, calls=%fused_computation.42 | convolution fusion | flops 102825472 | bytes 3543194 | tf_op jit(solution)/shard_map/the,hef->thf/dot_general | solution.py:133
  145.7 1.5 fusion.86
  147.4 14.4 %collective-permute-start.21 = (f32[128,4,512]{2,0,1:T(8,128)S(1)}, f32[128,4,512]{2,0,1:T(8,128)}, u32[]{:S(2)}, u32[]{:S(2)}) collective-permute-start(f32[128,4,512]{2,0,1:T(8,128)S(1)} %select_bitcast_fusion), channel_id=1, source_target_pairs={{0,1},{1,0},{2,3},{3,2},{4,5},{5,4},{6,7},{7,6},{8,9},{9,8},{10,11... | collective-permute-start | bytes 3145736 | tf_op jit(solution)/shard_map/ppermute | solution.py:103
  161.9 2.3 %collective-permute-done.21 = f32[128,4,512]{2,0,1:T(8,128)} collective-permute-done((f32[128,4,512]{2,0,1:T(8,128)S(1)}, f32[128,4,512]{2,0,1:T(8,128)}, u32[]{:S(2)}, u32[]{:S(2)}) %collective-permute-start.21) | collective-permute-done | bytes 1048608 | tf_op jit(solution)/shard_map/ppermute | solution.py:103
  164.2 1.6 fusion.8
  165.8 3.2 %collective-permute-start.22 = (f32[128,512]{1,0:T(8,128)S(1)}, f32[128,512]{1,0:T(8,128)S(1)}, u32[]{:S(2)}, u32[]{:S(2)}) collective-permute-start(f32[128,512]{1,0:T(8,128)S(1)} %get-tuple-element.47), channel_id=1, source_target_pairs={{0,2},{1,3},{2,4},{3,5},{4,6},{5,7},{6,0},{7,1},{8,10},{9,11},{10,... | collective-permute-start | bytes 786440 | tf_op jit(solution)/shard_map/ppermute | solution.py:108
  169.0 2.6 %collective-permute-start.23 = (f32[128,512]{1,0:T(8,128)S(1)}, f32[128,512]{1,0:T(8,128)S(1)}, u32[]{:S(2)}, u32[]{:S(2)}) collective-permute-start(f32[128,512]{1,0:T(8,128)S(1)} %get-tuple-element.49), channel_id=1, source_target_pairs={{0,4},{1,5},{2,6},{3,7},{4,0},{5,1},{6,2},{7,3},{8,12},{9,13},{10,... | collective-permute-start | bytes 786440 | tf_op jit(solution)/shard_map/ppermute | solution.py:108
  171.7 4.0 %collective-permute-start.24 = (f32[128,512]{1,0:T(8,128)S(1)}, f32[128,512]{1,0:T(8,128)S(1)}, u32[]{:S(2)}, u32[]{:S(2)}) collective-permute-start(f32[128,512]{1,0:T(8,128)S(1)} %get-tuple-element.48), channel_id=1, source_target_pairs={{0,6},{1,7},{2,0},{3,1},{4,2},{5,3},{6,4},{7,5},{8,14},{9,15},{10,... | collective-permute-start | bytes 786440 | tf_op jit(solution)/shard_map/ppermute | solution.py:108
  175.9 3.8 %collective-permute-done.23 = f32[128,512]{1,0:T(8,128)S(1)} collective-permute-done((f32[128,512]{1,0:T(8,128)S(1)}, f32[128,512]{1,0:T(8,128)S(1)}, u32[]{:S(2)}, u32[]{:S(2)}) %collective-permute-start.23) | collective-permute-done | bytes 262176 | tf_op jit(solution)/shard_map/ppermute | solution.py:108
  179.7 6.6 %collective-permute-done.24 = f32[128,512]{1,0:T(8,128)S(1)} collective-permute-done((f32[128,512]{1,0:T(8,128)S(1)}, f32[128,512]{1,0:T(8,128)S(1)}, u32[]{:S(2)}, u32[]{:S(2)}) %collective-permute-start.24) | collective-permute-done | bytes 262176 | tf_op jit(solution)/shard_map/ppermute | solution.py:108
  (107 shorter events, 33.7 us)
Async XLA Ops:
  3.7 9.2 %collective-permute-start.10 = (f32[4,128,128]{2,1,0:T(8,128)S(1)}, f32[4,128,128]{2,1,0:T(8,128)S(1)}, u32[]{:S(2)}, u32[]{:S(2)}) collective-permute-start(f32[4,128,128]{2,1,0:T(8,128)S(1)} %convolution_add_fusion), channel_id=1, source_target_pairs={{0,8},{16,24},{32,40},{48,56},{64,72},{80,88},{96,104},{112,120},{... | collective-permute-start | bytes 786440 | tf_op jit(solution)/shard_map/ppermute | solution.py:82
  8.0 4.2 %collective-permute-start = (f32[4]{0:T(128)S(1)}, f32[4]{0:T(128)S(1)}, u32[]{:S(2)}, u32[]{:S(2)}) collective-permute-start(f32[4]{0:T(128)S(1)} %reduce_sum.18), channel_id=1, source_target_pairs={{0,8},{16,24},{32,40},{48,56},{64,72},{80,88},{96,104},{112,120},{... | collective-permute-start | bytes 56 | tf_op jit(solution)/shard_map/ppermute | solution.py:82
  13.6 1.9 %collective-permute-start.11 = (f32[4,128,128]{2,1,0:T(8,128)S(1)}, f32[4,128,128]{2,1,0:T(8,128)S(1)}, u32[]{:S(2)}, u32[]{:S(2)}) collective-permute-start(f32[4,128,128]{2,1,0:T(8,128)S(1)} %add_select_fusion.17), channel_id=1, source_target_pairs={{8,24},{40,56},{72,88},{104,120},{136,152},{168,184},{200,216},{23... | collective-permute-start | bytes 786440 | tf_op jit(solution)/shard_map/ppermute | solution.py:82
  16.3 3.3 %collective-permute-start.12 = (f32[4,128,128]{2,1,0:T(8,128)S(1)}, f32[4,128,128]{2,1,0:T(8,128)S(1)}, u32[]{:S(2)}, u32[]{:S(2)}) collective-permute-start(f32[4,128,128]{2,1,0:T(8,128)S(1)} %add_select_fusion.16), channel_id=1, source_target_pairs={{24,56},{88,120},{152,184},{216,248},{280,312},{344,376},{408,440}... | collective-permute-start | bytes 786440 | tf_op jit(solution)/shard_map/ppermute | solution.py:82
  18.3 0.7 collective-permute-start.1
  20.3 3.3 %collective-permute-start.13 = (f32[4,128,128]{2,1,0:T(8,128)S(1)}, f32[4,128,128]{2,1,0:T(8,128)S(1)}, u32[]{:S(2)}, u32[]{:S(2)}) collective-permute-start(f32[4,128,128]{2,1,0:T(8,128)S(1)} %add_select_fusion.15), channel_id=1, source_target_pairs={{56,120},{184,248},{312,376},{440,504},{57,121},{185,249},{313,377... | collective-permute-start | bytes 786440 | tf_op jit(solution)/shard_map/ppermute | solution.py:82
  22.3 0.7 collective-permute-start.2
  24.4 2.7 %collective-permute-start.14 = (f32[4,128,128]{2,1,0:T(8,128)S(1)}, f32[4,128,128]{2,1,0:T(8,128)S(1)}, u32[]{:S(2)}, u32[]{:S(2)}) collective-permute-start(f32[4,128,128]{2,1,0:T(8,128)S(1)} %add_select_fusion.14), channel_id=1, source_target_pairs={{120,248},{376,504},{121,249},{377,505},{122,250},{378,506},{123,2... | collective-permute-start | bytes 786440 | tf_op jit(solution)/shard_map/ppermute | solution.py:82
  27.9 3.5 %collective-permute-start.15 = (f32[4,128,128]{2,1,0:T(8,128)S(1)}, f32[4,128,128]{2,1,0:T(8,128)S(1)}, u32[]{:S(2)}, u32[]{:S(2)}) collective-permute-start(f32[4,128,128]{2,1,0:T(8,128)S(1)} %add_select_fusion.13), channel_id=1, source_target_pairs={{248,504},{249,505},{250,506},{251,507},{252,508},{253,509},{254,5... | collective-permute-start | bytes 786440 | tf_op jit(solution)/shard_map/ppermute | solution.py:82
  28.5 2.8 %collective-permute-start.16 = (f32[4,128,128]{2,1,0:T(8,128)S(1)}, f32[4,128,128]{2,1,0:T(8,128)S(1)}, u32[]{:S(2)}, u32[]{:S(2)}) collective-permute-start(f32[4,128,128]{2,1,0:T(8,128)S(1)} %add_select_fusion.13), channel_id=1, source_target_pairs={{248,376},{249,377},{250,378},{251,379},{252,380},{253,381},{254,3... | collective-permute-start | bytes 786440 | tf_op jit(solution)/shard_map/ppermute | solution.py:82
  30.0 0.7 collective-permute-start.4
  32.2 3.7 %collective-permute-start.17 = (f32[4,128,128]{2,1,0:T(8,128)S(1)}, f32[4,128,128]{2,1,0:T(8,128)S(1)}, u32[]{:S(2)}, u32[]{:S(2)}) collective-permute-start(f32[4,128,128]{2,1,0:T(8,128)S(1)} %add_select_fusion.12), channel_id=1, source_target_pairs={{120,184},{248,312},{376,440},{121,185},{249,313},{377,441},{122,1... | collective-permute-start | bytes 786440 | tf_op jit(solution)/shard_map/ppermute | solution.py:82
  33.8 1.3 collective-permute-start.5
  34.4 0.7 collective-permute-start.6
  36.5 12.3 %collective-permute-start.18 = (f32[4,128,128]{2,1,0:T(8,128)S(1)}, f32[4,128,128]{2,1,0:T(8,128)S(1)}, u32[]{:S(2)}, u32[]{:S(2)}) collective-permute-start(f32[4,128,128]{2,1,0:T(8,128)S(1)} %add_select_fusion.11), channel_id=1, source_target_pairs={{56,88},{120,152},{184,216},{248,280},{312,344},{376,408},{440,472... | collective-permute-start | bytes 786440 | tf_op jit(solution)/shard_map/ppermute | solution.py:82
  46.3 0.8 collective-permute-start.7
  48.1 2.1 %collective-permute-start.8 = (f32[4]{0:T(128)S(1)}, f32[4]{0:T(128)S(1)}, u32[]{:S(2)}, u32[]{:S(2)}) collective-permute-start(f32[4]{0:T(128)S(1)} %get-tuple-element.34), channel_id=1, source_target_pairs={{56,88},{120,152},{184,216},{248,280},{312,344},{376,408},{440,472... | collective-permute-start | bytes 56 | tf_op jit(solution)/shard_map/ppermute | solution.py:82
  49.5 7.7 %collective-permute-start.19 = (f32[4,128,128]{2,1,0:T(8,128)S(1)}, f32[4,128,128]{2,1,0:T(8,128)S(1)}, u32[]{:S(2)}, u32[]{:S(2)}) collective-permute-start(f32[4,128,128]{2,1,0:T(8,128)S(1)} %add_select_fusion.10), channel_id=1, source_target_pairs={{24,40},{56,72},{88,104},{120,136},{152,168},{184,200},{216,232},{... | collective-permute-start | bytes 786440 | tf_op jit(solution)/shard_map/ppermute | solution.py:82
  50.9 0.7 collective-permute-start.9
  58.0 80.5 %collective-permute-start.20 = (f32[4,128,128]{2,1,0:T(8,128)S(1)}, f32[4,128,128]{2,1,0:T(8,128)S(1)}, u32[]{:S(2)}, u32[]{:S(2)}) collective-permute-start(f32[4,128,128]{2,1,0:T(8,128)S(1)} %add_select_fusion.9), channel_id=1, source_target_pairs={{8,16},{24,32},{40,48},{56,64},{72,80},{88,96},{104,112},{120,128}... | collective-permute-start | bytes 786440 | tf_op jit(solution)/shard_map/ppermute | solution.py:82
  147.4 16.8 %collective-permute-start.21 = (f32[128,4,512]{2,0,1:T(8,128)S(1)}, f32[128,4,512]{2,0,1:T(8,128)}, u32[]{:S(2)}, u32[]{:S(2)}) collective-permute-start(f32[128,4,512]{2,0,1:T(8,128)S(1)} %select_bitcast_fusion), channel_id=1, source_target_pairs={{0,1},{1,0},{2,3},{3,2},{4,5},{5,4},{6,7},{7,6},{8,9},{9,8},{10,11... | collective-permute-start | bytes 3145736 | tf_op jit(solution)/shard_map/ppermute | solution.py:103
  165.8 10.1 %collective-permute-start.22 = (f32[128,512]{1,0:T(8,128)S(1)}, f32[128,512]{1,0:T(8,128)S(1)}, u32[]{:S(2)}, u32[]{:S(2)}) collective-permute-start(f32[128,512]{1,0:T(8,128)S(1)} %get-tuple-element.47), channel_id=1, source_target_pairs={{0,2},{1,3},{2,4},{3,5},{4,6},{5,7},{6,0},{7,1},{8,10},{9,11},{10,... | collective-permute-start | bytes 786440 | tf_op jit(solution)/shard_map/ppermute | solution.py:108
  169.0 10.6 %collective-permute-start.23 = (f32[128,512]{1,0:T(8,128)S(1)}, f32[128,512]{1,0:T(8,128)S(1)}, u32[]{:S(2)}, u32[]{:S(2)}) collective-permute-start(f32[128,512]{1,0:T(8,128)S(1)} %get-tuple-element.49), channel_id=1, source_target_pairs={{0,4},{1,5},{2,6},{3,7},{4,0},{5,1},{6,2},{7,3},{8,12},{9,13},{10,... | collective-permute-start | bytes 786440 | tf_op jit(solution)/shard_map/ppermute | solution.py:108
  171.7 14.6 %collective-permute-start.24 = (f32[128,512]{1,0:T(8,128)S(1)}, f32[128,512]{1,0:T(8,128)S(1)}, u32[]{:S(2)}, u32[]{:S(2)}) collective-permute-start(f32[128,512]{1,0:T(8,128)S(1)} %get-tuple-element.48), channel_id=1, source_target_pairs={{0,6},{1,7},{2,0},{3,1},{4,2},{5,3},{6,4},{7,5},{8,14},{9,15},{10,... | collective-permute-start | bytes 786440 | tf_op jit(solution)/shard_map/ppermute | solution.py:108
  (13 other events, 660.9 us)

commit v2 on v1

--- a/solution.py
+++ b/solution.py
@@ -30,11 +30,20 @@
     return (new_state, intra + inter)
 
 
-def join_memory(earlier, later):
-    return (earlier[0] + later[0], jnp.exp(later[0])[:, None, None] * earlier[1] + later[1])
-
-
-def scan_rounds(n):
+def pack(log_total, memory):
+    heads, rows, cols = memory.shape
+    extra = jnp.broadcast_to(log_total[:, None, None], (heads, 8, cols))
+    return jnp.concatenate([memory, extra], axis=1)
+
+
+def join(earlier, later):
+    rows = earlier.shape[1] - 8
+    row = lax.broadcasted_iota(jnp.int32, earlier.shape, 1)
+    scale = jnp.where(row < rows, jnp.exp(later[:, rows:rows + 1, :]), 1.0)
+    return scale * earlier + later
+
+
+def bk_rounds(n):
     top = 1
     while top < n:
         top *= 2
@@ -60,32 +69,47 @@
     return [r for r in rounds if r]
 
 
-def exclusive_scan(part, axis, n):
-    place = lax.axis_index(axis)
+def unique_sources(pairs):
+    groups = []
+    for pair in pairs:
+        for group in groups:
+            if all(pair[0] != other[0] for other in group):
+                group.append(pair)
+                break
+        else:
+            groups.append([pair])
+    return groups
+
+
+def receive(value, axis, pairs):
+    got = None
+    for group in unique_sources(pairs):
+        one = lax.ppermute(value, axis, group)
+        got = one if got is None else got + one
+    return got
+
+
+def exclusive_scan(part, axis, lines, width):
     held = part
-    before = (jnp.zeros_like(part[0]), jnp.zeros_like(part[1]))
-    for pairs in scan_rounds(n):
-        table = np.zeros((n,), np.bool_)
-        for _, dst in pairs:
-            table[dst] = True
-        takes = jnp.asarray(table)[place]
-        groups = []
-        for pair in pairs:
-            for group in groups:
-                if all(pair[0] != other[0] for other in group):
-                    group.append(pair)
-                    break
-            else:
-                groups.append([pair])
-        got = None
-        for group in groups:
-            one = (lax.ppermute(held[0], axis, group), lax.ppermute(held[1], axis, group))
-            got = one if got is None else jax.tree.map(jnp.add, got, one)
-        new_held = join_memory(got, held)
-        new_before = join_memory(got, before)
-        held = jax.tree.map(lambda a, b: jnp.where(takes, a, b), new_held, held)
-        before = jax.tree.map(lambda a, b: jnp.where(takes, a, b), new_before, before)
-    return before
+    before = jnp.zeros_like(part)
+    after = part
+    for pairs in bk_rounds(width):
+        fwd = [(l * width + s, l * width + d) for l in range(lines) for s, d in pairs]
+        bwd = [(l * width + width - 1 - s, l * width + width - 1 - d) for l in range(lines) for s, d in pairs]
+        got = receive(held, axis, fwd)
+        back = receive(after, axis, bwd)
+        held = join(got, held)
+        before = join(got, before)
+        after = join(after, back)
+    total = join(before, after)
+    if lines == 1:
+        return before
+    earlier = None
+    for shift in range(lines - 1, 0, -1):
+        pairs = [((l - shift) * width + p, l * width + p) for l in range(shift, lines) for p in range(width)]
+        got = lax.ppermute(total, axis, pairs)
+        earlier = got if earlier is None else join(earlier, got)
+    return join(earlier, before)
 
 
 def scatter_heads(partial, axis, n):
@@ -111,7 +135,7 @@
     return lax.dynamic_slice_in_dim(whole, place * width, width, 1)
 
 
-def shards(queries, keys, values, log_decay, norm_gain, out_weight, steer_ids, steer_table, seq_n, head_n):
+def shards(queries, keys, values, log_decay, norm_gain, out_weight, steer_ids, steer_table, seq_n, seq_width, head_n):
     tok_rows, features = queries.shape
     heads_here = log_decay.shape[1]
     head_size = features // heads_here
@@ -126,8 +150,9 @@
         block_step, start, (split(queries), split(keys), split(values), decays)
     )
     device_log = jnp.sum(log_decay, axis=0)
-    passed = exclusive_scan((device_log, local_memory), "seq", seq_n)
-    earlier_memory = passed[1]
+    lines, width = seq_n // seq_width, seq_width
+    passed = exclusive_scan(pack(device_log, local_memory), "seq", lines, width)
+    earlier_memory = passed[:, :head_size, :]
     running = jnp.cumsum(log_decay, axis=0)
     query_heads = queries.reshape(tok_rows, heads_here, head_size).astype(jnp.float32)
     carried = jnp.exp(running)[:, :, None] * jnp.einsum(
@@ -146,6 +171,19 @@
     return (summed + steering).astype(jnp.bfloat16)
 
 
+def line_width(mesh):
+    devices = np.moveaxis(mesh.devices, mesh.axis_names.index("seq"), 0)
+    order = devices.reshape(devices.shape[0], -1)[:, 0]
+    n = len(order)
+    firsts = [tuple(getattr(d, "coords", (0,)))[0] for d in order]
+    width = 1
+    while width < n and firsts[width] == firsts[0]:
+        width += 1
+    if n % width or width & (width - 1):
+        return n
+    return width
+
+
 def solution(mesh):
     in_specs = (
         P("seq", "head"),
@@ -160,8 +198,9 @@
     out_specs = P("seq", "head")
     seq_n = mesh.shape["seq"]
     head_n = mesh.shape["head"]
+    seq_width = line_width(mesh)
 
     def body(*args):
-        return shards(*args, seq_n=seq_n, head_n=head_n)
+        return shards(*args, seq_n=seq_n, seq_width=seq_width, head_n=head_n)
 
     return jax.shard_map(body, mesh=mesh, in_specs=in_specs, out_specs=out_specs, check_vma=False)

time: 188 us -> 140 us (0.74)
  the two profiles are of different devices: /device:TPU:77 before, /device:TPU:335 now
where the time goes in v2:
time: 140 us; the launch traced here: 139 us
  starting transfers between devices  67 us (48%)
  waiting for transfers between devices  50.4 us (36%)
  local copies, waits for them, and re-layouts  9.18 us (7%)
  other arithmetic  6.17 us (4%)
  matrix products  5.42 us (4%)
    ppermute x14, starting transfers between devices, receive(): one = lax.ppermute(value, axis, group)  46.8 us
    ppermute x14, waiting for transfers between devices, receive(): one = lax.ppermute(value, axis, group)  29.4 us
    ppermute x3, waiting for transfers between devices, scatter_heads(): out = out + lax.ppermute(send, axis, pairs)  10.4 us
    ppermute x3, starting transfers between devices, scatter_heads(): out = out + lax.ppermute(send, axis, pairs)  9.8 us
    ppermute x3, waiting for transfers between devices, exclusive_scan(): got = lax.ppermute(total, axis, pairs)  8.29 us
    ppermute x1, starting transfers between devices, scatter_heads(): mine = keep + lax.ppermute(away, axis, pairs)  6.56 us
    dot_general x1, local copies, waits for them, and re-layouts, shards(): jnp.dot(normed, out_weight, preferred_element_type=jnp.float32)  6.5 us
    ppermute x3, starting transfers between devices, exclusive_scan(): got = lax.ppermute(total, axis, pairs)  3.86 us
  transfers between devices with their start and end apart: 21, of which 11 were waited for; matrix products, arithmetic and copies ran while one was open for 6% of the time, Pallas kernels for 0%

profile of v2, /device:TPU:335, one launch (start us, length us, event | category | flops | bytes accessed | tf_op | source)
XLA Modules:
  0.0 138.9 jit_solution(11223107028628259391)
XLA Ops:
  4.4 1.3 collective-permute-start.7
  5.7 4.0 %collective-permute-start = (f32[4,136,128]{2,1,0:T(8,128)S(1)}, f32[4,136,128]{2,1,0:T(8,128)S(1)}, u32[]{:S(2)}, u32[]{:S(2)}) collective-permute-start(f32[4,136,128]{2,1,0:T(8,128)S(1)} %pad_maximum_fusion), channel_id=1, source_target_pairs={{0,8},{16,24},{32,40},{48,56},{64,72},{80,88},{96,104},{112,120},{... | collective-permute-start | bytes 835592 | tf_op jit(solution)/shard_map/ppermute | solution.py:87
  9.8 4.1 %collective-permute-done.7 = f32[4,136,128]{2,1,0:T(8,128)S(1)} collective-permute-done((f32[4,136,128]{2,1,0:T(8,128)S(1)}, f32[4,136,128]{2,1,0:T(8,128)S(1)}, u32[]{:S(2)}, u32[]{:S(2)}) %collective-permute-start.7) | collective-permute-done | bytes 278560 | tf_op jit(solution)/shard_map/ppermute | solution.py:87
  15.6 3.1 %collective-permute-start.8 = (f32[4,136,128]{2,1,0:T(8,128)S(1)}, f32[4,136,128]{2,1,0:T(8,128)S(1)}, u32[]{:S(2)}, u32[]{:S(2)}) collective-permute-start(f32[4,136,128]{2,1,0:T(8,128)S(1)} %get-tuple-element.40), channel_id=1, source_target_pairs={{112,96},{80,64},{48,32},{16,0},{240,224},{208,192},{176,160},{144... | collective-permute-start | bytes 835592 | tf_op jit(solution)/shard_map/ppermute | solution.py:87
  19.7 3.2 %collective-permute-done.8 = f32[4,136,128]{2,1,0:T(8,128)S(1)} collective-permute-done((f32[4,136,128]{2,1,0:T(8,128)S(1)}, f32[4,136,128]{2,1,0:T(8,128)S(1)}, u32[]{:S(2)}, u32[]{:S(2)}) %collective-permute-start.8) | collective-permute-done | bytes 278560 | tf_op jit(solution)/shard_map/ppermute | solution.py:87
  27.9 1.3 collective-permute-start.12
  29.3 14.9 %collective-permute-done.12 = f32[4,136,128]{2,1,0:T(8,128)S(1)} collective-permute-done((f32[4,136,128]{2,1,0:T(8,128)S(1)}, f32[4,136,128]{2,1,0:T(8,128)S(1)}, u32[]{:S(2)}, u32[]{:S(2)}) %collective-permute-start.12) | collective-permute-done | bytes 278560 | tf_op jit(solution)/shard_map/ppermute | solution.py:87
  44.3 30.3 %collective-permute-start.13 = (f32[4,136,128]{2,1,0:T(8,128)S(1)}, f32[4,136,128]{2,1,0:T(8,128)S(1)}, u32[]{:S(2)}, u32[]{:S(2)}) collective-permute-start(f32[4,136,128]{2,1,0:T(8,128)S(1)} %multiply_add_fusion.2), channel_id=1, source_target_pairs={{112,104},{96,88},{80,72},{64,56},{48,40},{32,24},{16,8},{240,232}... | collective-permute-start | bytes 835592 | tf_op jit(solution)/shard_map/ppermute | solution.py:87
  75.0 1.3 collective-permute-start.6
  76.3 2.2 %collective-permute-done.13 = f32[4,136,128]{2,1,0:T(8,128)S(1)} collective-permute-done((f32[4,136,128]{2,1,0:T(8,128)S(1)}, f32[4,136,128]{2,1,0:T(8,128)S(1)}, u32[]{:S(2)}, u32[]{:S(2)}) %collective-permute-start.13) | collective-permute-done | bytes 278560 | tf_op jit(solution)/shard_map/ppermute | solution.py:87
  78.6 4.1 %collective-permute-done.6 = f32[4,136,128]{2,1,0:T(8,128)S(1)} collective-permute-done((f32[4,136,128]{2,1,0:T(8,128)S(1)}, f32[4,136,128]{2,1,0:T(8,128)S(1)}, u32[]{:S(2)}, u32[]{:S(2)}) %collective-permute-start.6) | collective-permute-done | bytes 278560 | tf_op jit(solution)/shard_map/ppermute | solution.py:87
  82.9 1.3 collective-permute-start.15
  85.0 6.5 %copy.47 = bf16[4096,512]{1,0:T(8,128)(2,1)} copy(bf16[4096,512]{0,1:T(8,128)(2,1)} %bitcast.119) | data formatting | bytes 8388608 | tf_op jit(solution)/shard_map/dot_general | solution.py:165
  94.1 4.7 %collective-permute-done.14 = f32[4,136,128]{2,1,0:T(8,128)S(1)} collective-permute-done((f32[4,136,128]{2,1,0:T(8,128)S(1)}, f32[4,136,128]{2,1,0:T(8,128)S(1)}, u32[]{:S(2)}, u32[]{:S(2)}) %collective-permute-start.14) | collective-permute-done | bytes 278560 | tf_op jit(solution)/shard_map/ppermute | solution.py:110
  98.8 3.6 %collective-permute-done.16 = f32[4,136,128]{2,1,0:T(8,128)S(1)} collective-permute-done((f32[4,136,128]{2,1,0:T(8,128)S(1)}, f32[4,136,128]{2,1,0:T(8,128)S(1)}, u32[]{:S(2)}, u32[]{:S(2)}) %collective-permute-start.16) | collective-permute-done | bytes 278560 | tf_op jit(solution)/shard_map/ppermute | solution.py:110
  103.1 3.7 %fusion.53 = f32[128,4,2,512]{3,0,2,1:T(8,128)S(1)} fusion(bf16[128,512,1,1]{0,1,3,2:T(8,128)(2,1)S(1)} %bitcast.120, bf16[4,2,512,512]{3,2,1,0:T(8,128)(2,1)} %bitcast.118), kind=kOutput, calls=%fused_computation.110 | convolution fusion | flops 536870912 | bytes 6422528 | tf_op jit(solution)/shard_map/dot_general | solution.py:165
  107.1 6.6 %collective-permute-start.17 = (f32[128,4,512]{2,0,1:T(8,128)S(1)}, f32[128,4,512]{2,0,1:T(8,128)}, u32[]{:S(2)}, u32[]{:S(2)}) collective-permute-start(f32[128,4,512]{2,0,1:T(8,128)S(1)} %select_bitcast_fusion), channel_id=1, source_target_pairs={{0,1},{1,0},{2,3},{3,2},{4,5},{5,4},{6,7},{7,6},{8,9},{9,8},{10,11... | collective-permute-start | bytes 3145736 | tf_op jit(solution)/shard_map/ppermute | solution.py:127
  113.7 2.3 %collective-permute-done.17 = f32[128,4,512]{2,0,1:T(8,128)} collective-permute-done((f32[128,4,512]{2,0,1:T(8,128)S(1)}, f32[128,4,512]{2,0,1:T(8,128)}, u32[]{:S(2)}, u32[]{:S(2)}) %collective-permute-start.17) | collective-permute-done | bytes 1048608 | tf_op jit(solution)/shard_map/ppermute | solution.py:127
  116.0 1.6 %fusion.8 = f32[128,4,512]{2,0,1:T(8,128)S(1)} fusion(f32[128,4,512]{2,0,1:T(8,128)} %collective-permute-done.17, f32[128,4,2,512]{3,0,2,1:T(8,128)S(1)} %fusion.53, pred[]{:T(512)S(6)} %eq.22), kind=kLoop, calls=%fused_computation.13 | loop fusion | flops 524288 | bytes 4194305 | tf_op jit(solution)/shard_map/add | solution.py:127
  117.7 3.2 %collective-permute-start.18 = (f32[128,512]{1,0:T(8,128)S(1)}, f32[128,512]{1,0:T(8,128)S(1)}, u32[]{:S(2)}, u32[]{:S(2)}) collective-permute-start(f32[128,512]{1,0:T(8,128)S(1)} %get-tuple-element.19), channel_id=1, source_target_pairs={{0,2},{1,3},{2,4},{3,5},{4,6},{5,7},{6,0},{7,1},{8,10},{9,11},{10,... | collective-permute-start | bytes 786440 | tf_op jit(solution)/shard_map/ppermute | solution.py:132
  120.9 2.6 %collective-permute-start.19 = (f32[128,512]{1,0:T(8,128)S(1)}, f32[128,512]{1,0:T(8,128)S(1)}, u32[]{:S(2)}, u32[]{:S(2)}) collective-permute-start(f32[128,512]{1,0:T(8,128)S(1)} %get-tuple-element.28), channel_id=1, source_target_pairs={{0,4},{1,5},{2,6},{3,7},{4,0},{5,1},{6,2},{7,3},{8,12},{9,13},{10,... | collective-permute-start | bytes 786440 | tf_op jit(solution)/shard_map/ppermute | solution.py:132
  123.5 4.0 %collective-permute-start.20 = (f32[128,512]{1,0:T(8,128)S(1)}, f32[128,512]{1,0:T(8,128)S(1)}, u32[]{:S(2)}, u32[]{:S(2)}) collective-permute-start(f32[128,512]{1,0:T(8,128)S(1)} %get-tuple-element.20), channel_id=1, source_target_pairs={{0,6},{1,7},{2,0},{3,1},{4,2},{5,3},{6,4},{7,5},{8,14},{9,15},{10,... | collective-permute-start | bytes 786440 | tf_op jit(solution)/shard_map/ppermute | solution.py:132
  127.8 3.8 %collective-permute-done.19 = f32[128,512]{1,0:T(8,128)S(1)} collective-permute-done((f32[128,512]{1,0:T(8,128)S(1)}, f32[128,512]{1,0:T(8,128)S(1)}, u32[]{:S(2)}, u32[]{:S(2)}) %collective-permute-start.19) | collective-permute-done | bytes 262176 | tf_op jit(solution)/shard_map/ppermute | solution.py:132
  131.5 6.6 %collective-permute-done.20 = f32[128,512]{1,0:T(8,128)S(1)} collective-permute-done((f32[128,512]{1,0:T(8,128)S(1)}, f32[128,512]{1,0:T(8,128)S(1)}, u32[]{:S(2)}, u32[]{:S(2)}) %collective-permute-start.20) | collective-permute-done | bytes 262176 | tf_op jit(solution)/shard_map/ppermute | solution.py:132
  (88 shorter events, 18.1 us)
Async XLA Ops:
  0.0 127.5 %copy-start = (bf16[16,512]{1,0:T(8,128)(2,1)S(1)}, bf16[16,512]{1,0:T(8,128)(2,1)}, u32[]{:S(2)}) copy-start(bf16[16,512]{1,0:T(8,128)(2,1)} %param.15) | copy-start | bytes 49156
  4.4 9.4 %collective-permute-start.7 = (f32[4,136,128]{2,1,0:T(8,128)S(1)}, f32[4,136,128]{2,1,0:T(8,128)S(1)}, u32[]{:S(2)}, u32[]{:S(2)}) collective-permute-start(f32[4,136,128]{2,1,0:T(8,128)S(1)} %pad_maximum_fusion), channel_id=1, source_target_pairs={{120,112},{104,96},{88,80},{72,64},{56,48},{40,32},{24,16},{8,0},{... | collective-permute-start | bytes 835592 | tf_op jit(solution)/shard_map/ppermute | solution.py:87
  5.7 9.1 %collective-permute-start = (f32[4,136,128]{2,1,0:T(8,128)S(1)}, f32[4,136,128]{2,1,0:T(8,128)S(1)}, u32[]{:S(2)}, u32[]{:S(2)}) collective-permute-start(f32[4,136,128]{2,1,0:T(8,128)S(1)} %pad_maximum_fusion), channel_id=1, source_target_pairs={{0,8},{16,24},{32,40},{48,56},{64,72},{80,88},{96,104},{112,120},{... | collective-permute-start | bytes 835592 | tf_op jit(solution)/shard_map/ppermute | solution.py:87
  14.9 3.8 %collective-permute-start.1 = (f32[4,136,128]{2,1,0:T(8,128)S(1)}, f32[4,136,128]{2,1,0:T(8,128)S(1)}, u32[]{:S(2)}, u32[]{:S(2)}) collective-permute-start(f32[4,136,128]{2,1,0:T(8,128)S(1)} %get-tuple-element.39), channel_id=1, source_target_pairs={{8,24},{40,56},{72,88},{104,120},{136,152},{168,184},{200,216},{23... | collective-permute-start | bytes 835592 | tf_op jit(solution)/shard_map/ppermute | solution.py:87
  15.6 7.3 %collective-permute-start.8 = (f32[4,136,128]{2,1,0:T(8,128)S(1)}, f32[4,136,128]{2,1,0:T(8,128)S(1)}, u32[]{:S(2)}, u32[]{:S(2)}) collective-permute-start(f32[4,136,128]{2,1,0:T(8,128)S(1)} %get-tuple-element.40), channel_id=1, source_target_pairs={{112,96},{80,64},{48,32},{16,0},{240,224},{208,192},{176,160},{144... | collective-permute-start | bytes 835592 | tf_op jit(solution)/shard_map/ppermute | solution.py:87
  18.9 4.0 %collective-permute-start.2 = (f32[4,136,128]{2,1,0:T(8,128)S(1)}, f32[4,136,128]{2,1,0:T(8,128)S(1)}, u32[]{:S(2)}, u32[]{:S(2)}) collective-permute-start(f32[4,136,128]{2,1,0:T(8,128)S(1)} %get-tuple-element.37), channel_id=1, source_target_pairs={{24,56},{88,120},{152,184},{216,248},{280,312},{344,376},{408,440}... | collective-permute-start | bytes 835592 | tf_op jit(solution)/shard_map/ppermute | solution.py:87
  23.1 1.4 %collective-permute-start.3 = (f32[4,136,128]{2,1,0:T(8,128)S(1)}, f32[4,136,128]{2,1,0:T(8,128)S(1)}, u32[]{:S(2)}, u32[]{:S(2)}) collective-permute-start(f32[4,136,128]{2,1,0:T(8,128)S(1)} %get-tuple-element.35), channel_id=1, source_target_pairs={{56,120},{184,248},{312,376},{440,504},{57,121},{185,249},{313,377... | collective-permute-start | bytes 835592 | tf_op jit(solution)/shard_map/ppermute | solution.py:87
  23.8 0.7 collective-permute-start.4
  24.6 0.7 collective-permute-start.5
  25.5 59.0 %copy-start.2 = (f32[128,4]{0,1:T(4,128)S(1)}, f32[128,4]{0,1:T(4,128)}, u32[]{:S(2)}) copy-start(f32[128,4]{0,1:T(4,128)} %param.11) | copy-start | bytes 6148
  25.5 0.7 collective-permute-start.9
  26.4 1.4 collective-permute-start.10
  27.0 0.7 collective-permute-start.11
  27.9 16.3 %collective-permute-start.12 = (f32[4,136,128]{2,1,0:T(8,128)S(1)}, f32[4,136,128]{2,1,0:T(8,128)S(1)}, u32[]{:S(2)}, u32[]{:S(2)}) collective-permute-start(f32[4,136,128]{2,1,0:T(8,128)S(1)} %multiply_add_fusion.3), channel_id=1, source_target_pairs={{96,80},{64,48},{32,16},{224,208},{192,176},{160,144},{352,336},{3... | collective-permute-start | bytes 835592 | tf_op jit(solution)/shard_map/ppermute | solution.py:87
  44.3 34.2 %collective-permute-start.13 = (f32[4,136,128]{2,1,0:T(8,128)S(1)}, f32[4,136,128]{2,1,0:T(8,128)S(1)}, u32[]{:S(2)}, u32[]{:S(2)}) collective-permute-start(f32[4,136,128]{2,1,0:T(8,128)S(1)} %multiply_add_fusion.2), channel_id=1, source_target_pairs={{112,104},{96,88},{80,72},{64,56},{48,40},{32,24},{16,8},{240,232}... | collective-permute-start | bytes 835592 | tf_op jit(solution)/shard_map/ppermute | solution.py:87
  75.0 7.7 %collective-permute-start.6 = (f32[4,136,128]{2,1,0:T(8,128)S(1)}, f32[4,136,128]{2,1,0:T(8,128)S(1)}, u32[]{:S(2)}, u32[]{:S(2)}) collective-permute-start(f32[4,136,128]{2,1,0:T(8,128)S(1)} %get-tuple-element.33), channel_id=1, source_target_pairs={{8,16},{24,32},{40,48},{56,64},{72,80},{88,96},{104,112},{136,144}... | collective-permute-start | bytes 835592 | tf_op jit(solution)/shard_map/ppermute | solution.py:87
  82.9 11.2 %collective-permute-start.15 = (f32[4,136,128]{2,1,0:T(8,128)S(1)}, f32[4,136,128]{2,1,0:T(8,128)S(1)}, u32[]{:S(2)}, u32[]{:S(2)}) collective-permute-start(f32[4,136,128]{2,1,0:T(8,128)S(1)} %get-tuple-element.17), channel_id=1, source_target_pairs={{0,256},{8,264},{16,272},{24,280},{32,288},{40,296},{48,304},{56,3... | collective-permute-start | bytes 835592 | tf_op jit(solution)/shard_map/ppermute | solution.py:110
  91.5 7.3 %collective-permute-start.14 = (f32[4,136,128]{2,1,0:T(8,128)S(1)}, f32[4,136,128]{2,1,0:T(8,128)S(1)}, u32[]{:S(2)}, u32[]{:S(2)}) collective-permute-start(f32[4,136,128]{2,1,0:T(8,128)S(1)} %get-tuple-element.17), channel_id=1, source_target_pairs={{0,128},{8,136},{16,144},{24,152},{32,160},{40,168},{48,176},{56,1... | collective-permute-start | bytes 835592 | tf_op jit(solution)/shard_map/ppermute | solution.py:110
  92.7 9.7 %collective-permute-start.16 = (f32[4,136,128]{2,1,0:T(8,128)S(1)}, f32[4,136,128]{2,1,0:T(8,128)S(1)}, u32[]{:S(2)}, u32[]{:S(2)}) collective-permute-start(f32[4,136,128]{2,1,0:T(8,128)S(1)} %get-tuple-element.17), channel_id=1, source_target_pairs={{0,384},{8,392},{16,400},{24,408},{32,416},{40,424},{48,432},{56,4... | collective-permute-start | bytes 835592 | tf_op jit(solution)/shard_map/ppermute | solution.py:110
  106.8 20.7 %copy-start.4 = (s32[128]{0:T(128)S(1)}, s32[128]{0:T(128)}, u32[]{:S(2)}) copy-start(s32[128]{0:T(128)} %param.14) | copy-start | bytes 1540
  107.1 9.0 %collective-permute-start.17 = (f32[128,4,512]{2,0,1:T(8,128)S(1)}, f32[128,4,512]{2,0,1:T(8,128)}, u32[]{:S(2)}, u32[]{:S(2)}) collective-permute-start(f32[128,4,512]{2,0,1:T(8,128)S(1)} %select_bitcast_fusion), channel_id=1, source_target_pairs={{0,1},{1,0},{2,3},{3,2},{4,5},{5,4},{6,7},{7,6},{8,9},{9,8},{10,11... | collective-permute-start | bytes 3145736 | tf_op jit(solution)/shard_map/ppermute | solution.py:127
  117.7 10.1 %collective-permute-start.18 = (f32[128,512]{1,0:T(8,128)S(1)}, f32[128,512]{1,0:T(8,128)S(1)}, u32[]{:S(2)}, u32[]{:S(2)}) collective-permute-start(f32[128,512]{1,0:T(8,128)S(1)} %get-tuple-element.19), channel_id=1, source_target_pairs={{0,2},{1,3},{2,4},{3,5},{4,6},{5,7},{6,0},{7,1},{8,10},{9,11},{10,... | collective-permute-start | bytes 786440 | tf_op jit(solution)/shard_map/ppermute | solution.py:132
  120.9 10.6 %collective-permute-start.19 = (f32[128,512]{1,0:T(8,128)S(1)}, f32[128,512]{1,0:T(8,128)S(1)}, u32[]{:S(2)}, u32[]{:S(2)}) collective-permute-start(f32[128,512]{1,0:T(8,128)S(1)} %get-tuple-element.28), channel_id=1, source_target_pairs={{0,4},{1,5},{2,6},{3,7},{4,0},{5,1},{6,2},{7,3},{8,12},{9,13},{10,... | collective-permute-start | bytes 786440 | tf_op jit(solution)/shard_map/ppermute | solution.py:132
  123.5 14.6 %collective-permute-start.20 = (f32[128,512]{1,0:T(8,128)S(1)}, f32[128,512]{1,0:T(8,128)S(1)}, u32[]{:S(2)}, u32[]{:S(2)}) collective-permute-start(f32[128,512]{1,0:T(8,128)S(1)} %get-tuple-element.20), channel_id=1, source_target_pairs={{0,6},{1,7},{2,0},{3,1},{4,2},{5,3},{6,4},{7,5},{8,14},{9,15},{10,... | collective-permute-start | bytes 786440 | tf_op jit(solution)/shard_map/ppermute | solution.py:132
  (2 other events, 28.3 us)

commit v3 on v2

--- a/solution.py
+++ b/solution.py
@@ -89,18 +89,36 @@
     return got
 
 
+def member(position, spots):
+    bits = 0
+    for spot in spots:
+        bits |= 1 << spot
+    return ((jnp.int32(bits) >> position) & 1) == 1
+
+
 def exclusive_scan(part, axis, lines, width):
+    pos = lax.axis_index(axis) % width
     held = part
     before = jnp.zeros_like(part)
     after = part
     for pairs in bk_rounds(width):
-        fwd = [(l * width + s, l * width + d) for l in range(lines) for s, d in pairs]
-        bwd = [(l * width + width - 1 - s, l * width + width - 1 - d) for l in range(lines) for s, d in pairs]
-        got = receive(held, axis, fwd)
-        back = receive(after, axis, bwd)
-        held = join(got, held)
-        before = join(got, before)
-        after = join(after, back)
+        fwd_groups = unique_sources(pairs)
+        ahead = None
+        behind = None
+        for group in fwd_groups:
+            back = [(width - 1 - s, width - 1 - d) for s, d in group]
+            both = group + back
+            assert len({s for s, _ in both}) == len(both) and len({d for _, d in both}) == len(both)
+            send = jnp.where(member(pos, [s for s, _ in group]), held, after)
+            full = [(l * width + s, l * width + d) for l in range(lines) for s, d in both]
+            got = lax.ppermute(send, axis, full)
+            one_ahead = jnp.where(member(pos, [d for _, d in group]), got, 0.0)
+            one_behind = jnp.where(member(pos, [d for _, d in back]), got, 0.0)
+            ahead = one_ahead if ahead is None else ahead + one_ahead
+            behind = one_behind if behind is None else behind + one_behind
+        held = join(ahead, held)
+        before = join(ahead, before)
+        after = join(after, behind)
     total = join(before, after)
     if lines == 1:
         return before
@@ -162,7 +180,7 @@
     mean_sq = jnp.mean(attended * attended, axis=-1, keepdims=True)
     normed = (attended * lax.rsqrt(mean_sq + 1e-06)).reshape(tok_rows, features) * norm_gain
     normed = normed.astype(jnp.bfloat16)
-    partial_term = jnp.dot(normed, out_weight, preferred_element_type=jnp.float32)
+    partial_term = lax.optimization_barrier(jnp.dot(normed, out_weight, preferred_element_type=jnp.float32))
     onehot = (
         steer_ids[:, None] == jnp.arange(steer_table.shape[0], dtype=jnp.int32)[None, :]
     ).astype(jnp.bfloat16)

time: 140 us -> 136 us (0.971)
  the two profiles are of different devices: /device:TPU:335 before, /device:TPU:79 now
where the time goes in v3:
time: 136 us; the launch traced here: 135 us
  waiting for transfers between devices  73.4 us (54%)
  starting transfers between devices  39.5 us (29%)
  other arithmetic  9.34 us (7%)
  local copies, waits for them, and re-layouts  7.64 us (6%)
  matrix products  4.68 us (3%)
    ppermute x7, waiting for transfers between devices, exclusive_scan(): got = lax.ppermute(send, axis, full)  52.4 us
    ppermute x1, starting transfers between devices, scatter_heads(): mine = keep + lax.ppermute(away, axis, pairs)  15.8 us
    ppermute x3, waiting for transfers between devices, scatter_heads(): out = out + lax.ppermute(send, axis, pairs)  10.3 us
    ppermute x7, starting transfers between devices, exclusive_scan(): got = lax.ppermute(send, axis, full)  10.1 us
    ppermute x3, starting transfers between devices, scatter_heads(): out = out + lax.ppermute(send, axis, pairs)  9.78 us
    ppermute x3, waiting for transfers between devices, exclusive_scan(): got = lax.ppermute(total, axis, pairs)  8.29 us
    slice x1, other arithmetic, scatter_heads(): keep = jnp.where(core == 0, blocks[:, :, 0], blocks[:, :, 1])  4.37 us
    ppermute x3, starting transfers between devices, exclusive_scan(): got = lax.ppermute(total, axis, pairs)  3.89 us
  transfers between devices with their start and end apart: 14, of which 10 were waited for; matrix products, arithmetic and copies ran while one was open for 1% of the time, Pallas kernels for 0%

profile of v3, /device:TPU:79, one launch (start us, length us, event | category | flops | bytes accessed | tf_op | source)
XLA Modules:
  0.0 135.3 jit_solution(9359491586102226585)
XLA Ops:
  4.4 3.5 %collective-permute-start = (f32[4,136,128]{2,1,0:T(8,128)S(1)}, f32[4,136,128]{2,1,0:T(8,128)S(1)}, u32[]{:S(2)}, u32[]{:S(2)}) collective-permute-start(f32[4,136,128]{2,1,0:T(8,128)S(1)} %pad_maximum_fusion), channel_id=1, source_target_pairs={{0,8},{16,24},{32,40},{48,56},{64,72},{80,88},{96,104},{112,120},{... | collective-permute-start | bytes 835592 | tf_op jit(solution)/shard_map/ppermute | solution.py:114
  8.0 6.2 %collective-permute-done = f32[4,136,128]{2,1,0:T(8,128)S(1)} collective-permute-done((f32[4,136,128]{2,1,0:T(8,128)S(1)}, f32[4,136,128]{2,1,0:T(8,128)S(1)}, u32[]{:S(2)}, u32[]{:S(2)}) %collective-permute-start) | collective-permute-done | bytes 278560 | tf_op jit(solution)/shard_map/ppermute | solution.py:114
  14.4 1.3 collective-permute-start.1
  15.8 4.6 %collective-permute-done.1 = f32[4,136,128]{2,1,0:T(8,128)S(1)} collective-permute-done((f32[4,136,128]{2,1,0:T(8,128)S(1)}, f32[4,136,128]{2,1,0:T(8,128)S(1)}, u32[]{:S(2)}, u32[]{:S(2)}) %collective-permute-start.1) | collective-permute-done | bytes 278560 | tf_op jit(solution)/shard_map/ppermute | solution.py:114
  23.3 1.3 collective-permute-start.5
  24.7 34.1 %collective-permute-done.5 = f32[4,136,128]{2,1,0:T(8,128)S(1)} collective-permute-done((f32[4,136,128]{2,1,0:T(8,128)S(1)}, f32[4,136,128]{2,1,0:T(8,128)S(1)}, u32[]{:S(2)}, u32[]{:S(2)}) %collective-permute-start.5) | collective-permute-done | bytes 278560 | tf_op jit(solution)/shard_map/ppermute | solution.py:114
  59.0 1.9 %collective-permute-start.6 = (f32[4,136,128]{2,1,0:T(8,128)S(1)}, f32[4,136,128]{2,1,0:T(8,128)S(1)}, u32[]{:S(2)}, u32[]{:S(2)}) collective-permute-start(f32[4,136,128]{2,1,0:T(8,128)S(1)} %add_select_fusion), channel_id=1, source_target_pairs={{8,16},{24,32},{40,48},{56,64},{72,80},{88,96},{104,112},{112,104}... | collective-permute-start | bytes 835592 | tf_op jit(solution)/shard_map/ppermute | solution.py:114
  61.4 7.5 %collective-permute-done.6 = f32[4,136,128]{2,1,0:T(8,128)S(1)} collective-permute-done((f32[4,136,128]{2,1,0:T(8,128)S(1)}, f32[4,136,128]{2,1,0:T(8,128)S(1)}, u32[]{:S(2)}, u32[]{:S(2)}) %collective-permute-start.6) | collective-permute-done | bytes 278560 | tf_op jit(solution)/shard_map/ppermute | solution.py:114
  69.2 1.3 collective-permute-start.8
  71.3 1.3 collective-permute-start.7
  72.6 1.3 collective-permute-start.9
  73.9 4.1 %collective-permute-done.8 = f32[4,136,128]{2,1,0:T(8,128)S(1)} collective-permute-done((f32[4,136,128]{2,1,0:T(8,128)S(1)}, f32[4,136,128]{2,1,0:T(8,128)S(1)}, u32[]{:S(2)}, u32[]{:S(2)}) %collective-permute-start.8) | collective-permute-done | bytes 278560 | tf_op jit(solution)/shard_map/ppermute | solution.py:128
  79.0 3.3 %collective-permute-done.9 = f32[4,136,128]{2,1,0:T(8,128)S(1)} collective-permute-done((f32[4,136,128]{2,1,0:T(8,128)S(1)}, f32[4,136,128]{2,1,0:T(8,128)S(1)}, u32[]{:S(2)}, u32[]{:S(2)}) %collective-permute-start.9) | collective-permute-done | bytes 278560 | tf_op jit(solution)/shard_map/ppermute | solution.py:128
  83.0 2.9 %fusion.55 = f32[128,4096]{1,0:T(8,128)S(1)} fusion(bf16[128,512]{0,1:T(8,128)(2,1)S(1)} %fusion.18, bf16[512,4096]{1,0:T(8,128)(2,1)} %param.13), kind=kOutput, calls=%fused_computation.130 | convolution fusion | flops 536870912 | bytes 6422528 | tf_op jit(solution)/shard_map/dot_general | solution.py:183
  85.9 2.8 %reshape.96 = f32[128,4,2,512]{3,2,1,0:T(2,128)} reshape(f32[128,4096]{1,0:T(8,128)S(1)} %fusion.55) | data formatting | bytes 4194304 | tf_op jit(solution)/shard_map/reshape | solution.py:141
  88.8 4.4 %fusion.54 = (f32[128,4,1,512]{3,2,1,0:T(1,128)S(1)}, f32[128,4,1,512]{3,2,1,0:T(1,128)S(1)}, f32[128,4,1,512]{3,2,1,0:T(1,128)S(1)}) fusion(f32[128,4,2,512]{3,2,1,0:T(2,128)} %reshape.96, pred[]{:T(512)S(6)} %eq.80), kind=kLoop, calls=%fused_computation.129 | loop fusion | flops 262144 | bytes 5242881 | tf_op jit(solution)/shard_map/slice | solution.py:142
  93.1 1.3 copy.82
  94.4 15.8 %collective-permute-start.10 = (f32[128,4,512]{2,1,0:T(4,128)}, f32[128,4,512]{2,1,0:T(4,128)S(1)}, u32[]{:S(2)}, u32[]{:S(2)}) collective-permute-start(f32[128,4,512]{2,1,0:T(4,128)} %bitcast.103), channel_id=1, source_target_pairs={{0,1},{1,0},{2,3},{3,2},{4,5},{5,4},{6,7},{7,6},{8,9},{9,8},{10,11... | collective-permute-start | bytes 3145736 | tf_op jit(solution)/shard_map/ppermute | solution.py:145
  110.2 2.4 %collective-permute-done.10 = f32[128,4,512]{2,1,0:T(4,128)S(1)} collective-permute-done((f32[128,4,512]{2,1,0:T(4,128)}, f32[128,4,512]{2,1,0:T(4,128)S(1)}, u32[]{:S(2)}, u32[]{:S(2)}) %collective-permute-start.10) | collective-permute-done | bytes 1048608 | tf_op jit(solution)/shard_map/ppermute | solution.py:145
  114.1 3.2 %collective-permute-start.11 = (f32[128,512]{1,0:T(8,128)S(1)}, f32[128,512]{1,0:T(8,128)S(1)}, u32[]{:S(2)}, u32[]{:S(2)}) collective-permute-start(f32[128,512]{1,0:T(8,128)S(1)} %bitcast.110), channel_id=1, source_target_pairs={{0,2},{1,3},{2,4},{3,5},{4,6},{5,7},{6,0},{7,1},{8,10},{9,11},{10,... | collective-permute-start | bytes 786440 | tf_op jit(solution)/shard_map/ppermute | solution.py:150
  117.3 2.6 %collective-permute-start.12 = (f32[128,512]{1,0:T(8,128)S(1)}, f32[128,512]{1,0:T(8,128)S(1)}, u32[]{:S(2)}, u32[]{:S(2)}) collective-permute-start(f32[128,512]{1,0:T(8,128)S(1)} %bitcast.111), channel_id=1, source_target_pairs={{0,4},{1,5},{2,6},{3,7},{4,0},{5,1},{6,2},{7,3},{8,12},{9,13},{10,... | collective-permute-start | bytes 786440 | tf_op jit(solution)/shard_map/ppermute | solution.py:150
  120.0 4.0 %collective-permute-start.13 = (f32[128,512]{1,0:T(8,128)S(1)}, f32[128,512]{1,0:T(8,128)S(1)}, u32[]{:S(2)}, u32[]{:S(2)}) collective-permute-start(f32[128,512]{1,0:T(8,128)S(1)} %bitcast.112), channel_id=1, source_target_pairs={{0,6},{1,7},{2,0},{3,1},{4,2},{5,3},{6,4},{7,5},{8,14},{9,15},{10,... | collective-permute-start | bytes 786440 | tf_op jit(solution)/shard_map/ppermute | solution.py:150
  124.2 3.7 %collective-permute-done.12 = f32[128,512]{1,0:T(8,128)S(1)} collective-permute-done((f32[128,512]{1,0:T(8,128)S(1)}, f32[128,512]{1,0:T(8,128)S(1)}, u32[]{:S(2)}, u32[]{:S(2)}) %collective-permute-start.12) | collective-permute-done | bytes 262176 | tf_op jit(solution)/shard_map/ppermute | solution.py:150
  127.9 6.6 %collective-permute-done.13 = f32[128,512]{1,0:T(8,128)S(1)} collective-permute-done((f32[128,512]{1,0:T(8,128)S(1)}, f32[128,512]{1,0:T(8,128)S(1)}, u32[]{:S(2)}, u32[]{:S(2)}) %collective-permute-start.13) | collective-permute-done | bytes 262176 | tf_op jit(solution)/shard_map/ppermute | solution.py:150
  (81 shorter events, 13.2 us)
Async XLA Ops:
  0.0 123.9 %copy-start = (bf16[16,512]{1,0:T(8,128)(2,1)S(1)}, bf16[16,512]{1,0:T(8,128)(2,1)}, u32[]{:S(2)}) copy-start(bf16[16,512]{1,0:T(8,128)(2,1)} %param.15) | copy-start | bytes 49156
  4.4 9.8 %collective-permute-start = (f32[4,136,128]{2,1,0:T(8,128)S(1)}, f32[4,136,128]{2,1,0:T(8,128)S(1)}, u32[]{:S(2)}, u32[]{:S(2)}) collective-permute-start(f32[4,136,128]{2,1,0:T(8,128)S(1)} %pad_maximum_fusion), channel_id=1, source_target_pairs={{0,8},{16,24},{32,40},{48,56},{64,72},{80,88},{96,104},{112,120},{... | collective-permute-start | bytes 835592 | tf_op jit(solution)/shard_map/ppermute | solution.py:114
  14.4 6.0 %collective-permute-start.1 = (f32[4,136,128]{2,1,0:T(8,128)S(1)}, f32[4,136,128]{2,1,0:T(8,128)S(1)}, u32[]{:S(2)}, u32[]{:S(2)}) collective-permute-start(f32[4,136,128]{2,1,0:T(8,128)S(1)} %get-tuple-element.36), channel_id=1, source_target_pairs={{8,24},{40,56},{72,88},{104,120},{112,96},{80,64},{48,32},{16,0},{... | collective-permute-start | bytes 835592 | tf_op jit(solution)/shard_map/ppermute | solution.py:114
  20.4 4.2 %copy-start.1 = (bf16[128,512]{1,0:T(8,128)(2,1)S(1)}, bf16[128,512]{1,0:T(8,128)(2,1)}, u32[]{:S(2)}) copy-start(bf16[128,512]{1,0:T(8,128)(2,1)} %param.8) | copy-start | bytes 393220
  20.7 0.7 collective-permute-start.2
  21.6 1.4 %collective-permute-start.3 = (f32[4,136,128]{2,1,0:T(8,128)S(1)}, f32[4,136,128]{2,1,0:T(8,128)S(1)}, u32[]{:S(2)}, u32[]{:S(2)}) collective-permute-start(f32[4,136,128]{2,1,0:T(8,128)S(1)} %get-tuple-element.30), channel_id=1, source_target_pairs={{56,120},{64,0},{184,248},{192,128},{312,376},{320,256},{440,504},... | collective-permute-start | bytes 835592 | tf_op jit(solution)/shard_map/ppermute | solution.py:114
  22.3 0.7 collective-permute-start.4
  23.3 47.6 %copy-start.2 = (f32[128,4]{0,1:T(4,128)S(1)}, f32[128,4]{0,1:T(4,128)}, u32[]{:S(2)}) copy-start(f32[128,4]{0,1:T(4,128)} %param.11) | copy-start | bytes 6148
  23.3 35.5 %collective-permute-start.5 = (f32[4,136,128]{2,1,0:T(8,128)S(1)}, f32[4,136,128]{2,1,0:T(8,128)S(1)}, u32[]{:S(2)}, u32[]{:S(2)}) collective-permute-start(f32[4,136,128]{2,1,0:T(8,128)S(1)} %get-tuple-element.19), channel_id=1, source_target_pairs={{24,40},{56,72},{88,104},{96,80},{64,48},{32,16},{152,168},{184,20... | collective-permute-start | bytes 835592 | tf_op jit(solution)/shard_map/ppermute | solution.py:114
  59.0 23.8 %copy-start.3 = (f32[512]{0:T(512)S(1)}, f32[512]{0:T(512)}, u32[]{:S(2)}) copy-start(f32[512]{0:T(512)} %param.12) | copy-start | bytes 6148
  59.0 9.8 %collective-permute-start.6 = (f32[4,136,128]{2,1,0:T(8,128)S(1)}, f32[4,136,128]{2,1,0:T(8,128)S(1)}, u32[]{:S(2)}, u32[]{:S(2)}) collective-permute-start(f32[4,136,128]{2,1,0:T(8,128)S(1)} %add_select_fusion), channel_id=1, source_target_pairs={{8,16},{24,32},{40,48},{56,64},{72,80},{88,96},{104,112},{112,104}... | collective-permute-start | bytes 835592 | tf_op jit(solution)/shard_map/ppermute | solution.py:114
  69.2 8.8 %collective-permute-start.8 = (f32[4,136,128]{2,1,0:T(8,128)S(1)}, f32[4,136,128]{2,1,0:T(8,128)S(1)}, u32[]{:S(2)}, u32[]{:S(2)}) collective-permute-start(f32[4,136,128]{2,1,0:T(8,128)S(1)} %get-tuple-element.17), channel_id=1, source_target_pairs={{0,256},{8,264},{16,272},{24,280},{32,288},{40,296},{48,304},{56,3... | collective-permute-start | bytes 835592 | tf_op jit(solution)/shard_map/ppermute | solution.py:128
  71.3 7.6 %collective-permute-start.7 = (f32[4,136,128]{2,1,0:T(8,128)S(1)}, f32[4,136,128]{2,1,0:T(8,128)S(1)}, u32[]{:S(2)}, u32[]{:S(2)}) collective-permute-start(f32[4,136,128]{2,1,0:T(8,128)S(1)} %get-tuple-element.17), channel_id=1, source_target_pairs={{0,128},{8,136},{16,144},{24,152},{32,160},{40,168},{48,176},{56,1... | collective-permute-start | bytes 835592 | tf_op jit(solution)/shard_map/ppermute | solution.py:128
  72.6 9.7 %collective-permute-start.9 = (f32[4,136,128]{2,1,0:T(8,128)S(1)}, f32[4,136,128]{2,1,0:T(8,128)S(1)}, u32[]{:S(2)}, u32[]{:S(2)}) collective-permute-start(f32[4,136,128]{2,1,0:T(8,128)S(1)} %get-tuple-element.17), channel_id=1, source_target_pairs={{0,384},{8,392},{16,400},{24,408},{32,416},{40,424},{48,432},{56,4... | collective-permute-start | bytes 835592 | tf_op jit(solution)/shard_map/ppermute | solution.py:128
  94.4 29.6 %copy-start.4 = (s32[128]{0:T(128)S(1)}, s32[128]{0:T(128)}, u32[]{:S(2)}) copy-start(s32[128]{0:T(128)} %param.14) | copy-start | bytes 1540
  94.4 18.3 %collective-permute-start.10 = (f32[128,4,512]{2,1,0:T(4,128)}, f32[128,4,512]{2,1,0:T(4,128)S(1)}, u32[]{:S(2)}, u32[]{:S(2)}) collective-permute-start(f32[128,4,512]{2,1,0:T(4,128)} %bitcast.103), channel_id=1, source_target_pairs={{0,1},{1,0},{2,3},{3,2},{4,5},{5,4},{6,7},{7,6},{8,9},{9,8},{10,11... | collective-permute-start | bytes 3145736 | tf_op jit(solution)/shard_map/ppermute | solution.py:145
  114.1 10.1 %collective-permute-start.11 = (f32[128,512]{1,0:T(8,128)S(1)}, f32[128,512]{1,0:T(8,128)S(1)}, u32[]{:S(2)}, u32[]{:S(2)}) collective-permute-start(f32[128,512]{1,0:T(8,128)S(1)} %bitcast.110), channel_id=1, source_target_pairs={{0,2},{1,3},{2,4},{3,5},{4,6},{5,7},{6,0},{7,1},{8,10},{9,11},{10,... | collective-permute-start | bytes 786440 | tf_op jit(solution)/shard_map/ppermute | solution.py:150
  117.3 10.6 %collective-permute-start.12 = (f32[128,512]{1,0:T(8,128)S(1)}, f32[128,512]{1,0:T(8,128)S(1)}, u32[]{:S(2)}, u32[]{:S(2)}) collective-permute-start(f32[128,512]{1,0:T(8,128)S(1)} %bitcast.111), channel_id=1, source_target_pairs={{0,4},{1,5},{2,6},{3,7},{4,0},{5,1},{6,2},{7,3},{8,12},{9,13},{10,... | collective-permute-start | bytes 786440 | tf_op jit(solution)/shard_map/ppermute | solution.py:150
  120.0 14.6 %collective-permute-start.13 = (f32[128,512]{1,0:T(8,128)S(1)}, f32[128,512]{1,0:T(8,128)S(1)}, u32[]{:S(2)}, u32[]{:S(2)}) collective-permute-start(f32[128,512]{1,0:T(8,128)S(1)} %bitcast.112), channel_id=1, source_target_pairs={{0,6},{1,7},{2,0},{3,1},{4,2},{5,3},{6,4},{7,5},{8,14},{9,15},{10,... | collective-permute-start | bytes 786440 | tf_op jit(solution)/shard_map/ppermute | solution.py:150

commit v4 on v3

--- a/solution.py
+++ b/solution.py
@@ -138,14 +138,17 @@
         chips = n // 2
         core = place % 2
         chip = place // 2
-        blocks = partial.reshape(rows, chips, 2, width)
-        keep = jnp.where(core == 0, blocks[:, :, 0], blocks[:, :, 1])
-        away = jnp.where(core == 0, blocks[:, :, 1], blocks[:, :, 0])
+
+        def block(index):
+            return lax.dynamic_slice_in_dim(partial, index * width, width, 1)
+
+        keep = jnp.stack([block(2 * y + core) for y in range(chips)])
+        away = jnp.stack([block(2 * y + 1 - core) for y in range(chips)])
         pairs = [(h, h ^ 1) for h in range(n)]
         mine = keep + lax.ppermute(away, axis, pairs)
-        out = lax.dynamic_index_in_dim(mine, chip, 1, False)
+        out = lax.dynamic_index_in_dim(mine, chip, 0, False)
         for shift in range(1, chips):
-            send = lax.dynamic_index_in_dim(mine, (chip + shift) % chips, 1, False)
+            send = lax.dynamic_index_in_dim(mine, (chip + shift) % chips, 0, False)
             pairs = [(2 * y + c, 2 * ((y + shift) % chips) + c) for y in range(chips) for c in range(2)]
             out = out + lax.ppermute(send, axis, pairs)
         return out

time: 136 us -> 126 us (0.926)
  local copies, waits for them, and re-layouts: 7.64 us -> 2.92 us
  other arithmetic: 9.34 us -> 4.76 us
    slice x1 -> x0, other arithmetic: 4.37 us -> none  [scatter_heads(): keep = jnp.where(core == 0, blocks[:, :, 0], blocks[:, :, 1])]
    reshape x1 -> x0, local copies, waits for them, and re-layouts: 2.8 us -> none  [scatter_heads(): blocks = partial.reshape(rows, chips, 2, width)]
where the time goes in v4:
time: 126 us
  waiting for transfers between devices  73.2 us (58%)
  starting transfers between devices  39.4 us (31%)
  other arithmetic  4.76 us (4%)
  matrix products  4.68 us (4%)
  local copies, waits for them, and re-layouts  2.92 us (2%)
    ppermute x7, waiting for transfers between devices, exclusive_scan(): got = lax.ppermute(send, axis, full)  52.4 us
    ppermute x1, starting transfers between devices, scatter_heads(): mine = keep + lax.ppermute(away, axis, pairs)  15.7 us
    ppermute x3, waiting for transfers between devices, scatter_heads(): out = out + lax.ppermute(send, axis, pairs)  10.4 us
    ppermute x7, starting transfers between devices, exclusive_scan(): got = lax.ppermute(send, axis, full)  10.1 us
    ppermute x3, starting transfers between devices, scatter_heads(): out = out + lax.ppermute(send, axis, pairs)  9.78 us
    ppermute x3, waiting for transfers between devices, exclusive_scan(): got = lax.ppermute(total, axis, pairs)  8.29 us
    ppermute x3, starting transfers between devices, exclusive_scan(): got = lax.ppermute(total, axis, pairs)  3.89 us
    dot_general x1, matrix products, shards(): jnp.dot(normed, out_weight, preferred_element_type=jnp.float32)  2.94 us
  transfers between devices with their start and end apart: 14, of which 10 were waited for; matrix products, arithmetic and copies ran while one was open for 1% of the time, Pallas kernels for 0%

profile of v4, /device:TPU:79, one launch (start us, length us, event | category | flops | bytes accessed | tf_op | source)
XLA Modules:
  0.0 125.7 jit_solution(11479366629283596914)
XLA Ops:
  0.0 1.0 reduce_window_sum.23
  2.1 1.0 copy.30
  3.1 0.9 reshape.85
  4.4 3.5 %collective-permute-start = (f32[4,136,128]{2,1,0:T(8,128)S(1)}, f32[4,136,128]{2,1,0:T(8,128)S(1)}, u32[]{:S(2)}, u32[]{:S(2)}) collective-permute-start(f32[4,136,128]{2,1,0:T(8,128)S(1)} %pad_maximum_fusion.1), channel_id=1, source_target_pairs={{0,8},{16,24},{32,40},{48,56},{64,72},{80,88},{96,104},{112,120},{... | collective-permute-start | bytes 835592 | tf_op jit(solution)/shard_map/ppermute | solution.py:114
  8.0 6.2 %collective-permute-done = f32[4,136,128]{2,1,0:T(8,128)S(1)} collective-permute-done((f32[4,136,128]{2,1,0:T(8,128)S(1)}, f32[4,136,128]{2,1,0:T(8,128)S(1)}, u32[]{:S(2)}, u32[]{:S(2)}) %collective-permute-start) | collective-permute-done | bytes 278560 | tf_op jit(solution)/shard_map/ppermute | solution.py:114
  14.4 1.3 %collective-permute-start.1 = (f32[4,136,128]{2,1,0:T(8,128)S(1)}, f32[4,136,128]{2,1,0:T(8,128)S(1)}, u32[]{:S(2)}, u32[]{:S(2)}) collective-permute-start(f32[4,136,128]{2,1,0:T(8,128)S(1)} %get-tuple-element.36), channel_id=1, source_target_pairs={{8,24},{40,56},{72,88},{104,120},{112,96},{80,64},{48,32},{16,0},{... | collective-permute-start | bytes 835592 | tf_op jit(solution)/shard_map/ppermute | solution.py:114
  15.8 4.6 %collective-permute-done.1 = f32[4,136,128]{2,1,0:T(8,128)S(1)} collective-permute-done((f32[4,136,128]{2,1,0:T(8,128)S(1)}, f32[4,136,128]{2,1,0:T(8,128)S(1)}, u32[]{:S(2)}, u32[]{:S(2)}) %collective-permute-start.1) | collective-permute-done | bytes 278560 | tf_op jit(solution)/shard_map/ppermute | solution.py:114
  23.3 1.3 %collective-permute-start.5 = (f32[4,136,128]{2,1,0:T(8,128)S(1)}, f32[4,136,128]{2,1,0:T(8,128)S(1)}, u32[]{:S(2)}, u32[]{:S(2)}) collective-permute-start(f32[4,136,128]{2,1,0:T(8,128)S(1)} %get-tuple-element.19), channel_id=1, source_target_pairs={{24,40},{56,72},{88,104},{96,80},{64,48},{32,16},{152,168},{184,20... | collective-permute-start | bytes 835592 | tf_op jit(solution)/shard_map/ppermute | solution.py:114
  24.7 34.1 %collective-permute-done.5 = f32[4,136,128]{2,1,0:T(8,128)S(1)} collective-permute-done((f32[4,136,128]{2,1,0:T(8,128)S(1)}, f32[4,136,128]{2,1,0:T(8,128)S(1)}, u32[]{:S(2)}, u32[]{:S(2)}) %collective-permute-start.5) | collective-permute-done | bytes 278560 | tf_op jit(solution)/shard_map/ppermute | solution.py:114
  59.0 1.9 %collective-permute-start.6 = (f32[4,136,128]{2,1,0:T(8,128)S(1)}, f32[4,136,128]{2,1,0:T(8,128)S(1)}, u32[]{:S(2)}, u32[]{:S(2)}) collective-permute-start(f32[4,136,128]{2,1,0:T(8,128)S(1)} %add_select_fusion), channel_id=1, source_target_pairs={{8,16},{24,32},{40,48},{56,64},{72,80},{88,96},{104,112},{112,104}... | collective-permute-start | bytes 835592 | tf_op jit(solution)/shard_map/ppermute | solution.py:114
  61.4 7.5 %collective-permute-done.6 = f32[4,136,128]{2,1,0:T(8,128)S(1)} collective-permute-done((f32[4,136,128]{2,1,0:T(8,128)S(1)}, f32[4,136,128]{2,1,0:T(8,128)S(1)}, u32[]{:S(2)}, u32[]{:S(2)}) %collective-permute-start.6) | collective-permute-done | bytes 278560 | tf_op jit(solution)/shard_map/ppermute | solution.py:114
  69.2 1.3 %collective-permute-start.8 = (f32[4,136,128]{2,1,0:T(8,128)S(1)}, f32[4,136,128]{2,1,0:T(8,128)S(1)}, u32[]{:S(2)}, u32[]{:S(2)}) collective-permute-start(f32[4,136,128]{2,1,0:T(8,128)S(1)} %get-tuple-element.17), channel_id=1, source_target_pairs={{0,256},{8,264},{16,272},{24,280},{32,288},{40,296},{48,304},{56,3... | collective-permute-start | bytes 835592 | tf_op jit(solution)/shard_map/ppermute | solution.py:128
  71.3 1.3 %collective-permute-start.7 = (f32[4,136,128]{2,1,0:T(8,128)S(1)}, f32[4,136,128]{2,1,0:T(8,128)S(1)}, u32[]{:S(2)}, u32[]{:S(2)}) collective-permute-start(f32[4,136,128]{2,1,0:T(8,128)S(1)} %get-tuple-element.17), channel_id=1, source_target_pairs={{0,128},{8,136},{16,144},{24,152},{32,160},{40,168},{48,176},{56,1... | collective-permute-start | bytes 835592 | tf_op jit(solution)/shard_map/ppermute | solution.py:128
  72.6 1.3 %collective-permute-start.9 = (f32[4,136,128]{2,1,0:T(8,128)S(1)}, f32[4,136,128]{2,1,0:T(8,128)S(1)}, u32[]{:S(2)}, u32[]{:S(2)}) collective-permute-start(f32[4,136,128]{2,1,0:T(8,128)S(1)} %get-tuple-element.17), channel_id=1, source_target_pairs={{0,384},{8,392},{16,400},{24,408},{32,416},{40,424},{48,432},{56,4... | collective-permute-start | bytes 835592 | tf_op jit(solution)/shard_map/ppermute | solution.py:128
  74.0 4.1 %collective-permute-done.8 = f32[4,136,128]{2,1,0:T(8,128)S(1)} collective-permute-done((f32[4,136,128]{2,1,0:T(8,128)S(1)}, f32[4,136,128]{2,1,0:T(8,128)S(1)}, u32[]{:S(2)}, u32[]{:S(2)}) %collective-permute-start.8) | collective-permute-done | bytes 278560 | tf_op jit(solution)/shard_map/ppermute | solution.py:128
  79.0 3.3 %collective-permute-done.9 = f32[4,136,128]{2,1,0:T(8,128)S(1)} collective-permute-done((f32[4,136,128]{2,1,0:T(8,128)S(1)}, f32[4,136,128]{2,1,0:T(8,128)S(1)}, u32[]{:S(2)}, u32[]{:S(2)}) %collective-permute-start.9) | collective-permute-done | bytes 278560 | tf_op jit(solution)/shard_map/ppermute | solution.py:128
  83.0 2.9 %fusion.52 = f32[128,4096]{1,0:T(8,128)S(1)} fusion(bf16[128,512]{0,1:T(8,128)(2,1)S(1)} %fusion.16, bf16[512,4096]{1,0:T(8,128)(2,1)} %param.13), kind=kOutput, calls=%fused_computation.130 | convolution fusion | flops 536870912 | bytes 6422528 | tf_op jit(solution)/shard_map/dot_general | solution.py:186
  86.3 15.7 %collective-permute-start.10 = (f32[4,128,512]{2,1,0:T(8,128)S(1)}, f32[4,128,512]{2,1,0:T(8,128)S(1)}, u32[]{:S(2)}, u32[]{:S(2)}) collective-permute-start(f32[4,128,512]{2,1,0:T(8,128)S(1)} %pad_maximum_fusion), channel_id=1, source_target_pairs={{0,1},{1,0},{2,3},{3,2},{4,5},{5,4},{6,7},{7,6},{8,9},{9,8},{10,11... | collective-permute-start | bytes 3145736 | tf_op jit(solution)/shard_map/ppermute | solution.py:148
  102.0 2.2 %collective-permute-done.10 = f32[4,128,512]{2,1,0:T(8,128)S(1)} collective-permute-done((f32[4,128,512]{2,1,0:T(8,128)S(1)}, f32[4,128,512]{2,1,0:T(8,128)S(1)}, u32[]{:S(2)}, u32[]{:S(2)}) %collective-permute-start.10) | collective-permute-done | bytes 1048608 | tf_op jit(solution)/shard_map/ppermute | solution.py:148
  104.5 3.2 %collective-permute-start.11 = (f32[128,512]{1,0:T(8,128)S(1)}, f32[128,512]{1,0:T(8,128)S(1)}, u32[]{:S(2)}, u32[]{:S(2)}) collective-permute-start(f32[128,512]{1,0:T(8,128)S(1)} %get-tuple-element.47), channel_id=1, source_target_pairs={{0,2},{1,3},{2,4},{3,5},{4,6},{5,7},{6,0},{7,1},{8,10},{9,11},{10,... | collective-permute-start | bytes 786440 | tf_op jit(solution)/shard_map/ppermute | solution.py:153
  107.7 2.6 %collective-permute-start.12 = (f32[128,512]{1,0:T(8,128)S(1)}, f32[128,512]{1,0:T(8,128)S(1)}, u32[]{:S(2)}, u32[]{:S(2)}) collective-permute-start(f32[128,512]{1,0:T(8,128)S(1)} %get-tuple-element.49), channel_id=1, source_target_pairs={{0,4},{1,5},{2,6},{3,7},{4,0},{5,1},{6,2},{7,3},{8,12},{9,13},{10,... | collective-permute-start | bytes 786440 | tf_op jit(solution)/shard_map/ppermute | solution.py:153
  110.4 4.0 %collective-permute-start.13 = (f32[128,512]{1,0:T(8,128)S(1)}, f32[128,512]{1,0:T(8,128)S(1)}, u32[]{:S(2)}, u32[]{:S(2)}) collective-permute-start(f32[128,512]{1,0:T(8,128)S(1)} %get-tuple-element.48), channel_id=1, source_target_pairs={{0,6},{1,7},{2,0},{3,1},{4,2},{5,3},{6,4},{7,5},{8,14},{9,15},{10,... | collective-permute-start | bytes 786440 | tf_op jit(solution)/shard_map/ppermute | solution.py:153
  114.6 3.8 %collective-permute-done.12 = f32[128,512]{1,0:T(8,128)S(1)} collective-permute-done((f32[128,512]{1,0:T(8,128)S(1)}, f32[128,512]{1,0:T(8,128)S(1)}, u32[]{:S(2)}, u32[]{:S(2)}) %collective-permute-start.12) | collective-permute-done | bytes 262176 | tf_op jit(solution)/shard_map/ppermute | solution.py:153
  118.4 6.6 %collective-permute-done.13 = f32[128,512]{1,0:T(8,128)S(1)} collective-permute-done((f32[128,512]{1,0:T(8,128)S(1)}, f32[128,512]{1,0:T(8,128)S(1)}, u32[]{:S(2)}, u32[]{:S(2)}) %collective-permute-start.13) | collective-permute-done | bytes 262176 | tf_op jit(solution)/shard_map/ppermute | solution.py:153
  (77 shorter events, 9.4 us)
Async XLA Ops:
  0.0 114.3 %copy-start = (bf16[16,512]{1,0:T(8,128)(2,1)S(1)}, bf16[16,512]{1,0:T(8,128)(2,1)}, u32[]{:S(2)}) copy-start(bf16[16,512]{1,0:T(8,128)(2,1)} %param.15) | copy-start | bytes 49156
  4.4 9.8 %collective-permute-start = (f32[4,136,128]{2,1,0:T(8,128)S(1)}, f32[4,136,128]{2,1,0:T(8,128)S(1)}, u32[]{:S(2)}, u32[]{:S(2)}) collective-permute-start(f32[4,136,128]{2,1,0:T(8,128)S(1)} %pad_maximum_fusion.1), channel_id=1, source_target_pairs={{0,8},{16,24},{32,40},{48,56},{64,72},{80,88},{96,104},{112,120},{... | collective-permute-start | bytes 835592 | tf_op jit(solution)/shard_map/ppermute | solution.py:114
  14.4 6.0 %collective-permute-start.1 = (f32[4,136,128]{2,1,0:T(8,128)S(1)}, f32[4,136,128]{2,1,0:T(8,128)S(1)}, u32[]{:S(2)}, u32[]{:S(2)}) collective-permute-start(f32[4,136,128]{2,1,0:T(8,128)S(1)} %get-tuple-element.36), channel_id=1, source_target_pairs={{8,24},{40,56},{72,88},{104,120},{112,96},{80,64},{48,32},{16,0},{... | collective-permute-start | bytes 835592 | tf_op jit(solution)/shard_map/ppermute | solution.py:114
  20.4 4.2 %copy-start.1 = (bf16[128,512]{1,0:T(8,128)(2,1)S(1)}, bf16[128,512]{1,0:T(8,128)(2,1)}, u32[]{:S(2)}) copy-start(bf16[128,512]{1,0:T(8,128)(2,1)} %param.8) | copy-start | bytes 393220
  20.7 0.7 collective-permute-start.2
  21.6 1.4 %collective-permute-start.3 = (f32[4,136,128]{2,1,0:T(8,128)S(1)}, f32[4,136,128]{2,1,0:T(8,128)S(1)}, u32[]{:S(2)}, u32[]{:S(2)}) collective-permute-start(f32[4,136,128]{2,1,0:T(8,128)S(1)} %get-tuple-element.30), channel_id=1, source_target_pairs={{56,120},{64,0},{184,248},{192,128},{312,376},{320,256},{440,504},... | collective-permute-start | bytes 835592 | tf_op jit(solution)/shard_map/ppermute | solution.py:114
  22.3 0.7 collective-permute-start.4
  23.3 47.6 %copy-start.2 = (f32[128,4]{0,1:T(4,128)S(1)}, f32[128,4]{0,1:T(4,128)}, u32[]{:S(2)}) copy-start(f32[128,4]{0,1:T(4,128)} %param.11) | copy-start | bytes 6148
  23.3 35.5 %collective-permute-start.5 = (f32[4,136,128]{2,1,0:T(8,128)S(1)}, f32[4,136,128]{2,1,0:T(8,128)S(1)}, u32[]{:S(2)}, u32[]{:S(2)}) collective-permute-start(f32[4,136,128]{2,1,0:T(8,128)S(1)} %get-tuple-element.19), channel_id=1, source_target_pairs={{24,40},{56,72},{88,104},{96,80},{64,48},{32,16},{152,168},{184,20... | collective-permute-start | bytes 835592 | tf_op jit(solution)/shard_map/ppermute | solution.py:114
  59.0 23.9 %copy-start.3 = (f32[512]{0:T(512)S(1)}, f32[512]{0:T(512)}, u32[]{:S(2)}) copy-start(f32[512]{0:T(512)} %param.12) | copy-start | bytes 6148
  59.0 9.8 %collective-permute-start.6 = (f32[4,136,128]{2,1,0:T(8,128)S(1)}, f32[4,136,128]{2,1,0:T(8,128)S(1)}, u32[]{:S(2)}, u32[]{:S(2)}) collective-permute-start(f32[4,136,128]{2,1,0:T(8,128)S(1)} %add_select_fusion), channel_id=1, source_target_pairs={{8,16},{24,32},{40,48},{56,64},{72,80},{88,96},{104,112},{112,104}... | collective-permute-start | bytes 835592 | tf_op jit(solution)/shard_map/ppermute | solution.py:114
  69.2 8.8 %collective-permute-start.8 = (f32[4,136,128]{2,1,0:T(8,128)S(1)}, f32[4,136,128]{2,1,0:T(8,128)S(1)}, u32[]{:S(2)}, u32[]{:S(2)}) collective-permute-start(f32[4,136,128]{2,1,0:T(8,128)S(1)} %get-tuple-element.17), channel_id=1, source_target_pairs={{0,256},{8,264},{16,272},{24,280},{32,288},{40,296},{48,304},{56,3... | collective-permute-start | bytes 835592 | tf_op jit(solution)/shard_map/ppermute | solution.py:128
  71.3 7.6 %collective-permute-start.7 = (f32[4,136,128]{2,1,0:T(8,128)S(1)}, f32[4,136,128]{2,1,0:T(8,128)S(1)}, u32[]{:S(2)}, u32[]{:S(2)}) collective-permute-start(f32[4,136,128]{2,1,0:T(8,128)S(1)} %get-tuple-element.17), channel_id=1, source_target_pairs={{0,128},{8,136},{16,144},{24,152},{32,160},{40,168},{48,176},{56,1... | collective-permute-start | bytes 835592 | tf_op jit(solution)/shard_map/ppermute | solution.py:128
  72.6 9.7 %collective-permute-start.9 = (f32[4,136,128]{2,1,0:T(8,128)S(1)}, f32[4,136,128]{2,1,0:T(8,128)S(1)}, u32[]{:S(2)}, u32[]{:S(2)}) collective-permute-start(f32[4,136,128]{2,1,0:T(8,128)S(1)} %get-tuple-element.17), channel_id=1, source_target_pairs={{0,384},{8,392},{16,400},{24,408},{32,416},{40,424},{48,432},{56,4... | collective-permute-start | bytes 835592 | tf_op jit(solution)/shard_map/ppermute | solution.py:128
  86.2 28.1 %copy-start.4 = (s32[128]{0:T(128)S(1)}, s32[128]{0:T(128)}, u32[]{:S(2)}) copy-start(s32[128]{0:T(128)} %param.14) | copy-start | bytes 1540
  86.3 17.9 %collective-permute-start.10 = (f32[4,128,512]{2,1,0:T(8,128)S(1)}, f32[4,128,512]{2,1,0:T(8,128)S(1)}, u32[]{:S(2)}, u32[]{:S(2)}) collective-permute-start(f32[4,128,512]{2,1,0:T(8,128)S(1)} %pad_maximum_fusion), channel_id=1, source_target_pairs={{0,1},{1,0},{2,3},{3,2},{4,5},{5,4},{6,7},{7,6},{8,9},{9,8},{10,11... | collective-permute-start | bytes 3145736 | tf_op jit(solution)/shard_map/ppermute | solution.py:148
  104.5 10.1 %collective-permute-start.11 = (f32[128,512]{1,0:T(8,128)S(1)}, f32[128,512]{1,0:T(8,128)S(1)}, u32[]{:S(2)}, u32[]{:S(2)}) collective-permute-start(f32[128,512]{1,0:T(8,128)S(1)} %get-tuple-element.47), channel_id=1, source_target_pairs={{0,2},{1,3},{2,4},{3,5},{4,6},{5,7},{6,0},{7,1},{8,10},{9,11},{10,... | collective-permute-start | bytes 786440 | tf_op jit(solution)/shard_map/ppermute | solution.py:153
  107.7 10.6 %collective-permute-start.12 = (f32[128,512]{1,0:T(8,128)S(1)}, f32[128,512]{1,0:T(8,128)S(1)}, u32[]{:S(2)}, u32[]{:S(2)}) collective-permute-start(f32[128,512]{1,0:T(8,128)S(1)} %get-tuple-element.49), channel_id=1, source_target_pairs={{0,4},{1,5},{2,6},{3,7},{4,0},{5,1},{6,2},{7,3},{8,12},{9,13},{10,... | collective-permute-start | bytes 786440 | tf_op jit(solution)/shard_map/ppermute | solution.py:153
  110.4 14.6 %collective-permute-start.13 = (f32[128,512]{1,0:T(8,128)S(1)}, f32[128,512]{1,0:T(8,128)S(1)}, u32[]{:S(2)}, u32[]{:S(2)}) collective-permute-start(f32[128,512]{1,0:T(8,128)S(1)} %get-tuple-element.48), channel_id=1, source_target_pairs={{0,6},{1,7},{2,0},{3,1},{4,2},{5,3},{6,4},{7,5},{8,14},{9,15},{10,... | collective-permute-start | bytes 786440 | tf_op jit(solution)/shard_map/ppermute | solution.py:153

commit v5 on v4

--- a/solution.py
+++ b/solution.py
@@ -43,52 +43,6 @@
     return scale * earlier + later
 
 
-def bk_rounds(n):
-    top = 1
-    while top < n:
-        top *= 2
-    levels = top.bit_length() - 1
-    ups = []
-    for k in range(levels):
-        step = 1 << k
-        ups.append([(p - step, p) for p in range(2 * step - 1, n, 2 * step)])
-    downs = []
-    for k in range(levels - 1, -1, -1):
-        step = 1 << k
-        downs.append([(p - step, p) for p in range(3 * step - 1, n, 2 * step)])
-    rounds = ups[:-1]
-    tail = ups[-1] if ups else []
-    downs = [d for d in downs if d]
-    if tail and downs and all(s == tail[0][0] for s, _ in tail) and downs[0][0][0] == tail[0][0]:
-        rounds.append(tail + downs[0])
-        rounds.extend(downs[1:])
-    else:
-        if tail:
-            rounds.append(tail)
-        rounds.extend(downs)
-    return [r for r in rounds if r]
-
-
-def unique_sources(pairs):
-    groups = []
-    for pair in pairs:
-        for group in groups:
-            if all(pair[0] != other[0] for other in group):
-                group.append(pair)
-                break
-        else:
-            groups.append([pair])
-    return groups
-
-
-def receive(value, axis, pairs):
-    got = None
-    for group in unique_sources(pairs):
-        one = lax.ppermute(value, axis, group)
-        got = one if got is None else got + one
-    return got
-
-
 def member(position, spots):
     bits = 0
     for spot in spots:
@@ -96,26 +50,42 @@
     return ((jnp.int32(bits) >> position) & 1) == 1
 
 
+def line_rounds(width):
+    levels = width.bit_length() - 1
+    rounds = []
+
+    def both(pairs):
+        fwd = [(s, d, True, True) for s, d in pairs]
+        bwd = [(width - 1 - s, width - 1 - d, False, False) for s, d in pairs]
+        return fwd + bwd
+
+    for k in range(levels - 1):
+        step = 1 << k
+        rounds.append(both([(p - step, p) for p in range(2 * step - 1, width, 2 * step)]))
+    if width >= 2:
+        close = [(0, width - 1, False, True), (width - 1, 0, True, False)]
+        if levels >= 2:
+            step = width // 4
+            close += both([(width // 2 - 1, 3 * step - 1)])
+        rounds.append(close)
+    for k in range(levels - 3, -1, -1):
+        step = 1 << k
+        rounds.append(both([(p - step, p) for p in range(3 * step - 1, width, 2 * step)]))
+    return rounds
+
+
 def exclusive_scan(part, axis, lines, width):
     pos = lax.axis_index(axis) % width
     held = part
     before = jnp.zeros_like(part)
     after = part
-    for pairs in bk_rounds(width):
-        fwd_groups = unique_sources(pairs)
-        ahead = None
-        behind = None
-        for group in fwd_groups:
-            back = [(width - 1 - s, width - 1 - d) for s, d in group]
-            both = group + back
-            assert len({s for s, _ in both}) == len(both) and len({d for _, d in both}) == len(both)
-            send = jnp.where(member(pos, [s for s, _ in group]), held, after)
-            full = [(l * width + s, l * width + d) for l in range(lines) for s, d in both]
-            got = lax.ppermute(send, axis, full)
-            one_ahead = jnp.where(member(pos, [d for _, d in group]), got, 0.0)
-            one_behind = jnp.where(member(pos, [d for _, d in back]), got, 0.0)
-            ahead = one_ahead if ahead is None else ahead + one_ahead
-            behind = one_behind if behind is None else behind + one_behind
+    for entries in line_rounds(width):
+        assert len({e[0] for e in entries}) == len(entries) and len({e[1] for e in entries}) == len(entries)
+        send = jnp.where(member(pos, [e[0] for e in entries if e[2]]), held, after)
+        full = [(l * width + e[0], l * width + e[1]) for l in range(lines) for e in entries]
+        got = lax.ppermute(send, axis, full)
+        ahead = jnp.where(member(pos, [e[1] for e in entries if e[3]]), got, 0.0)
+        behind = jnp.where(member(pos, [e[1] for e in entries if not e[3]]), got, 0.0)
         held = join(ahead, held)
         before = join(ahead, before)
         after = join(after, behind)

time: 126 us -> 121 us (0.960)
  waiting for transfers between devices: 73.2 us -> 70.3 us
  starting transfers between devices: 39.4 us -> 36.6 us
    ppermute x7 -> x6, waiting for transfers between devices: 52.4 us -> 49.5 us  [exclusive_scan(): got = lax.ppermute(send, axis, full)]
    ppermute x1, starting transfers between devices: 15.7 us -> 13.5 us  [scatter_heads(): mine = keep + lax.ppermute(away, axis, pairs)]
    ppermute x7 -> x6, starting transfers between devices: 10.1 us -> 9.42 us  [exclusive_scan(): got = lax.ppermute(send, axis, full)]
  transfers between devices with their start and end apart: 14 -> 13, of which waited for: 10 -> 10; matrix products, arithmetic and copies ran while one was open for 1% -> 1% of each run, Pallas kernels for 0% -> 0%
where the time goes in v5:
time: 121 us; the launch traced here: 120 us
  waiting for transfers between devices  70.3 us (58%)
  starting transfers between devices  36.6 us (30%)
  other arithmetic  4.74 us (4%)
  matrix products  4.7 us (4%)
  local copies, waits for them, and re-layouts  2.92 us (2%)
    ppermute x6, waiting for transfers between devices, exclusive_scan(): got = lax.ppermute(send, axis, full)  49.5 us
    ppermute x1, starting transfers between devices, scatter_heads(): mine = keep + lax.ppermute(away, axis, pairs)  13.5 us
    ppermute x3, waiting for transfers between devices, scatter_heads(): out = out + lax.ppermute(send, axis, pairs)  10.4 us
    ppermute x3, starting transfers between devices, scatter_heads(): out = out + lax.ppermute(send, axis, pairs)  9.81 us
    ppermute x6, starting transfers between devices, exclusive_scan(): got = lax.ppermute(send, axis, full)  9.42 us
    ppermute x3, waiting for transfers between devices, exclusive_scan(): got = lax.ppermute(total, axis, pairs)  8.3 us
    ppermute x3, starting transfers between devices, exclusive_scan(): got = lax.ppermute(total, axis, pairs)  3.89 us
    dot_general x1, matrix products, shards(): jnp.dot(normed, out_weight, preferred_element_type=jnp.float32)  2.94 us
  transfers between devices with their start and end apart: 13, of which 10 were waited for; matrix products, arithmetic and copies ran while one was open for 1% of the time, Pallas kernels for 0%

profile of v5, /device:TPU:79, one launch (start us, length us, event | category | flops | bytes accessed | tf_op | source)
XLA Modules:
  0.0 120.0 jit_solution(8795284116664629913)
XLA Ops:
  0.0 1.0 reduce_window_sum.23
  2.1 1.0 copy.30
  3.1 0.9 reshape.85
  4.4 3.5 %collective-permute-start = (f32[4,136,128]{2,1,0:T(8,128)S(1)}, f32[4,136,128]{2,1,0:T(8,128)S(1)}, u32[]{:S(2)}, u32[]{:S(2)}) collective-permute-start(f32[4,136,128]{2,1,0:T(8,128)S(1)} %pad_maximum_fusion.1), channel_id=1, source_target_pairs={{0,8},{16,24},{32,40},{48,56},{64,72},{80,88},{96,104},{112,120},{... | collective-permute-start | bytes 835592 | tf_op jit(solution)/shard_map/ppermute | solution.py:86
  8.0 6.2 %collective-permute-done = f32[4,136,128]{2,1,0:T(8,128)S(1)} collective-permute-done((f32[4,136,128]{2,1,0:T(8,128)S(1)}, f32[4,136,128]{2,1,0:T(8,128)S(1)}, u32[]{:S(2)}, u32[]{:S(2)}) %collective-permute-start) | collective-permute-done | bytes 278560 | tf_op jit(solution)/shard_map/ppermute | solution.py:86
  14.4 1.3 %collective-permute-start.1 = (f32[4,136,128]{2,1,0:T(8,128)S(1)}, f32[4,136,128]{2,1,0:T(8,128)S(1)}, u32[]{:S(2)}, u32[]{:S(2)}) collective-permute-start(f32[4,136,128]{2,1,0:T(8,128)S(1)} %get-tuple-element.36), channel_id=1, source_target_pairs={{8,24},{40,56},{72,88},{104,120},{112,96},{80,64},{48,32},{16,0},{... | collective-permute-start | bytes 835592 | tf_op jit(solution)/shard_map/ppermute | solution.py:86
  15.8 4.6 %collective-permute-done.1 = f32[4,136,128]{2,1,0:T(8,128)S(1)} collective-permute-done((f32[4,136,128]{2,1,0:T(8,128)S(1)}, f32[4,136,128]{2,1,0:T(8,128)S(1)}, u32[]{:S(2)}, u32[]{:S(2)}) %collective-permute-start.1) | collective-permute-done | bytes 278560 | tf_op jit(solution)/shard_map/ppermute | solution.py:86
  22.6 1.3 %collective-permute-start.4 = (f32[4,136,128]{2,1,0:T(8,128)S(1)}, f32[4,136,128]{2,1,0:T(8,128)S(1)}, u32[]{:S(2)}, u32[]{:S(2)}) collective-permute-start(f32[4,136,128]{2,1,0:T(8,128)S(1)} %get-tuple-element.19), channel_id=1, source_target_pairs={{24,40},{56,72},{88,104},{96,80},{64,48},{32,16},{152,168},{184,20... | collective-permute-start | bytes 835592 | tf_op jit(solution)/shard_map/ppermute | solution.py:86
  24.0 33.5 %collective-permute-done.4 = f32[4,136,128]{2,1,0:T(8,128)S(1)} collective-permute-done((f32[4,136,128]{2,1,0:T(8,128)S(1)}, f32[4,136,128]{2,1,0:T(8,128)S(1)}, u32[]{:S(2)}, u32[]{:S(2)}) %collective-permute-start.4) | collective-permute-done | bytes 278560 | tf_op jit(solution)/shard_map/ppermute | solution.py:86
  57.7 1.9 %collective-permute-start.5 = (f32[4,136,128]{2,1,0:T(8,128)S(1)}, f32[4,136,128]{2,1,0:T(8,128)S(1)}, u32[]{:S(2)}, u32[]{:S(2)}) collective-permute-start(f32[4,136,128]{2,1,0:T(8,128)S(1)} %add_select_fusion), channel_id=1, source_target_pairs={{8,16},{24,32},{40,48},{56,64},{72,80},{88,96},{104,112},{112,104}... | collective-permute-start | bytes 835592 | tf_op jit(solution)/shard_map/ppermute | solution.py:86
  60.0 5.2 %collective-permute-done.5 = f32[4,136,128]{2,1,0:T(8,128)S(1)} collective-permute-done((f32[4,136,128]{2,1,0:T(8,128)S(1)}, f32[4,136,128]{2,1,0:T(8,128)S(1)}, u32[]{:S(2)}, u32[]{:S(2)}) %collective-permute-start.5) | collective-permute-done | bytes 278560 | tf_op jit(solution)/shard_map/ppermute | solution.py:86
  65.6 1.3 %collective-permute-start.7 = (f32[4,136,128]{2,1,0:T(8,128)S(1)}, f32[4,136,128]{2,1,0:T(8,128)S(1)}, u32[]{:S(2)}, u32[]{:S(2)}) collective-permute-start(f32[4,136,128]{2,1,0:T(8,128)S(1)} %get-tuple-element.17), channel_id=1, source_target_pairs={{0,256},{8,264},{16,272},{24,280},{32,288},{40,296},{48,304},{56,3... | collective-permute-start | bytes 835592 | tf_op jit(solution)/shard_map/ppermute | solution.py:98
  67.7 1.3 %collective-permute-start.6 = (f32[4,136,128]{2,1,0:T(8,128)S(1)}, f32[4,136,128]{2,1,0:T(8,128)S(1)}, u32[]{:S(2)}, u32[]{:S(2)}) collective-permute-start(f32[4,136,128]{2,1,0:T(8,128)S(1)} %get-tuple-element.17), channel_id=1, source_target_pairs={{0,128},{8,136},{16,144},{24,152},{32,160},{40,168},{48,176},{56,1... | collective-permute-start | bytes 835592 | tf_op jit(solution)/shard_map/ppermute | solution.py:98
  69.0 1.3 %collective-permute-start.8 = (f32[4,136,128]{2,1,0:T(8,128)S(1)}, f32[4,136,128]{2,1,0:T(8,128)S(1)}, u32[]{:S(2)}, u32[]{:S(2)}) collective-permute-start(f32[4,136,128]{2,1,0:T(8,128)S(1)} %get-tuple-element.17), channel_id=1, source_target_pairs={{0,384},{8,392},{16,400},{24,408},{32,416},{40,424},{48,432},{56,4... | collective-permute-start | bytes 835592 | tf_op jit(solution)/shard_map/ppermute | solution.py:98
  70.4 4.1 %collective-permute-done.7 = f32[4,136,128]{2,1,0:T(8,128)S(1)} collective-permute-done((f32[4,136,128]{2,1,0:T(8,128)S(1)}, f32[4,136,128]{2,1,0:T(8,128)S(1)}, u32[]{:S(2)}, u32[]{:S(2)}) %collective-permute-start.7) | collective-permute-done | bytes 278560 | tf_op jit(solution)/shard_map/ppermute | solution.py:98
  75.1 3.6 %collective-permute-done.8 = f32[4,136,128]{2,1,0:T(8,128)S(1)} collective-permute-done((f32[4,136,128]{2,1,0:T(8,128)S(1)}, f32[4,136,128]{2,1,0:T(8,128)S(1)}, u32[]{:S(2)}, u32[]{:S(2)}) %collective-permute-start.8) | collective-permute-done | bytes 278560 | tf_op jit(solution)/shard_map/ppermute | solution.py:98
  79.4 2.9 %fusion.52 = f32[128,4096]{1,0:T(8,128)S(1)} fusion(bf16[128,512]{0,1:T(8,128)(2,1)S(1)} %fusion.16, bf16[512,4096]{1,0:T(8,128)(2,1)} %param.13), kind=kOutput, calls=%fused_computation.129 | convolution fusion | flops 536870912 | bytes 6422528 | tf_op jit(solution)/shard_map/dot_general | solution.py:156
  82.7 13.5 %collective-permute-start.9 = (f32[4,128,512]{2,1,0:T(8,128)S(1)}, f32[4,128,512]{2,1,0:T(8,128)S(1)}, u32[]{:S(2)}, u32[]{:S(2)}) collective-permute-start(f32[4,128,512]{2,1,0:T(8,128)S(1)} %pad_maximum_fusion), channel_id=1, source_target_pairs={{0,1},{1,0},{2,3},{3,2},{4,5},{5,4},{6,7},{7,6},{8,9},{9,8},{10,11... | collective-permute-start | bytes 3145736 | tf_op jit(solution)/shard_map/ppermute | solution.py:118
  96.3 2.2 %collective-permute-done.9 = f32[4,128,512]{2,1,0:T(8,128)S(1)} collective-permute-done((f32[4,128,512]{2,1,0:T(8,128)S(1)}, f32[4,128,512]{2,1,0:T(8,128)S(1)}, u32[]{:S(2)}, u32[]{:S(2)}) %collective-permute-start.9) | collective-permute-done | bytes 1048608 | tf_op jit(solution)/shard_map/ppermute | solution.py:118
  98.7 3.2 %collective-permute-start.10 = (f32[128,512]{1,0:T(8,128)S(1)}, f32[128,512]{1,0:T(8,128)S(1)}, u32[]{:S(2)}, u32[]{:S(2)}) collective-permute-start(f32[128,512]{1,0:T(8,128)S(1)} %get-tuple-element.47), channel_id=1, source_target_pairs={{0,2},{1,3},{2,4},{3,5},{4,6},{5,7},{6,0},{7,1},{8,10},{9,11},{10,... | collective-permute-start | bytes 786440 | tf_op jit(solution)/shard_map/ppermute | solution.py:123
  102.0 2.6 %collective-permute-start.11 = (f32[128,512]{1,0:T(8,128)S(1)}, f32[128,512]{1,0:T(8,128)S(1)}, u32[]{:S(2)}, u32[]{:S(2)}) collective-permute-start(f32[128,512]{1,0:T(8,128)S(1)} %get-tuple-element.49), channel_id=1, source_target_pairs={{0,4},{1,5},{2,6},{3,7},{4,0},{5,1},{6,2},{7,3},{8,12},{9,13},{10,... | collective-permute-start | bytes 786440 | tf_op jit(solution)/shard_map/ppermute | solution.py:123
  104.6 4.0 %collective-permute-start.12 = (f32[128,512]{1,0:T(8,128)S(1)}, f32[128,512]{1,0:T(8,128)S(1)}, u32[]{:S(2)}, u32[]{:S(2)}) collective-permute-start(f32[128,512]{1,0:T(8,128)S(1)} %get-tuple-element.48), channel_id=1, source_target_pairs={{0,6},{1,7},{2,0},{3,1},{4,2},{5,3},{6,4},{7,5},{8,14},{9,15},{10,... | collective-permute-start | bytes 786440 | tf_op jit(solution)/shard_map/ppermute | solution.py:123
  108.9 3.8 %collective-permute-done.11 = f32[128,512]{1,0:T(8,128)S(1)} collective-permute-done((f32[128,512]{1,0:T(8,128)S(1)}, f32[128,512]{1,0:T(8,128)S(1)}, u32[]{:S(2)}, u32[]{:S(2)}) %collective-permute-start.11) | collective-permute-done | bytes 262176 | tf_op jit(solution)/shard_map/ppermute | solution.py:123
  112.6 6.6 %collective-permute-done.12 = f32[128,512]{1,0:T(8,128)S(1)} collective-permute-done((f32[128,512]{1,0:T(8,128)S(1)}, f32[128,512]{1,0:T(8,128)S(1)}, u32[]{:S(2)}, u32[]{:S(2)}) %collective-permute-start.12) | collective-permute-done | bytes 262176 | tf_op jit(solution)/shard_map/ppermute | solution.py:123
  (75 shorter events, 8.4 us)
Async XLA Ops:
  0.0 108.6 %copy-start = (bf16[16,512]{1,0:T(8,128)(2,1)S(1)}, bf16[16,512]{1,0:T(8,128)(2,1)}, u32[]{:S(2)}) copy-start(bf16[16,512]{1,0:T(8,128)(2,1)} %param.15) | copy-start | bytes 49156
  4.4 9.8 %collective-permute-start = (f32[4,136,128]{2,1,0:T(8,128)S(1)}, f32[4,136,128]{2,1,0:T(8,128)S(1)}, u32[]{:S(2)}, u32[]{:S(2)}) collective-permute-start(f32[4,136,128]{2,1,0:T(8,128)S(1)} %pad_maximum_fusion.1), channel_id=1, source_target_pairs={{0,8},{16,24},{32,40},{48,56},{64,72},{80,88},{96,104},{112,120},{... | collective-permute-start | bytes 835592 | tf_op jit(solution)/shard_map/ppermute | solution.py:86
  14.4 6.0 %collective-permute-start.1 = (f32[4,136,128]{2,1,0:T(8,128)S(1)}, f32[4,136,128]{2,1,0:T(8,128)S(1)}, u32[]{:S(2)}, u32[]{:S(2)}) collective-permute-start(f32[4,136,128]{2,1,0:T(8,128)S(1)} %get-tuple-element.36), channel_id=1, source_target_pairs={{8,24},{40,56},{72,88},{104,120},{112,96},{80,64},{48,32},{16,0},{... | collective-permute-start | bytes 835592 | tf_op jit(solution)/shard_map/ppermute | solution.py:86
  20.4 3.5 %copy-start.1 = (bf16[128,512]{1,0:T(8,128)(2,1)S(1)}, bf16[128,512]{1,0:T(8,128)(2,1)}, u32[]{:S(2)}) copy-start(bf16[128,512]{1,0:T(8,128)(2,1)} %param.8) | copy-start | bytes 393220
  20.7 0.7 collective-permute-start.2
  21.6 0.7 collective-permute-start.3
  22.6 44.7 %copy-start.2 = (f32[128,4]{0,1:T(4,128)S(1)}, f32[128,4]{0,1:T(4,128)}, u32[]{:S(2)}) copy-start(f32[128,4]{0,1:T(4,128)} %param.11) | copy-start | bytes 6148
  22.6 34.9 %collective-permute-start.4 = (f32[4,136,128]{2,1,0:T(8,128)S(1)}, f32[4,136,128]{2,1,0:T(8,128)S(1)}, u32[]{:S(2)}, u32[]{:S(2)}) collective-permute-start(f32[4,136,128]{2,1,0:T(8,128)S(1)} %get-tuple-element.19), channel_id=1, source_target_pairs={{24,40},{56,72},{88,104},{96,80},{64,48},{32,16},{152,168},{184,20... | collective-permute-start | bytes 835592 | tf_op jit(solution)/shard_map/ppermute | solution.py:86
  57.7 21.6 %copy-start.3 = (f32[512]{0:T(512)S(1)}, f32[512]{0:T(512)}, u32[]{:S(2)}) copy-start(f32[512]{0:T(512)} %param.12) | copy-start | bytes 6148
  57.7 7.6 %collective-permute-start.5 = (f32[4,136,128]{2,1,0:T(8,128)S(1)}, f32[4,136,128]{2,1,0:T(8,128)S(1)}, u32[]{:S(2)}, u32[]{:S(2)}) collective-permute-start(f32[4,136,128]{2,1,0:T(8,128)S(1)} %add_select_fusion), channel_id=1, source_target_pairs={{8,16},{24,32},{40,48},{56,64},{72,80},{88,96},{104,112},{112,104}... | collective-permute-start | bytes 835592 | tf_op jit(solution)/shard_map/ppermute | solution.py:86
  65.6 8.8 %collective-permute-start.7 = (f32[4,136,128]{2,1,0:T(8,128)S(1)}, f32[4,136,128]{2,1,0:T(8,128)S(1)}, u32[]{:S(2)}, u32[]{:S(2)}) collective-permute-start(f32[4,136,128]{2,1,0:T(8,128)S(1)} %get-tuple-element.17), channel_id=1, source_target_pairs={{0,256},{8,264},{16,272},{24,280},{32,288},{40,296},{48,304},{56,3... | collective-permute-start | bytes 835592 | tf_op jit(solution)/shard_map/ppermute | solution.py:98
  67.7 7.3 %collective-permute-start.6 = (f32[4,136,128]{2,1,0:T(8,128)S(1)}, f32[4,136,128]{2,1,0:T(8,128)S(1)}, u32[]{:S(2)}, u32[]{:S(2)}) collective-permute-start(f32[4,136,128]{2,1,0:T(8,128)S(1)} %get-tuple-element.17), channel_id=1, source_target_pairs={{0,128},{8,136},{16,144},{24,152},{32,160},{40,168},{48,176},{56,1... | collective-permute-start | bytes 835592 | tf_op jit(solution)/shard_map/ppermute | solution.py:98
  69.0 9.7 %collective-permute-start.8 = (f32[4,136,128]{2,1,0:T(8,128)S(1)}, f32[4,136,128]{2,1,0:T(8,128)S(1)}, u32[]{:S(2)}, u32[]{:S(2)}) collective-permute-start(f32[4,136,128]{2,1,0:T(8,128)S(1)} %get-tuple-element.17), channel_id=1, source_target_pairs={{0,384},{8,392},{16,400},{24,408},{32,416},{40,424},{48,432},{56,4... | collective-permute-start | bytes 835592 | tf_op jit(solution)/shard_map/ppermute | solution.py:98
  82.6 26.0 %copy-start.4 = (s32[128]{0:T(128)S(1)}, s32[128]{0:T(128)}, u32[]{:S(2)}) copy-start(s32[128]{0:T(128)} %param.14) | copy-start | bytes 1540
  82.7 15.7 %collective-permute-start.9 = (f32[4,128,512]{2,1,0:T(8,128)S(1)}, f32[4,128,512]{2,1,0:T(8,128)S(1)}, u32[]{:S(2)}, u32[]{:S(2)}) collective-permute-start(f32[4,128,512]{2,1,0:T(8,128)S(1)} %pad_maximum_fusion), channel_id=1, source_target_pairs={{0,1},{1,0},{2,3},{3,2},{4,5},{5,4},{6,7},{7,6},{8,9},{9,8},{10,11... | collective-permute-start | bytes 3145736 | tf_op jit(solution)/shard_map/ppermute | solution.py:118
  98.7 10.1 %collective-permute-start.10 = (f32[128,512]{1,0:T(8,128)S(1)}, f32[128,512]{1,0:T(8,128)S(1)}, u32[]{:S(2)}, u32[]{:S(2)}) collective-permute-start(f32[128,512]{1,0:T(8,128)S(1)} %get-tuple-element.47), channel_id=1, source_target_pairs={{0,2},{1,3},{2,4},{3,5},{4,6},{5,7},{6,0},{7,1},{8,10},{9,11},{10,... | collective-permute-start | bytes 786440 | tf_op jit(solution)/shard_map/ppermute | solution.py:123
  102.0 10.6 %collective-permute-start.11 = (f32[128,512]{1,0:T(8,128)S(1)}, f32[128,512]{1,0:T(8,128)S(1)}, u32[]{:S(2)}, u32[]{:S(2)}) collective-permute-start(f32[128,512]{1,0:T(8,128)S(1)} %get-tuple-element.49), channel_id=1, source_target_pairs={{0,4},{1,5},{2,6},{3,7},{4,0},{5,1},{6,2},{7,3},{8,12},{9,13},{10,... | collective-permute-start | bytes 786440 | tf_op jit(solution)/shard_map/ppermute | solution.py:123
  104.6 14.6 %collective-permute-start.12 = (f32[128,512]{1,0:T(8,128)S(1)}, f32[128,512]{1,0:T(8,128)S(1)}, u32[]{:S(2)}, u32[]{:S(2)}) collective-permute-start(f32[128,512]{1,0:T(8,128)S(1)} %get-tuple-element.48), channel_id=1, source_target_pairs={{0,6},{1,7},{2,0},{3,1},{4,2},{5,3},{6,4},{7,5},{8,14},{9,15},{10,... | collective-permute-start | bytes 786440 | tf_op jit(solution)/shard_map/ppermute | solution.py:123

commit v6 on v5

--- a/solution.py
+++ b/solution.py
@@ -74,30 +74,37 @@
     return rounds
 
 
-def exclusive_scan(part, axis, lines, width):
+def exclusive_scan(parts, axis, lines, width):
     pos = lax.axis_index(axis) % width
-    held = part
-    before = jnp.zeros_like(part)
-    after = part
+    held = list(parts)
+    before = [jnp.zeros_like(p) for p in parts]
+    after = list(parts)
+    if len(parts) > 1:
+        held, before, after = lax.optimization_barrier((held, before, after))
     for entries in line_rounds(width):
         assert len({e[0] for e in entries}) == len(entries) and len({e[1] for e in entries}) == len(entries)
-        send = jnp.where(member(pos, [e[0] for e in entries if e[2]]), held, after)
         full = [(l * width + e[0], l * width + e[1]) for l in range(lines) for e in entries]
-        got = lax.ppermute(send, axis, full)
-        ahead = jnp.where(member(pos, [e[1] for e in entries if e[3]]), got, 0.0)
-        behind = jnp.where(member(pos, [e[1] for e in entries if not e[3]]), got, 0.0)
-        held = join(ahead, held)
-        before = join(ahead, before)
-        after = join(after, behind)
-    total = join(before, after)
+        sends_held = member(pos, [e[0] for e in entries if e[2]])
+        into_ahead = member(pos, [e[1] for e in entries if e[3]])
+        into_behind = member(pos, [e[1] for e in entries if not e[3]])
+        got = [lax.ppermute(jnp.where(sends_held, h, a), axis, full) for h, a in zip(held, after)]
+        for i, g in enumerate(got):
+            ahead = jnp.where(into_ahead, g, 0.0)
+            behind = jnp.where(into_behind, g, 0.0)
+            held[i] = join(ahead, held[i])
+            before[i] = join(ahead, before[i])
+            after[i] = join(after[i], behind)
+        if len(parts) > 1:
+            held, before, after = lax.optimization_barrier((held, before, after))
     if lines == 1:
         return before
-    earlier = None
+    total = [join(b, a) for b, a in zip(before, after)]
+    earlier = [None] * len(parts)
     for shift in range(lines - 1, 0, -1):
         pairs = [((l - shift) * width + p, l * width + p) for l in range(shift, lines) for p in range(width)]
-        got = lax.ppermute(total, axis, pairs)
-        earlier = got if earlier is None else join(earlier, got)
-    return join(earlier, before)
+        got = [lax.ppermute(t, axis, pairs) for t in total]
+        earlier = [g if e is None else join(e, g) for e, g in zip(earlier, got)]
+    return [join(e, b) for e, b in zip(earlier, before)]
 
 
 def scatter_heads(partial, axis, n):
@@ -142,7 +149,11 @@
     )
     device_log = jnp.sum(log_decay, axis=0)
     lines, width = seq_n // seq_width, seq_width
-    passed = exclusive_scan(pack(device_log, local_memory), "seq", lines, width)
+    packed = pack(device_log, local_memory)
+    streams = 2 if heads_here % 2 == 0 else 1
+    passed = jnp.concatenate(
+        exclusive_scan(jnp.split(packed, streams, axis=0), "seq", lines, width), axis=0
+    )
     earlier_memory = passed[:, :head_size, :]
     running = jnp.cumsum(log_decay, axis=0)
     query_heads = queries.reshape(tok_rows, heads_here, head_size).astype(jnp.float32)

time: 121 us -> 123 us (1.017)
  the two profiles are of different devices: /device:TPU:79 before, /device:TPU:47 now
where the time goes in v6:
time: 123 us; the launch traced here: 122 us
  starting transfers between devices  79.7 us (65%)
  waiting for transfers between devices  29.5 us (24%)
  other arithmetic  5.78 us (5%)
  local copies, waits for them, and re-layouts  3.93 us (3%)
  matrix products  2.43 us (2%)
    ppermute x12, starting transfers between devices, exclusive_scan(): lax.ppermute(jnp.where(sends_held, h, a), axis, full)  49.8 us
    ppermute x1, starting transfers between devices, scatter_heads(): mine = keep + lax.ppermute(away, axis, pairs)  12.4 us
    ppermute x3, waiting for transfers between devices, scatter_heads(): out = out + lax.ppermute(send, axis, pairs)  10.4 us
    ppermute x3, starting transfers between devices, scatter_heads(): out = out + lax.ppermute(send, axis, pairs)  9.81 us
    ppermute x12, waiting for transfers between devices, exclusive_scan(): lax.ppermute(jnp.where(sends_held, h, a), axis, full)  8.68 us
    ppermute x6, waiting for transfers between devices, exclusive_scan(): got = [lax.ppermute(t, axis, pairs) for t in total]  8.27 us
    ppermute x6, starting transfers between devices, exclusive_scan(): got = [lax.ppermute(t, axis, pairs) for t in total]  7.75 us
    reshape x3, local copies, waits for them, and re-layouts, split(): array.reshape(count, SPAN, heads_here, head_size).transpose(0, 2, 1, 3)  2.91 us
  transfers between devices with their start and end apart: 22, of which 13 were waited for; matrix products, arithmetic and copies ran while one was open for 3% of the time, Pallas kernels for 0%

profile of v6, /device:TPU:47, one launch (start us, length us, event | category | flops | bytes accessed | tf_op | source)
XLA Modules:
  0.0 122.4 jit_solution(1324309029165252039)
XLA Ops:
  4.5 1.9 %collective-permute-start.1 = (f32[2,136,128]{2,1,0:T(8,128)S(1)}, f32[2,136,128]{2,1,0:T(8,128)S(1)}, u32[]{:S(2)}, u32[]{:S(2)}) collective-permute-start(f32[2,136,128]{2,1,0:T(8,128)S(1)} %broadcast_select_fusion.22), channel_id=1, source_target_pairs={{0,8},{16,24},{32,40},{48,56},{64,72},{80,88},{96,104},{112,120},{... | collective-permute-start | bytes 417800 | tf_op jit(solution)/shard_map/ppermute | solution.py:90
  6.5 3.4 %collective-permute-start = (f32[2,136,128]{2,1,0:T(8,128)S(1)}, f32[2,136,128]{2,1,0:T(8,128)S(1)}, u32[]{:S(2)}, u32[]{:S(2)}) collective-permute-start(f32[2,136,128]{2,1,0:T(8,128)S(1)} %broadcast_select_fusion.23), channel_id=1, source_target_pairs={{0,8},{16,24},{32,40},{48,56},{64,72},{80,88},{96,104},{112,120},{... | collective-permute-start | bytes 417800 | tf_op jit(solution)/shard_map/ppermute | solution.py:90
  12.2 1.8 %collective-permute-done = f32[2,136,128]{2,1,0:T(8,128)S(1)} collective-permute-done((f32[2,136,128]{2,1,0:T(8,128)S(1)}, f32[2,136,128]{2,1,0:T(8,128)S(1)}, u32[]{:S(2)}, u32[]{:S(2)}) %collective-permute-start) | collective-permute-done | bytes 139296 | tf_op jit(solution)/shard_map/ppermute | solution.py:90
  14.3 4.9 %collective-permute-start.3 = (f32[2,136,128]{2,1,0:T(8,128)S(1)}, f32[2,136,128]{2,1,0:T(8,128)S(1)}, u32[]{:S(2)}, u32[]{:S(2)}) collective-permute-start(f32[2,136,128]{2,1,0:T(8,128)S(1)} %broadcast_select_fusion.20), channel_id=1, source_target_pairs={{8,24},{40,56},{72,88},{104,120},{112,96},{80,64},{48,32},{16,0},{... | collective-permute-start | bytes 417800 | tf_op jit(solution)/shard_map/ppermute | solution.py:90
  19.3 1.3 %collective-permute-start.2 = (f32[2,136,128]{2,1,0:T(8,128)S(1)}, f32[2,136,128]{2,1,0:T(8,128)S(1)}, u32[]{:S(2)}, u32[]{:S(2)}) collective-permute-start(f32[2,136,128]{2,1,0:T(8,128)S(1)} %broadcast_select_fusion.21), channel_id=1, source_target_pairs={{8,24},{40,56},{72,88},{104,120},{112,96},{80,64},{48,32},{16,0},{... | collective-permute-start | bytes 417800 | tf_op jit(solution)/shard_map/ppermute | solution.py:90
  21.4 2.4 %collective-permute-done.2 = f32[2,136,128]{2,1,0:T(8,128)S(1)} collective-permute-done((f32[2,136,128]{2,1,0:T(8,128)S(1)}, f32[2,136,128]{2,1,0:T(8,128)S(1)}, u32[]{:S(2)}, u32[]{:S(2)}) %collective-permute-start.2) | collective-permute-done | bytes 139296 | tf_op jit(solution)/shard_map/ppermute | solution.py:90
  29.8 32.2 %collective-permute-start.11 = (f32[2,136,128]{2,1,0:T(8,128)S(1)}, f32[2,136,128]{2,1,0:T(8,128)S(1)}, u32[]{:S(2)}, u32[]{:S(2)}) collective-permute-start(f32[2,136,128]{2,1,0:T(8,128)S(1)} %broadcast_select_fusion.12), channel_id=1, source_target_pairs={{8,16},{24,32},{40,48},{56,64},{72,80},{88,96},{104,112},{112,104}... | collective-permute-start | bytes 417800 | tf_op jit(solution)/shard_map/ppermute | solution.py:90
  62.1 1.9 %collective-permute-start.10 = (f32[2,136,128]{2,1,0:T(8,128)S(1)}, f32[2,136,128]{2,1,0:T(8,128)S(1)}, u32[]{:S(2)}, u32[]{:S(2)}) collective-permute-start(f32[2,136,128]{2,1,0:T(8,128)S(1)} %broadcast_select_fusion.13), channel_id=1, source_target_pairs={{8,16},{24,32},{40,48},{56,64},{72,80},{88,96},{104,112},{112,104}... | collective-permute-start | bytes 417800 | tf_op jit(solution)/shard_map/ppermute | solution.py:90
  64.5 3.3 %collective-permute-done.10 = f32[2,136,128]{2,1,0:T(8,128)S(1)} collective-permute-done((f32[2,136,128]{2,1,0:T(8,128)S(1)}, f32[2,136,128]{2,1,0:T(8,128)S(1)}, u32[]{:S(2)}, u32[]{:S(2)}) %collective-permute-start.10) | collective-permute-done | bytes 139296 | tf_op jit(solution)/shard_map/ppermute | solution.py:90
  68.2 1.3 %collective-permute-start.12 = (f32[2,136,128]{2,1,0:T(8,128)S(1)}, f32[2,136,128]{2,1,0:T(8,128)S(1)}, u32[]{:S(2)}, u32[]{:S(2)}) collective-permute-start(f32[2,136,128]{2,1,0:T(8,128)S(1)} %get-tuple-element.163), channel_id=1, source_target_pairs={{0,128},{8,136},{16,144},{24,152},{32,160},{40,168},{48,176},{56,1... | collective-permute-start | bytes 417800 | tf_op jit(solution)/shard_map/ppermute | solution.py:105
  69.5 1.3 %collective-permute-start.13 = (f32[2,136,128]{2,1,0:T(8,128)S(1)}, f32[2,136,128]{2,1,0:T(8,128)S(1)}, u32[]{:S(2)}, u32[]{:S(2)}) collective-permute-start(f32[2,136,128]{2,1,0:T(8,128)S(1)} %get-tuple-element.163), channel_id=1, source_target_pairs={{0,256},{8,264},{16,272},{24,280},{32,288},{40,296},{48,304},{56,3... | collective-permute-start | bytes 417800 | tf_op jit(solution)/shard_map/ppermute | solution.py:105
  70.8 1.3 %collective-permute-start.15 = (f32[2,136,128]{2,1,0:T(8,128)S(1)}, f32[2,136,128]{2,1,0:T(8,128)S(1)}, u32[]{:S(2)}, u32[]{:S(2)}) collective-permute-start(f32[2,136,128]{2,1,0:T(8,128)S(1)} %get-tuple-element.164), channel_id=1, source_target_pairs={{0,128},{8,136},{16,144},{24,152},{32,160},{40,168},{48,176},{56,1... | collective-permute-start | bytes 417800 | tf_op jit(solution)/shard_map/ppermute | solution.py:105
  72.1 1.3 %collective-permute-start.16 = (f32[2,136,128]{2,1,0:T(8,128)S(1)}, f32[2,136,128]{2,1,0:T(8,128)S(1)}, u32[]{:S(2)}, u32[]{:S(2)}) collective-permute-start(f32[2,136,128]{2,1,0:T(8,128)S(1)} %get-tuple-element.164), channel_id=1, source_target_pairs={{0,256},{8,264},{16,272},{24,280},{32,288},{40,296},{48,304},{56,3... | collective-permute-start | bytes 417800 | tf_op jit(solution)/shard_map/ppermute | solution.py:105
  73.4 1.3 %collective-permute-start.14 = (f32[2,136,128]{2,1,0:T(8,128)S(1)}, f32[2,136,128]{2,1,0:T(8,128)S(1)}, u32[]{:S(2)}, u32[]{:S(2)}) collective-permute-start(f32[2,136,128]{2,1,0:T(8,128)S(1)} %get-tuple-element.163), channel_id=1, source_target_pairs={{0,384},{8,392},{16,400},{24,408},{32,416},{40,424},{48,432},{56,4... | collective-permute-start | bytes 417800 | tf_op jit(solution)/shard_map/ppermute | solution.py:105
  77.2 3.1 %collective-permute-done.16 = f32[2,136,128]{2,1,0:T(8,128)S(1)} collective-permute-done((f32[2,136,128]{2,1,0:T(8,128)S(1)}, f32[2,136,128]{2,1,0:T(8,128)S(1)}, u32[]{:S(2)}, u32[]{:S(2)}) %collective-permute-start.16) | collective-permute-done | bytes 139296 | tf_op jit(solution)/shard_map/ppermute | solution.py:105
  80.3 2.5 %collective-permute-done.14 = f32[2,136,128]{2,1,0:T(8,128)S(1)} collective-permute-done((f32[2,136,128]{2,1,0:T(8,128)S(1)}, f32[2,136,128]{2,1,0:T(8,128)S(1)}, u32[]{:S(2)}, u32[]{:S(2)}) %collective-permute-start.14) | collective-permute-done | bytes 139296 | tf_op jit(solution)/shard_map/ppermute | solution.py:105
  82.9 1.5 %collective-permute-done.17 = f32[2,136,128]{2,1,0:T(8,128)S(1)} collective-permute-done((f32[2,136,128]{2,1,0:T(8,128)S(1)}, f32[2,136,128]{2,1,0:T(8,128)S(1)}, u32[]{:S(2)}, u32[]{:S(2)}) %collective-permute-start.17) | collective-permute-done | bytes 139296 | tf_op jit(solution)/shard_map/ppermute | solution.py:105
  86.2 12.4 %collective-permute-start.18 = (f32[4,128,512]{2,1,0:T(8,128)S(1)}, f32[4,128,512]{2,1,0:T(8,128)S(1)}, u32[]{:S(2)}, u32[]{:S(2)}) collective-permute-start(f32[4,128,512]{2,1,0:T(8,128)S(1)} %pad_maximum_fusion), channel_id=1, source_target_pairs={{0,1},{1,0},{2,3},{3,2},{4,5},{5,4},{6,7},{7,6},{8,9},{9,8},{10,11... | collective-permute-start | bytes 3145736 | tf_op jit(solution)/shard_map/ppermute | solution.py:125
  98.7 2.2 %collective-permute-done.18 = f32[4,128,512]{2,1,0:T(8,128)S(1)} collective-permute-done((f32[4,128,512]{2,1,0:T(8,128)S(1)}, f32[4,128,512]{2,1,0:T(8,128)S(1)}, u32[]{:S(2)}, u32[]{:S(2)}) %collective-permute-start.18) | collective-permute-done | bytes 1048608 | tf_op jit(solution)/shard_map/ppermute | solution.py:125
  101.2 3.2 %collective-permute-start.19 = (f32[128,512]{1,0:T(8,128)S(1)}, f32[128,512]{1,0:T(8,128)S(1)}, u32[]{:S(2)}, u32[]{:S(2)}) collective-permute-start(f32[128,512]{1,0:T(8,128)S(1)} %get-tuple-element.114), channel_id=1, source_target_pairs={{0,2},{1,3},{2,4},{3,5},{4,6},{5,7},{6,0},{7,1},{8,10},{9,11},{10,... | collective-permute-start | bytes 786440 | tf_op jit(solution)/shard_map/ppermute | solution.py:130
  104.4 2.6 %collective-permute-start.20 = (f32[128,512]{1,0:T(8,128)S(1)}, f32[128,512]{1,0:T(8,128)S(1)}, u32[]{:S(2)}, u32[]{:S(2)}) collective-permute-start(f32[128,512]{1,0:T(8,128)S(1)} %get-tuple-element.116), channel_id=1, source_target_pairs={{0,4},{1,5},{2,6},{3,7},{4,0},{5,1},{6,2},{7,3},{8,12},{9,13},{10,... | collective-permute-start | bytes 786440 | tf_op jit(solution)/shard_map/ppermute | solution.py:130
  107.1 4.0 %collective-permute-start.21 = (f32[128,512]{1,0:T(8,128)S(1)}, f32[128,512]{1,0:T(8,128)S(1)}, u32[]{:S(2)}, u32[]{:S(2)}) collective-permute-start(f32[128,512]{1,0:T(8,128)S(1)} %get-tuple-element.115), channel_id=1, source_target_pairs={{0,6},{1,7},{2,0},{3,1},{4,2},{5,3},{6,4},{7,5},{8,14},{9,15},{10,... | collective-permute-start | bytes 786440 | tf_op jit(solution)/shard_map/ppermute | solution.py:130
  111.3 3.8 %collective-permute-done.20 = f32[128,512]{1,0:T(8,128)S(1)} collective-permute-done((f32[128,512]{1,0:T(8,128)S(1)}, f32[128,512]{1,0:T(8,128)S(1)}, u32[]{:S(2)}, u32[]{:S(2)}) %collective-permute-start.20) | collective-permute-done | bytes 262176 | tf_op jit(solution)/shard_map/ppermute | solution.py:130
  115.1 6.6 %collective-permute-done.21 = f32[128,512]{1,0:T(8,128)S(1)} collective-permute-done((f32[128,512]{1,0:T(8,128)S(1)}, f32[128,512]{1,0:T(8,128)S(1)}, u32[]{:S(2)}, u32[]{:S(2)}) %collective-permute-start.21) | collective-permute-done | bytes 262176 | tf_op jit(solution)/shard_map/ppermute | solution.py:130
  (135 shorter events, 19.9 us)
Async XLA Ops:
  0.0 111.0 %copy-start = (bf16[16,512]{1,0:T(8,128)(2,1)S(1)}, bf16[16,512]{1,0:T(8,128)(2,1)}, u32[]{:S(2)}) copy-start(bf16[16,512]{1,0:T(8,128)(2,1)} %param.15) | copy-start | bytes 49156
  4.5 7.6 %collective-permute-start.1 = (f32[2,136,128]{2,1,0:T(8,128)S(1)}, f32[2,136,128]{2,1,0:T(8,128)S(1)}, u32[]{:S(2)}, u32[]{:S(2)}) collective-permute-start(f32[2,136,128]{2,1,0:T(8,128)S(1)} %broadcast_select_fusion.22), channel_id=1, source_target_pairs={{0,8},{16,24},{32,40},{48,56},{64,72},{80,88},{96,104},{112,120},{... | collective-permute-start | bytes 417800 | tf_op jit(solution)/shard_map/ppermute | solution.py:90
  6.5 7.6 %collective-permute-start = (f32[2,136,128]{2,1,0:T(8,128)S(1)}, f32[2,136,128]{2,1,0:T(8,128)S(1)}, u32[]{:S(2)}, u32[]{:S(2)}) collective-permute-start(f32[2,136,128]{2,1,0:T(8,128)S(1)} %broadcast_select_fusion.23), channel_id=1, source_target_pairs={{0,8},{16,24},{32,40},{48,56},{64,72},{80,88},{96,104},{112,120},{... | collective-permute-start | bytes 417800 | tf_op jit(solution)/shard_map/ppermute | solution.py:90
  14.3 6.9 %collective-permute-start.3 = (f32[2,136,128]{2,1,0:T(8,128)S(1)}, f32[2,136,128]{2,1,0:T(8,128)S(1)}, u32[]{:S(2)}, u32[]{:S(2)}) collective-permute-start(f32[2,136,128]{2,1,0:T(8,128)S(1)} %broadcast_select_fusion.20), channel_id=1, source_target_pairs={{8,24},{40,56},{72,88},{104,120},{112,96},{80,64},{48,32},{16,0},{... | collective-permute-start | bytes 417800 | tf_op jit(solution)/shard_map/ppermute | solution.py:90
  19.3 4.5 %collective-permute-start.2 = (f32[2,136,128]{2,1,0:T(8,128)S(1)}, f32[2,136,128]{2,1,0:T(8,128)S(1)}, u32[]{:S(2)}, u32[]{:S(2)}) collective-permute-start(f32[2,136,128]{2,1,0:T(8,128)S(1)} %broadcast_select_fusion.21), channel_id=1, source_target_pairs={{8,24},{40,56},{72,88},{104,120},{112,96},{80,64},{48,32},{16,0},{... | collective-permute-start | bytes 417800 | tf_op jit(solution)/shard_map/ppermute | solution.py:90
  24.1 1.4 %collective-permute-start.5 = (f32[2,136,128]{2,1,0:T(8,128)S(1)}, f32[2,136,128]{2,1,0:T(8,128)S(1)}, u32[]{:S(2)}, u32[]{:S(2)}) collective-permute-start(f32[2,136,128]{2,1,0:T(8,128)S(1)} %broadcast_select_fusion.16), channel_id=1, source_target_pairs={{24,56},{88,120},{96,64},{32,0},{152,184},{216,248},{224,192},{160... | collective-permute-start | bytes 417800 | tf_op jit(solution)/shard_map/ppermute | solution.py:90
  24.8 0.8 collective-permute-start.4
  25.9 1.4 %collective-permute-start.7 = (f32[2,136,128]{2,1,0:T(8,128)S(1)}, f32[2,136,128]{2,1,0:T(8,128)S(1)}, u32[]{:S(2)}, u32[]{:S(2)}) collective-permute-start(f32[2,136,128]{2,1,0:T(8,128)S(1)} %broadcast_select_fusion.18), channel_id=1, source_target_pairs={{0,120},{120,0},{56,88},{64,32},{128,248},{248,128},{184,216},{192... | collective-permute-start | bytes 417800 | tf_op jit(solution)/shard_map/ppermute | solution.py:90
  26.7 0.8 collective-permute-start.6
  27.7 56.8 %copy-start.2 = (bf16[128,512]{1,0:T(8,128)(2,1)S(1)}, bf16[128,512]{1,0:T(8,128)(2,1)}, u32[]{:S(2)}) copy-start(bf16[128,512]{1,0:T(8,128)(2,1)} %param.8) | copy-start | bytes 393220
  27.8 1.6 %collective-permute-start.9 = (f32[2,136,128]{2,1,0:T(8,128)S(1)}, f32[2,136,128]{2,1,0:T(8,128)S(1)}, u32[]{:S(2)}, u32[]{:S(2)}) collective-permute-start(f32[2,136,128]{2,1,0:T(8,128)S(1)} %broadcast_select_fusion.14), channel_id=1, source_target_pairs={{24,40},{56,72},{88,104},{96,80},{64,48},{32,16},{152,168},{184,20... | collective-permute-start | bytes 417800 | tf_op jit(solution)/shard_map/ppermute | solution.py:90
  28.7 0.8 collective-permute-start.8
  29.8 34.7 %collective-permute-start.11 = (f32[2,136,128]{2,1,0:T(8,128)S(1)}, f32[2,136,128]{2,1,0:T(8,128)S(1)}, u32[]{:S(2)}, u32[]{:S(2)}) collective-permute-start(f32[2,136,128]{2,1,0:T(8,128)S(1)} %broadcast_select_fusion.12), channel_id=1, source_target_pairs={{8,16},{24,32},{40,48},{56,64},{72,80},{88,96},{104,112},{112,104}... | collective-permute-start | bytes 417800 | tf_op jit(solution)/shard_map/ppermute | solution.py:90
  62.1 5.8 %collective-permute-start.10 = (f32[2,136,128]{2,1,0:T(8,128)S(1)}, f32[2,136,128]{2,1,0:T(8,128)S(1)}, u32[]{:S(2)}, u32[]{:S(2)}) collective-permute-start(f32[2,136,128]{2,1,0:T(8,128)S(1)} %broadcast_select_fusion.13), channel_id=1, source_target_pairs={{8,16},{24,32},{40,48},{56,64},{72,80},{88,96},{104,112},{112,104}... | collective-permute-start | bytes 417800 | tf_op jit(solution)/shard_map/ppermute | solution.py:90
  68.2 6.5 %collective-permute-start.12 = (f32[2,136,128]{2,1,0:T(8,128)S(1)}, f32[2,136,128]{2,1,0:T(8,128)S(1)}, u32[]{:S(2)}, u32[]{:S(2)}) collective-permute-start(f32[2,136,128]{2,1,0:T(8,128)S(1)} %get-tuple-element.163), channel_id=1, source_target_pairs={{0,128},{8,136},{16,144},{24,152},{32,160},{40,168},{48,176},{56,1... | collective-permute-start | bytes 417800 | tf_op jit(solution)/shard_map/ppermute | solution.py:105
  69.5 7.3 %collective-permute-start.13 = (f32[2,136,128]{2,1,0:T(8,128)S(1)}, f32[2,136,128]{2,1,0:T(8,128)S(1)}, u32[]{:S(2)}, u32[]{:S(2)}) collective-permute-start(f32[2,136,128]{2,1,0:T(8,128)S(1)} %get-tuple-element.163), channel_id=1, source_target_pairs={{0,256},{8,264},{16,272},{24,280},{32,288},{40,296},{48,304},{56,3... | collective-permute-start | bytes 417800 | tf_op jit(solution)/shard_map/ppermute | solution.py:105
  70.8 6.4 %collective-permute-start.15 = (f32[2,136,128]{2,1,0:T(8,128)S(1)}, f32[2,136,128]{2,1,0:T(8,128)S(1)}, u32[]{:S(2)}, u32[]{:S(2)}) collective-permute-start(f32[2,136,128]{2,1,0:T(8,128)S(1)} %get-tuple-element.164), channel_id=1, source_target_pairs={{0,128},{8,136},{16,144},{24,152},{32,160},{40,168},{48,176},{56,1... | collective-permute-start | bytes 417800 | tf_op jit(solution)/shard_map/ppermute | solution.py:105
  72.1 8.2 %collective-permute-start.16 = (f32[2,136,128]{2,1,0:T(8,128)S(1)}, f32[2,136,128]{2,1,0:T(8,128)S(1)}, u32[]{:S(2)}, u32[]{:S(2)}) collective-permute-start(f32[2,136,128]{2,1,0:T(8,128)S(1)} %get-tuple-element.164), channel_id=1, source_target_pairs={{0,256},{8,264},{16,272},{24,280},{32,288},{40,296},{48,304},{56,3... | collective-permute-start | bytes 417800 | tf_op jit(solution)/shard_map/ppermute | solution.py:105
  73.4 9.4 %collective-permute-start.14 = (f32[2,136,128]{2,1,0:T(8,128)S(1)}, f32[2,136,128]{2,1,0:T(8,128)S(1)}, u32[]{:S(2)}, u32[]{:S(2)}) collective-permute-start(f32[2,136,128]{2,1,0:T(8,128)S(1)} %get-tuple-element.163), channel_id=1, source_target_pairs={{0,384},{8,392},{16,400},{24,408},{32,416},{40,424},{48,432},{56,4... | collective-permute-start | bytes 417800 | tf_op jit(solution)/shard_map/ppermute | solution.py:105
  74.7 9.6 %collective-permute-start.17 = (f32[2,136,128]{2,1,0:T(8,128)S(1)}, f32[2,136,128]{2,1,0:T(8,128)S(1)}, u32[]{:S(2)}, u32[]{:S(2)}) collective-permute-start(f32[2,136,128]{2,1,0:T(8,128)S(1)} %get-tuple-element.164), channel_id=1, source_target_pairs={{0,384},{8,392},{16,400},{24,408},{32,416},{40,424},{48,432},{56,4... | collective-permute-start | bytes 417800 | tf_op jit(solution)/shard_map/ppermute | solution.py:105
  86.2 14.7 %collective-permute-start.18 = (f32[4,128,512]{2,1,0:T(8,128)S(1)}, f32[4,128,512]{2,1,0:T(8,128)S(1)}, u32[]{:S(2)}, u32[]{:S(2)}) collective-permute-start(f32[4,128,512]{2,1,0:T(8,128)S(1)} %pad_maximum_fusion), channel_id=1, source_target_pairs={{0,1},{1,0},{2,3},{3,2},{4,5},{5,4},{6,7},{7,6},{8,9},{9,8},{10,11... | collective-permute-start | bytes 3145736 | tf_op jit(solution)/shard_map/ppermute | solution.py:125
  101.2 10.1 %collective-permute-start.19 = (f32[128,512]{1,0:T(8,128)S(1)}, f32[128,512]{1,0:T(8,128)S(1)}, u32[]{:S(2)}, u32[]{:S(2)}) collective-permute-start(f32[128,512]{1,0:T(8,128)S(1)} %get-tuple-element.114), channel_id=1, source_target_pairs={{0,2},{1,3},{2,4},{3,5},{4,6},{5,7},{6,0},{7,1},{8,10},{9,11},{10,... | collective-permute-start | bytes 786440 | tf_op jit(solution)/shard_map/ppermute | solution.py:130
  104.4 10.6 %collective-permute-start.20 = (f32[128,512]{1,0:T(8,128)S(1)}, f32[128,512]{1,0:T(8,128)S(1)}, u32[]{:S(2)}, u32[]{:S(2)}) collective-permute-start(f32[128,512]{1,0:T(8,128)S(1)} %get-tuple-element.116), channel_id=1, source_target_pairs={{0,4},{1,5},{2,6},{3,7},{4,0},{5,1},{6,2},{7,3},{8,12},{9,13},{10,... | collective-permute-start | bytes 786440 | tf_op jit(solution)/shard_map/ppermute | solution.py:130
  107.1 14.6 %collective-permute-start.21 = (f32[128,512]{1,0:T(8,128)S(1)}, f32[128,512]{1,0:T(8,128)S(1)}, u32[]{:S(2)}, u32[]{:S(2)}) collective-permute-start(f32[128,512]{1,0:T(8,128)S(1)} %get-tuple-element.115), channel_id=1, source_target_pairs={{0,6},{1,7},{2,0},{3,1},{4,2},{5,3},{6,4},{7,5},{8,14},{9,15},{10,... | collective-permute-start | bytes 786440 | tf_op jit(solution)/shard_map/ppermute | solution.py:130
  (4 other events, 147.7 us)

commit v7 on v5

--- a/solution.py
+++ b/solution.py
@@ -112,6 +112,21 @@
         def block(index):
             return lax.dynamic_slice_in_dim(partial, index * width, width, 1)
 
+        if chips == 4:
+            def at(shift, parity):
+                return block(2 * ((chip + shift) % chips) + parity)
+
+            keep = jnp.stack([at(d, core) for d in (0, 1, 3)])
+            away = jnp.stack([at(d, 1 - core) for d in (0, 1, 3)])
+            mine = keep + lax.ppermute(away, axis, [(h, h ^ 1) for h in range(n)])
+            ring = [(y, c) for y in range(chips) for c in range(2)]
+            lower = [(2 * y + c, 2 * ((y - 1) % chips) + c) for y, c in ring]
+            upper = [(2 * y + c, 2 * ((y + 1) % chips) + c) for y, c in ring]
+            across = [(2 * y + c, 2 * ((y + 1) % chips) + 1 - c) for y, c in ring]
+            up = mine[1] + lax.ppermute(at(2, 1 - core), axis, across)
+            down = mine[2] + lax.ppermute(at(2, core), axis, lower)
+            return mine[0] + lax.ppermute(up, axis, upper) + lax.ppermute(down, axis, lower)
+
         keep = jnp.stack([block(2 * y + core) for y in range(chips)])
         away = jnp.stack([block(2 * y + 1 - core) for y in range(chips)])
         pairs = [(h, h ^ 1) for h in range(n)]

time: 121 us -> 123 us (1.017)
  the two profiles are of different devices: /device:TPU:79 before, /device:TPU:94 now
where the time goes in v7:
time: 123 us
  waiting for transfers between devices  82.2 us (67%)
  starting transfers between devices  27.6 us (22%)
  other arithmetic  4.75 us (4%)
  matrix products  4.69 us (4%)
  local copies, waits for them, and re-layouts  2.87 us (2%)
    ppermute x6, waiting for transfers between devices, exclusive_scan(): got = lax.ppermute(send, axis, full)  58.4 us
    ppermute x6, starting transfers between devices, exclusive_scan(): got = lax.ppermute(send, axis, full)  9.97 us
    ppermute x3, waiting for transfers between devices, exclusive_scan(): got = lax.ppermute(total, axis, pairs)  9.72 us
    ppermute x1, waiting for transfers between devices, scatter_heads(): down = mine[2] + lax.ppermute(at(2, core), axis, lower)  3.92 us
    ppermute x3, starting transfers between devices, exclusive_scan(): got = lax.ppermute(total, axis, pairs)  3.88 us
    ppermute x1, starting transfers between devices, scatter_heads(): lax.ppermute(down, axis, lower)  3.74 us
    ppermute x1, starting transfers between devices, scatter_heads(): down = mine[2] + lax.ppermute(at(2, core), axis, lower)  3.71 us
    ppermute x1, waiting for transfers between devices, scatter_heads(): up = mine[1] + lax.ppermute(at(2, 1 - core), axis, across)  3.67 us
  transfers between devices with their start and end apart: 14, of which 11 were waited for; matrix products, arithmetic and copies ran while one was open for 1% of the time, Pallas kernels for 0%

profile of v7, /device:TPU:94, one launch (start us, length us, event | category | flops | bytes accessed | tf_op | source)
XLA Modules:
  0.0 122.8 jit_solution(5708270434787932289)
XLA Ops:
  2.1 1.0 copy.30
  4.4 3.8 %collective-permute-start = (f32[4,136,128]{2,1,0:T(8,128)S(1)}, f32[4,136,128]{2,1,0:T(8,128)S(1)}, u32[]{:S(2)}, u32[]{:S(2)}) collective-permute-start(f32[4,136,128]{2,1,0:T(8,128)S(1)} %pad_maximum_fusion.1), channel_id=1, source_target_pairs={{0,8},{16,24},{32,40},{48,56},{64,72},{80,88},{96,104},{112,120},{... | collective-permute-start | bytes 835592 | tf_op jit(solution)/shard_map/ppermute | solution.py:86
  8.3 6.6 %collective-permute-done = f32[4,136,128]{2,1,0:T(8,128)S(1)} collective-permute-done((f32[4,136,128]{2,1,0:T(8,128)S(1)}, f32[4,136,128]{2,1,0:T(8,128)S(1)}, u32[]{:S(2)}, u32[]{:S(2)}) %collective-permute-start) | collective-permute-done | bytes 278560 | tf_op jit(solution)/shard_map/ppermute | solution.py:86
  15.1 1.6 %collective-permute-start.1 = (f32[4,136,128]{2,1,0:T(8,128)S(1)}, f32[4,136,128]{2,1,0:T(8,128)S(1)}, u32[]{:S(2)}, u32[]{:S(2)}) collective-permute-start(f32[4,136,128]{2,1,0:T(8,128)S(1)} %get-tuple-element.36), channel_id=1, source_target_pairs={{8,24},{40,56},{72,88},{104,120},{112,96},{80,64},{48,32},{16,0},{... | collective-permute-start | bytes 835592 | tf_op jit(solution)/shard_map/ppermute | solution.py:86
  16.7 5.2 %collective-permute-done.1 = f32[4,136,128]{2,1,0:T(8,128)S(1)} collective-permute-done((f32[4,136,128]{2,1,0:T(8,128)S(1)}, f32[4,136,128]{2,1,0:T(8,128)S(1)}, u32[]{:S(2)}, u32[]{:S(2)}) %collective-permute-start.1) | collective-permute-done | bytes 278560 | tf_op jit(solution)/shard_map/ppermute | solution.py:86
  24.1 1.3 %collective-permute-start.4 = (f32[4,136,128]{2,1,0:T(8,128)S(1)}, f32[4,136,128]{2,1,0:T(8,128)S(1)}, u32[]{:S(2)}, u32[]{:S(2)}) collective-permute-start(f32[4,136,128]{2,1,0:T(8,128)S(1)} %get-tuple-element.19), channel_id=1, source_target_pairs={{24,40},{56,72},{88,104},{96,80},{64,48},{32,16},{152,168},{184,20... | collective-permute-start | bytes 835592 | tf_op jit(solution)/shard_map/ppermute | solution.py:86
  25.5 40.5 %collective-permute-done.4 = f32[4,136,128]{2,1,0:T(8,128)S(1)} collective-permute-done((f32[4,136,128]{2,1,0:T(8,128)S(1)}, f32[4,136,128]{2,1,0:T(8,128)S(1)}, u32[]{:S(2)}, u32[]{:S(2)}) %collective-permute-start.4) | collective-permute-done | bytes 278560 | tf_op jit(solution)/shard_map/ppermute | solution.py:86
  66.3 1.9 %collective-permute-start.5 = (f32[4,136,128]{2,1,0:T(8,128)S(1)}, f32[4,136,128]{2,1,0:T(8,128)S(1)}, u32[]{:S(2)}, u32[]{:S(2)}) collective-permute-start(f32[4,136,128]{2,1,0:T(8,128)S(1)} %add_select_fusion), channel_id=1, source_target_pairs={{8,16},{24,32},{40,48},{56,64},{72,80},{88,96},{104,112},{112,104}... | collective-permute-start | bytes 835592 | tf_op jit(solution)/shard_map/ppermute | solution.py:86
  68.6 6.1 %collective-permute-done.5 = f32[4,136,128]{2,1,0:T(8,128)S(1)} collective-permute-done((f32[4,136,128]{2,1,0:T(8,128)S(1)}, f32[4,136,128]{2,1,0:T(8,128)S(1)}, u32[]{:S(2)}, u32[]{:S(2)}) %collective-permute-start.5) | collective-permute-done | bytes 278560 | tf_op jit(solution)/shard_map/ppermute | solution.py:86
  75.1 1.3 %collective-permute-start.7 = (f32[4,136,128]{2,1,0:T(8,128)S(1)}, f32[4,136,128]{2,1,0:T(8,128)S(1)}, u32[]{:S(2)}, u32[]{:S(2)}) collective-permute-start(f32[4,136,128]{2,1,0:T(8,128)S(1)} %get-tuple-element.17), channel_id=1, source_target_pairs={{0,256},{8,264},{16,272},{24,280},{32,288},{40,296},{48,304},{56,3... | collective-permute-start | bytes 835592 | tf_op jit(solution)/shard_map/ppermute | solution.py:98
  77.3 1.3 %collective-permute-start.6 = (f32[4,136,128]{2,1,0:T(8,128)S(1)}, f32[4,136,128]{2,1,0:T(8,128)S(1)}, u32[]{:S(2)}, u32[]{:S(2)}) collective-permute-start(f32[4,136,128]{2,1,0:T(8,128)S(1)} %get-tuple-element.17), channel_id=1, source_target_pairs={{0,128},{8,136},{16,144},{24,152},{32,160},{40,168},{48,176},{56,1... | collective-permute-start | bytes 835592 | tf_op jit(solution)/shard_map/ppermute | solution.py:98
  78.6 1.3 %collective-permute-start.8 = (f32[4,136,128]{2,1,0:T(8,128)S(1)}, f32[4,136,128]{2,1,0:T(8,128)S(1)}, u32[]{:S(2)}, u32[]{:S(2)}) collective-permute-start(f32[4,136,128]{2,1,0:T(8,128)S(1)} %get-tuple-element.17), channel_id=1, source_target_pairs={{0,384},{8,392},{16,400},{24,408},{32,416},{40,424},{48,432},{56,4... | collective-permute-start | bytes 835592 | tf_op jit(solution)/shard_map/ppermute | solution.py:98
  79.9 5.1 %collective-permute-done.7 = f32[4,136,128]{2,1,0:T(8,128)S(1)} collective-permute-done((f32[4,136,128]{2,1,0:T(8,128)S(1)}, f32[4,136,128]{2,1,0:T(8,128)S(1)}, u32[]{:S(2)}, u32[]{:S(2)}) %collective-permute-start.7) | collective-permute-done | bytes 278560 | tf_op jit(solution)/shard_map/ppermute | solution.py:98
  85.8 3.9 %collective-permute-done.8 = f32[4,136,128]{2,1,0:T(8,128)S(1)} collective-permute-done((f32[4,136,128]{2,1,0:T(8,128)S(1)}, f32[4,136,128]{2,1,0:T(8,128)S(1)}, u32[]{:S(2)}, u32[]{:S(2)}) %collective-permute-start.8) | collective-permute-done | bytes 278560 | tf_op jit(solution)/shard_map/ppermute | solution.py:98
  90.4 2.9 %fusion.54 = f32[128,4096]{1,0:T(8,128)S(1)} fusion(bf16[128,512]{0,1:T(8,128)(2,1)S(1)} %fusion.18, bf16[512,4096]{1,0:T(8,128)(2,1)} %param.13), kind=kOutput, calls=%fused_computation.130 | convolution fusion | flops 536870912 | bytes 6422528 | tf_op jit(solution)/shard_map/dot_general | solution.py:171
  93.7 1.9 %collective-permute-start.9 = (f32[3,128,512]{2,1,0:T(8,128)S(1)}, f32[3,128,512]{2,1,0:T(8,128)S(1)}, u32[]{:S(2)}, u32[]{:S(2)}) collective-permute-start(f32[3,128,512]{2,1,0:T(8,128)S(1)} %pad_maximum_fusion), channel_id=1, source_target_pairs={{0,1},{1,0},{2,3},{3,2},{4,5},{5,4},{6,7},{7,6},{8,9},{9,8},{10,11... | collective-permute-start | bytes 2359304 | tf_op jit(solution)/shard_map/ppermute | solution.py:121
  95.6 2.2 %collective-permute-start.10 = (f32[128,512]{1,0:T(8,128)S(1)}, f32[128,512]{1,0:T(8,128)S(1)}, u32[]{:S(2)}, u32[]{:S(2)}) collective-permute-start(f32[128,512]{1,0:T(8,128)S(1)} %get-tuple-element.39), channel_id=1, source_target_pairs={{0,3},{1,2},{2,5},{3,4},{4,7},{5,6},{6,1},{7,0},{8,11},{9,10},{10,... | collective-permute-start | bytes 786440 | tf_op jit(solution)/shard_map/ppermute | solution.py:126
  97.9 3.7 %collective-permute-start.12 = (f32[128,512]{1,0:T(8,128)S(1)}, f32[128,512]{1,0:T(8,128)S(1)}, u32[]{:S(2)}, u32[]{:S(2)}) collective-permute-start(f32[128,512]{1,0:T(8,128)S(1)} %get-tuple-element.40), channel_id=1, source_target_pairs={{0,6},{1,7},{2,0},{3,1},{4,2},{5,3},{6,4},{7,5},{8,14},{9,15},{10,... | collective-permute-start | bytes 786440 | tf_op jit(solution)/shard_map/ppermute | solution.py:127
  101.8 3.7 %collective-permute-done.10 = f32[128,512]{1,0:T(8,128)S(1)} collective-permute-done((f32[128,512]{1,0:T(8,128)S(1)}, f32[128,512]{1,0:T(8,128)S(1)}, u32[]{:S(2)}, u32[]{:S(2)}) %collective-permute-start.10) | collective-permute-done | bytes 262176 | tf_op jit(solution)/shard_map/ppermute | solution.py:126
  105.4 3.9 %collective-permute-done.12 = f32[128,512]{1,0:T(8,128)S(1)} collective-permute-done((f32[128,512]{1,0:T(8,128)S(1)}, f32[128,512]{1,0:T(8,128)S(1)}, u32[]{:S(2)}, u32[]{:S(2)}) %collective-permute-start.12) | collective-permute-done | bytes 262176 | tf_op jit(solution)/shard_map/ppermute | solution.py:127
  109.4 2.1 %collective-permute-start.11 = (f32[128,512]{1,0:T(8,128)S(1)}, f32[128,512]{1,0:T(8,128)S(1)}, u32[]{:S(2)}, u32[]{:S(2)}) collective-permute-start(f32[128,512]{1,0:T(8,128)S(1)} %get-tuple-element.47), channel_id=1, source_target_pairs={{0,2},{1,3},{2,4},{3,5},{4,6},{5,7},{6,0},{7,1},{8,10},{9,11},{10,... | collective-permute-start | bytes 786440 | tf_op jit(solution)/shard_map/ppermute | solution.py:128
  111.6 3.7 %collective-permute-start.13 = (f32[128,512]{1,0:T(8,128)S(1)}, f32[128,512]{1,0:T(8,128)S(1)}, u32[]{:S(2)}, u32[]{:S(2)}) collective-permute-start(f32[128,512]{1,0:T(8,128)S(1)} %get-tuple-element.48), channel_id=1, source_target_pairs={{0,6},{1,7},{2,0},{3,1},{4,2},{5,3},{6,4},{7,5},{8,14},{9,15},{10,... | collective-permute-start | bytes 786440 | tf_op jit(solution)/shard_map/ppermute | solution.py:128
  115.6 3.3 %collective-permute-done.11 = f32[128,512]{1,0:T(8,128)S(1)} collective-permute-done((f32[128,512]{1,0:T(8,128)S(1)}, f32[128,512]{1,0:T(8,128)S(1)}, u32[]{:S(2)}, u32[]{:S(2)}) %collective-permute-start.11) | collective-permute-done | bytes 262176 | tf_op jit(solution)/shard_map/ppermute | solution.py:128
  118.9 3.1 %collective-permute-done.13 = f32[128,512]{1,0:T(8,128)S(1)} collective-permute-done((f32[128,512]{1,0:T(8,128)S(1)}, f32[128,512]{1,0:T(8,128)S(1)}, u32[]{:S(2)}, u32[]{:S(2)}) %collective-permute-start.13) | collective-permute-done | bytes 262176 | tf_op jit(solution)/shard_map/ppermute | solution.py:128
  (77 shorter events, 10.4 us)
Async XLA Ops:
  0.0 115.3 %copy-start = (bf16[16,512]{1,0:T(8,128)(2,1)S(1)}, bf16[16,512]{1,0:T(8,128)(2,1)}, u32[]{:S(2)}) copy-start(bf16[16,512]{1,0:T(8,128)(2,1)} %param.15) | copy-start | bytes 49156
  4.4 10.5 %collective-permute-start = (f32[4,136,128]{2,1,0:T(8,128)S(1)}, f32[4,136,128]{2,1,0:T(8,128)S(1)}, u32[]{:S(2)}, u32[]{:S(2)}) collective-permute-start(f32[4,136,128]{2,1,0:T(8,128)S(1)} %pad_maximum_fusion.1), channel_id=1, source_target_pairs={{0,8},{16,24},{32,40},{48,56},{64,72},{80,88},{96,104},{112,120},{... | collective-permute-start | bytes 835592 | tf_op jit(solution)/shard_map/ppermute | solution.py:86
  15.1 6.8 %collective-permute-start.1 = (f32[4,136,128]{2,1,0:T(8,128)S(1)}, f32[4,136,128]{2,1,0:T(8,128)S(1)}, u32[]{:S(2)}, u32[]{:S(2)}) collective-permute-start(f32[4,136,128]{2,1,0:T(8,128)S(1)} %get-tuple-element.36), channel_id=1, source_target_pairs={{8,24},{40,56},{72,88},{104,120},{112,96},{80,64},{48,32},{16,0},{... | collective-permute-start | bytes 835592 | tf_op jit(solution)/shard_map/ppermute | solution.py:86
  21.9 3.5 %copy-start.1 = (bf16[128,512]{1,0:T(8,128)(2,1)S(1)}, bf16[128,512]{1,0:T(8,128)(2,1)}, u32[]{:S(2)}) copy-start(bf16[128,512]{1,0:T(8,128)(2,1)} %param.8) | copy-start | bytes 393220
  22.2 0.7 collective-permute-start.2
  23.1 0.7 collective-permute-start.3
  24.1 52.7 %copy-start.2 = (f32[128,4]{0,1:T(4,128)S(1)}, f32[128,4]{0,1:T(4,128)}, u32[]{:S(2)}) copy-start(f32[128,4]{0,1:T(4,128)} %param.11) | copy-start | bytes 6148
  24.1 41.9 %collective-permute-start.4 = (f32[4,136,128]{2,1,0:T(8,128)S(1)}, f32[4,136,128]{2,1,0:T(8,128)S(1)}, u32[]{:S(2)}, u32[]{:S(2)}) collective-permute-start(f32[4,136,128]{2,1,0:T(8,128)S(1)} %get-tuple-element.19), channel_id=1, source_target_pairs={{24,40},{56,72},{88,104},{96,80},{64,48},{32,16},{152,168},{184,20... | collective-permute-start | bytes 835592 | tf_op jit(solution)/shard_map/ppermute | solution.py:86
  66.3 24.0 %copy-start.3 = (f32[512]{0:T(512)S(1)}, f32[512]{0:T(512)}, u32[]{:S(2)}) copy-start(f32[512]{0:T(512)} %param.12) | copy-start | bytes 6148
  66.3 8.4 %collective-permute-start.5 = (f32[4,136,128]{2,1,0:T(8,128)S(1)}, f32[4,136,128]{2,1,0:T(8,128)S(1)}, u32[]{:S(2)}, u32[]{:S(2)}) collective-permute-start(f32[4,136,128]{2,1,0:T(8,128)S(1)} %add_select_fusion), channel_id=1, source_target_pairs={{8,16},{24,32},{40,48},{56,64},{72,80},{88,96},{104,112},{112,104}... | collective-permute-start | bytes 835592 | tf_op jit(solution)/shard_map/ppermute | solution.py:86
  75.1 9.9 %collective-permute-start.7 = (f32[4,136,128]{2,1,0:T(8,128)S(1)}, f32[4,136,128]{2,1,0:T(8,128)S(1)}, u32[]{:S(2)}, u32[]{:S(2)}) collective-permute-start(f32[4,136,128]{2,1,0:T(8,128)S(1)} %get-tuple-element.17), channel_id=1, source_target_pairs={{0,256},{8,264},{16,272},{24,280},{32,288},{40,296},{48,304},{56,3... | collective-permute-start | bytes 835592 | tf_op jit(solution)/shard_map/ppermute | solution.py:98
  77.3 8.4 %collective-permute-start.6 = (f32[4,136,128]{2,1,0:T(8,128)S(1)}, f32[4,136,128]{2,1,0:T(8,128)S(1)}, u32[]{:S(2)}, u32[]{:S(2)}) collective-permute-start(f32[4,136,128]{2,1,0:T(8,128)S(1)} %get-tuple-element.17), channel_id=1, source_target_pairs={{0,128},{8,136},{16,144},{24,152},{32,160},{40,168},{48,176},{56,1... | collective-permute-start | bytes 835592 | tf_op jit(solution)/shard_map/ppermute | solution.py:98
  78.6 11.2 %collective-permute-start.8 = (f32[4,136,128]{2,1,0:T(8,128)S(1)}, f32[4,136,128]{2,1,0:T(8,128)S(1)}, u32[]{:S(2)}, u32[]{:S(2)}) collective-permute-start(f32[4,136,128]{2,1,0:T(8,128)S(1)} %get-tuple-element.17), channel_id=1, source_target_pairs={{0,384},{8,392},{16,400},{24,408},{32,416},{40,424},{48,432},{56,4... | collective-permute-start | bytes 835592 | tf_op jit(solution)/shard_map/ppermute | solution.py:98
  93.4 22.0 %copy-start.4 = (s32[128]{0:T(128)S(1)}, s32[128]{0:T(128)}, u32[]{:S(2)}) copy-start(s32[128]{0:T(128)} %param.14) | copy-start | bytes 1540
  93.7 7.9 %collective-permute-start.9 = (f32[3,128,512]{2,1,0:T(8,128)S(1)}, f32[3,128,512]{2,1,0:T(8,128)S(1)}, u32[]{:S(2)}, u32[]{:S(2)}) collective-permute-start(f32[3,128,512]{2,1,0:T(8,128)S(1)} %pad_maximum_fusion), channel_id=1, source_target_pairs={{0,1},{1,0},{2,3},{3,2},{4,5},{5,4},{6,7},{7,6},{8,9},{9,8},{10,11... | collective-permute-start | bytes 2359304 | tf_op jit(solution)/shard_map/ppermute | solution.py:121
  95.6 9.8 %collective-permute-start.10 = (f32[128,512]{1,0:T(8,128)S(1)}, f32[128,512]{1,0:T(8,128)S(1)}, u32[]{:S(2)}, u32[]{:S(2)}) collective-permute-start(f32[128,512]{1,0:T(8,128)S(1)} %get-tuple-element.39), channel_id=1, source_target_pairs={{0,3},{1,2},{2,5},{3,4},{4,7},{5,6},{6,1},{7,0},{8,11},{9,10},{10,... | collective-permute-start | bytes 786440 | tf_op jit(solution)/shard_map/ppermute | solution.py:126
  97.9 11.5 %collective-permute-start.12 = (f32[128,512]{1,0:T(8,128)S(1)}, f32[128,512]{1,0:T(8,128)S(1)}, u32[]{:S(2)}, u32[]{:S(2)}) collective-permute-start(f32[128,512]{1,0:T(8,128)S(1)} %get-tuple-element.40), channel_id=1, source_target_pairs={{0,6},{1,7},{2,0},{3,1},{4,2},{5,3},{6,4},{7,5},{8,14},{9,15},{10,... | collective-permute-start | bytes 786440 | tf_op jit(solution)/shard_map/ppermute | solution.py:127
  109.4 9.4 %collective-permute-start.11 = (f32[128,512]{1,0:T(8,128)S(1)}, f32[128,512]{1,0:T(8,128)S(1)}, u32[]{:S(2)}, u32[]{:S(2)}) collective-permute-start(f32[128,512]{1,0:T(8,128)S(1)} %get-tuple-element.47), channel_id=1, source_target_pairs={{0,2},{1,3},{2,4},{3,5},{4,6},{5,7},{6,0},{7,1},{8,10},{9,11},{10,... | collective-permute-start | bytes 786440 | tf_op jit(solution)/shard_map/ppermute | solution.py:128
  111.6 10.5 %collective-permute-start.13 = (f32[128,512]{1,0:T(8,128)S(1)}, f32[128,512]{1,0:T(8,128)S(1)}, u32[]{:S(2)}, u32[]{:S(2)}) collective-permute-start(f32[128,512]{1,0:T(8,128)S(1)} %get-tuple-element.48), channel_id=1, source_target_pairs={{0,6},{1,7},{2,0},{3,1},{4,2},{5,3},{6,4},{7,5},{8,14},{9,15},{10,... | collective-permute-start | bytes 786440 | tf_op jit(solution)/shard_map/ppermute | solution.py:128

commit v8 on v5

--- a/solution.py
+++ b/solution.py
@@ -100,29 +100,25 @@
     return join(earlier, before)
 
 
-def scatter_heads(partial, axis, n):
-    rows, total_cols = partial.shape
-    width = total_cols // n
+def scatter_heads(block, n, width, axis):
     place = lax.axis_index(axis)
     if n % 2 == 0 and n > 2:
         chips = n // 2
         core = place % 2
         chip = place // 2
-
-        def block(index):
-            return lax.dynamic_slice_in_dim(partial, index * width, width, 1)
-
+        away = jnp.stack([block(2 * y + 1 - core) for y in range(chips)])
+        moved = lax.ppermute(away, axis, [(h, h ^ 1) for h in range(n)])
         keep = jnp.stack([block(2 * y + core) for y in range(chips)])
-        away = jnp.stack([block(2 * y + 1 - core) for y in range(chips)])
-        pairs = [(h, h ^ 1) for h in range(n)]
-        mine = keep + lax.ppermute(away, axis, pairs)
+        mine = keep + moved
         out = lax.dynamic_index_in_dim(mine, chip, 0, False)
-        for shift in range(1, chips):
+        shifts = sorted(range(1, chips), key=lambda s: -min(s, chips - s))
+        for shift in shifts:
             send = lax.dynamic_index_in_dim(mine, (chip + shift) % chips, 0, False)
             pairs = [(2 * y + c, 2 * ((y + shift) % chips) + c) for y in range(chips) for c in range(2)]
             out = out + lax.ppermute(send, axis, pairs)
         return out
-    whole = lax.psum(partial, axis)
+    whole = jnp.concatenate([block(i) for i in range(n)], axis=1)
+    whole = lax.psum(whole, axis)
     return lax.dynamic_slice_in_dim(whole, place * width, width, 1)
 
 
@@ -153,12 +149,17 @@
     mean_sq = jnp.mean(attended * attended, axis=-1, keepdims=True)
     normed = (attended * lax.rsqrt(mean_sq + 1e-06)).reshape(tok_rows, features) * norm_gain
     normed = normed.astype(jnp.bfloat16)
-    partial_term = lax.optimization_barrier(jnp.dot(normed, out_weight, preferred_element_type=jnp.float32))
+    width = out_weight.shape[1] // head_n
+
+    def block(index):
+        cols = lax.dynamic_slice_in_dim(out_weight, index * width, width, 1)
+        return jnp.dot(normed, cols, preferred_element_type=jnp.float32)
+
     onehot = (
         steer_ids[:, None] == jnp.arange(steer_table.shape[0], dtype=jnp.int32)[None, :]
     ).astype(jnp.bfloat16)
     steering = jnp.dot(onehot, steer_table, preferred_element_type=jnp.float32)
-    summed = scatter_heads(partial_term, "head", head_n)
+    summed = scatter_heads(block, head_n, width, "head")
     return (summed + steering).astype(jnp.bfloat16)
 
 

time: 121 us -> 123 us (1.017)
  the two profiles are of different devices: /device:TPU:79 before, /device:TPU:94 now
where the time goes in v8:
time: 123 us; the launch traced here: 122 us
  waiting for transfers between devices  77.2 us (63%)
  starting transfers between devices  24.9 us (20%)
  matrix products  12.1 us (10%)
  other arithmetic  4.75 us (4%)
  local copies, waits for them, and re-layouts  2.69 us (2%)
    ppermute x6, waiting for transfers between devices, exclusive_scan(): got = lax.ppermute(send, axis, full)  58.4 us
    dot_general x8, matrix products, block(): return jnp.dot(normed, cols, preferred_element_type=jnp.float32)  10.4 us
    ppermute x6, starting transfers between devices, exclusive_scan(): got = lax.ppermute(send, axis, full)  9.97 us
    ppermute x3, waiting for transfers between devices, exclusive_scan(): got = lax.ppermute(total, axis, pairs)  9.72 us
    ppermute x3, starting transfers between devices, scatter_heads(): out = out + lax.ppermute(send, axis, pairs)  9.15 us
    ppermute x3, waiting for transfers between devices, scatter_heads(): out = out + lax.ppermute(send, axis, pairs)  9.07 us
    ppermute x3, starting transfers between devices, exclusive_scan(): got = lax.ppermute(total, axis, pairs)  3.89 us
  transfers between devices with their start and end apart: 13, of which 10 were waited for; matrix products, arithmetic and copies ran while one was open for 6% of the time, Pallas kernels for 0%

profile of v8, /device:TPU:94, one launch (start us, length us, event | category | flops | bytes accessed | tf_op | source)
XLA Modules:
  0.0 122.4 jit_solution(17396339290346319887)
XLA Ops:
  4.4 3.8 %collective-permute-start = (f32[4,136,128]{2,1,0:T(8,128)S(1)}, f32[4,136,128]{2,1,0:T(8,128)S(1)}, u32[]{:S(2)}, u32[]{:S(2)}) collective-permute-start(f32[4,136,128]{2,1,0:T(8,128)S(1)} %pad_maximum_fusion.1), channel_id=1, source_target_pairs={{0,8},{16,24},{32,40},{48,56},{64,72},{80,88},{96,104},{112,120},{... | collective-permute-start | bytes 835592 | tf_op jit(solution)/shard_map/ppermute | solution.py:86
  8.3 6.6 %collective-permute-done = f32[4,136,128]{2,1,0:T(8,128)S(1)} collective-permute-done((f32[4,136,128]{2,1,0:T(8,128)S(1)}, f32[4,136,128]{2,1,0:T(8,128)S(1)}, u32[]{:S(2)}, u32[]{:S(2)}) %collective-permute-start) | collective-permute-done | bytes 278560 | tf_op jit(solution)/shard_map/ppermute | solution.py:86
  15.1 1.6 %collective-permute-start.1 = (f32[4,136,128]{2,1,0:T(8,128)S(1)}, f32[4,136,128]{2,1,0:T(8,128)S(1)}, u32[]{:S(2)}, u32[]{:S(2)}) collective-permute-start(f32[4,136,128]{2,1,0:T(8,128)S(1)} %get-tuple-element.36), channel_id=1, source_target_pairs={{8,24},{40,56},{72,88},{104,120},{112,96},{80,64},{48,32},{16,0},{... | collective-permute-start | bytes 835592 | tf_op jit(solution)/shard_map/ppermute | solution.py:86
  16.7 5.2 %collective-permute-done.1 = f32[4,136,128]{2,1,0:T(8,128)S(1)} collective-permute-done((f32[4,136,128]{2,1,0:T(8,128)S(1)}, f32[4,136,128]{2,1,0:T(8,128)S(1)}, u32[]{:S(2)}, u32[]{:S(2)}) %collective-permute-start.1) | collective-permute-done | bytes 278560 | tf_op jit(solution)/shard_map/ppermute | solution.py:86
  25.5 40.5 %collective-permute-done.4 = f32[4,136,128]{2,1,0:T(8,128)S(1)} collective-permute-done((f32[4,136,128]{2,1,0:T(8,128)S(1)}, f32[4,136,128]{2,1,0:T(8,128)S(1)}, u32[]{:S(2)}, u32[]{:S(2)}) %collective-permute-start.4) | collective-permute-done | bytes 278560 | tf_op jit(solution)/shard_map/ppermute | solution.py:86
  66.3 1.9 %collective-permute-start.5 = (f32[4,136,128]{2,1,0:T(8,128)S(1)}, f32[4,136,128]{2,1,0:T(8,128)S(1)}, u32[]{:S(2)}, u32[]{:S(2)}) collective-permute-start(f32[4,136,128]{2,1,0:T(8,128)S(1)} %add_select_fusion), channel_id=1, source_target_pairs={{8,16},{24,32},{40,48},{56,64},{72,80},{88,96},{104,112},{112,104}... | collective-permute-start | bytes 835592 | tf_op jit(solution)/shard_map/ppermute | solution.py:86
  68.6 6.1 %collective-permute-done.5 = f32[4,136,128]{2,1,0:T(8,128)S(1)} collective-permute-done((f32[4,136,128]{2,1,0:T(8,128)S(1)}, f32[4,136,128]{2,1,0:T(8,128)S(1)}, u32[]{:S(2)}, u32[]{:S(2)}) %collective-permute-start.5) | collective-permute-done | bytes 278560 | tf_op jit(solution)/shard_map/ppermute | solution.py:86
  77.2 1.3 %collective-permute-start.6 = (f32[4,136,128]{2,1,0:T(8,128)S(1)}, f32[4,136,128]{2,1,0:T(8,128)S(1)}, u32[]{:S(2)}, u32[]{:S(2)}) collective-permute-start(f32[4,136,128]{2,1,0:T(8,128)S(1)} %get-tuple-element.17), channel_id=1, source_target_pairs={{0,128},{8,136},{16,144},{24,152},{32,160},{40,168},{48,176},{56,1... | collective-permute-start | bytes 835592 | tf_op jit(solution)/shard_map/ppermute | solution.py:98
  79.8 5.2 %collective-permute-done.7 = f32[4,136,128]{2,1,0:T(8,128)S(1)} collective-permute-done((f32[4,136,128]{2,1,0:T(8,128)S(1)}, f32[4,136,128]{2,1,0:T(8,128)S(1)}, u32[]{:S(2)}, u32[]{:S(2)}) %collective-permute-start.7) | collective-permute-done | bytes 278560 | tf_op jit(solution)/shard_map/ppermute | solution.py:98
  85.7 3.9 %collective-permute-done.8 = f32[4,136,128]{2,1,0:T(8,128)S(1)} collective-permute-done((f32[4,136,128]{2,1,0:T(8,128)S(1)}, f32[4,136,128]{2,1,0:T(8,128)S(1)}, u32[]{:S(2)}, u32[]{:S(2)}) %collective-permute-start.8) | collective-permute-done | bytes 278560 | tf_op jit(solution)/shard_map/ppermute | solution.py:98
  90.3 1.3 %convolution_bitcast_fusion.1 = f32[1,128,512]{2,1,0:T(8,128)S(1)} fusion(bf16[128,512]{0,1:T(8,128)(2,1)S(1)} %fusion.24, bf16[512,4096]{1,0:T(8,128)(2,1)} %param.13, s32[]{:T(128)S(6)} %select_n.302), kind=kOutput, calls=%fused_computation.1 | convolution fusion | flops 67108864 | bytes 917508 | tf_op jit(solution)/shard_map/dot_general | solution.py:156
  91.6 1.3 %convolution_bitcast_fusion.2 = f32[1,128,512]{2,1,0:T(8,128)S(1)} fusion(bf16[128,512]{0,1:T(8,128)(2,1)S(1)} %fusion.24, bf16[512,4096]{1,0:T(8,128)(2,1)} %param.13, s32[]{:T(128)S(6)} %select_n.301), kind=kOutput, calls=%fused_computation.2 | convolution fusion | flops 67108864 | bytes 917508 | tf_op jit(solution)/shard_map/dot_general | solution.py:156
  92.9 1.3 %convolution_bitcast_fusion.3 = f32[1,128,512]{2,1,0:T(8,128)S(1)} fusion(bf16[128,512]{0,1:T(8,128)(2,1)S(1)} %fusion.24, bf16[512,4096]{1,0:T(8,128)(2,1)} %param.13, s32[]{:T(128)S(6)} %select_n.300), kind=kOutput, calls=%fused_computation.3 | convolution fusion | flops 67108864 | bytes 917508 | tf_op jit(solution)/shard_map/dot_general | solution.py:156
  94.2 1.3 %convolution_bitcast_fusion = f32[1,128,512]{2,1,0:T(8,128)S(1)} fusion(bf16[128,512]{0,1:T(8,128)(2,1)S(1)} %fusion.24, bf16[512,4096]{1,0:T(8,128)(2,1)} %param.13, s32[]{:T(128)S(6)} %select_n.303), kind=kOutput, calls=%fused_computation | convolution fusion | flops 67108864 | bytes 917508 | tf_op jit(solution)/shard_map/dot_general | solution.py:156
  95.6 1.9 %collective-permute-start.9 = (f32[4,128,512]{2,1,0:T(8,128)S(1)}, f32[4,128,512]{2,1,0:T(8,128)S(1)}, u32[]{:S(2)}, u32[]{:S(2)}) collective-permute-start(f32[4,128,512]{2,1,0:T(8,128)S(1)} %pad_maximum_fusion), channel_id=1, source_target_pairs={{0,1},{1,0},{2,3},{3,2},{4,5},{5,4},{6,7},{7,6},{8,9},{9,8},{10,11... | collective-permute-start | bytes 3145736 | tf_op jit(solution)/shard_map/ppermute | solution.py:110
  98.9 1.3 %convolution_bitcast_fusion.5 = f32[1,128,512]{2,1,0:T(8,128)S(1)} fusion(bf16[128,512]{0,1:T(8,128)(2,1)S(1)} %fusion.24, bf16[512,4096]{1,0:T(8,128)(2,1)} %param.13, s32[]{:T(128)S(6)} %select_n.298), kind=kOutput, calls=%fused_computation.5 | convolution fusion | flops 67108864 | bytes 917508 | tf_op jit(solution)/shard_map/dot_general | solution.py:156
  100.2 1.3 %convolution_bitcast_fusion.6 = f32[1,128,512]{2,1,0:T(8,128)S(1)} fusion(bf16[128,512]{0,1:T(8,128)(2,1)S(1)} %fusion.24, bf16[512,4096]{1,0:T(8,128)(2,1)} %param.13, s32[]{:T(128)S(6)} %select_n.297), kind=kOutput, calls=%fused_computation.6 | convolution fusion | flops 67108864 | bytes 917508 | tf_op jit(solution)/shard_map/dot_general | solution.py:156
  101.5 1.3 %convolution_bitcast_fusion.7 = f32[1,128,512]{2,1,0:T(8,128)S(1)} fusion(bf16[128,512]{0,1:T(8,128)(2,1)S(1)} %fusion.24, bf16[512,4096]{1,0:T(8,128)(2,1)} %param.13, s32[]{:T(128)S(6)} %select_n.296), kind=kOutput, calls=%fused_computation.7 | convolution fusion | flops 67108864 | bytes 917508 | tf_op jit(solution)/shard_map/dot_general | solution.py:156
  103.1 3.1 %collective-permute-start.10 = (f32[128,512]{1,0:T(8,128)S(1)}, f32[128,512]{1,0:T(8,128)S(1)}, u32[]{:S(2)}, u32[]{:S(2)}) collective-permute-start(f32[128,512]{1,0:T(8,128)S(1)} %get-tuple-element.39), channel_id=1, source_target_pairs={{0,4},{1,5},{2,6},{3,7},{4,0},{5,1},{6,2},{7,3},{8,12},{9,13},{10,... | collective-permute-start | bytes 786440 | tf_op jit(solution)/shard_map/ppermute | solution.py:118
  106.3 4.1 %collective-permute-start.11 = (f32[128,512]{1,0:T(8,128)S(1)}, f32[128,512]{1,0:T(8,128)S(1)}, u32[]{:S(2)}, u32[]{:S(2)}) collective-permute-start(f32[128,512]{1,0:T(8,128)S(1)} %get-tuple-element.41), channel_id=1, source_target_pairs={{0,2},{1,3},{2,4},{3,5},{4,6},{5,7},{6,0},{7,1},{8,10},{9,11},{10,... | collective-permute-start | bytes 786440 | tf_op jit(solution)/shard_map/ppermute | solution.py:118
  110.4 1.9 %collective-permute-start.12 = (f32[128,512]{1,0:T(8,128)S(1)}, f32[128,512]{1,0:T(8,128)S(1)}, u32[]{:S(2)}, u32[]{:S(2)}) collective-permute-start(f32[128,512]{1,0:T(8,128)S(1)} %get-tuple-element.40), channel_id=1, source_target_pairs={{0,6},{1,7},{2,0},{3,1},{4,2},{5,3},{6,4},{7,5},{8,14},{9,15},{10,... | collective-permute-start | bytes 786440 | tf_op jit(solution)/shard_map/ppermute | solution.py:118
  112.6 3.0 %collective-permute-done.10 = f32[128,512]{1,0:T(8,128)S(1)} collective-permute-done((f32[128,512]{1,0:T(8,128)S(1)}, f32[128,512]{1,0:T(8,128)S(1)}, u32[]{:S(2)}, u32[]{:S(2)}) %collective-permute-start.10) | collective-permute-done | bytes 262176 | tf_op jit(solution)/shard_map/ppermute | solution.py:118
  115.6 2.8 %collective-permute-done.11 = f32[128,512]{1,0:T(8,128)S(1)} collective-permute-done((f32[128,512]{1,0:T(8,128)S(1)}, f32[128,512]{1,0:T(8,128)S(1)}, u32[]{:S(2)}, u32[]{:S(2)}) %collective-permute-start.11) | collective-permute-done | bytes 262176 | tf_op jit(solution)/shard_map/ppermute | solution.py:118
  118.4 3.2 %collective-permute-done.12 = f32[128,512]{1,0:T(8,128)S(1)} collective-permute-done((f32[128,512]{1,0:T(8,128)S(1)}, f32[128,512]{1,0:T(8,128)S(1)}, u32[]{:S(2)}, u32[]{:S(2)}) %collective-permute-start.12) | collective-permute-done | bytes 262176 | tf_op jit(solution)/shard_map/ppermute | solution.py:118
  (81 shorter events, 16.3 us)
Async XLA Ops:
  0.0 112.3 %copy-start = (bf16[16,512]{1,0:T(8,128)(2,1)S(1)}, bf16[16,512]{1,0:T(8,128)(2,1)}, u32[]{:S(2)}) copy-start(bf16[16,512]{1,0:T(8,128)(2,1)} %param.15) | copy-start | bytes 49156
  4.4 10.5 %collective-permute-start = (f32[4,136,128]{2,1,0:T(8,128)S(1)}, f32[4,136,128]{2,1,0:T(8,128)S(1)}, u32[]{:S(2)}, u32[]{:S(2)}) collective-permute-start(f32[4,136,128]{2,1,0:T(8,128)S(1)} %pad_maximum_fusion.1), channel_id=1, source_target_pairs={{0,8},{16,24},{32,40},{48,56},{64,72},{80,88},{96,104},{112,120},{... | collective-permute-start | bytes 835592 | tf_op jit(solution)/shard_map/ppermute | solution.py:86
  15.1 6.8 %collective-permute-start.1 = (f32[4,136,128]{2,1,0:T(8,128)S(1)}, f32[4,136,128]{2,1,0:T(8,128)S(1)}, u32[]{:S(2)}, u32[]{:S(2)}) collective-permute-start(f32[4,136,128]{2,1,0:T(8,128)S(1)} %get-tuple-element.36), channel_id=1, source_target_pairs={{8,24},{40,56},{72,88},{104,120},{112,96},{80,64},{48,32},{16,0},{... | collective-permute-start | bytes 835592 | tf_op jit(solution)/shard_map/ppermute | solution.py:86
  21.9 3.5 %copy-start.1 = (bf16[128,512]{1,0:T(8,128)(2,1)S(1)}, bf16[128,512]{1,0:T(8,128)(2,1)}, u32[]{:S(2)}) copy-start(bf16[128,512]{1,0:T(8,128)(2,1)} %param.8) | copy-start | bytes 393220
  22.2 0.7 collective-permute-start.2
  23.1 0.7 collective-permute-start.3
  24.1 52.7 %copy-start.2 = (f32[128,4]{0,1:T(4,128)S(1)}, f32[128,4]{0,1:T(4,128)}, u32[]{:S(2)}) copy-start(f32[128,4]{0,1:T(4,128)} %param.11) | copy-start | bytes 6148
  24.1 41.9 %collective-permute-start.4 = (f32[4,136,128]{2,1,0:T(8,128)S(1)}, f32[4,136,128]{2,1,0:T(8,128)S(1)}, u32[]{:S(2)}, u32[]{:S(2)}) collective-permute-start(f32[4,136,128]{2,1,0:T(8,128)S(1)} %get-tuple-element.19), channel_id=1, source_target_pairs={{24,40},{56,72},{88,104},{96,80},{64,48},{32,16},{152,168},{184,20... | collective-permute-start | bytes 835592 | tf_op jit(solution)/shard_map/ppermute | solution.py:86
  66.3 23.9 %copy-start.3 = (f32[512]{0:T(512)S(1)}, f32[512]{0:T(512)}, u32[]{:S(2)}) copy-start(f32[512]{0:T(512)} %param.12) | copy-start | bytes 6148
  66.3 8.4 %collective-permute-start.5 = (f32[4,136,128]{2,1,0:T(8,128)S(1)}, f32[4,136,128]{2,1,0:T(8,128)S(1)}, u32[]{:S(2)}, u32[]{:S(2)}) collective-permute-start(f32[4,136,128]{2,1,0:T(8,128)S(1)} %add_select_fusion), channel_id=1, source_target_pairs={{8,16},{24,32},{40,48},{56,64},{72,80},{88,96},{104,112},{112,104}... | collective-permute-start | bytes 835592 | tf_op jit(solution)/shard_map/ppermute | solution.py:86
  75.1 9.9 %collective-permute-start.7 = (f32[4,136,128]{2,1,0:T(8,128)S(1)}, f32[4,136,128]{2,1,0:T(8,128)S(1)}, u32[]{:S(2)}, u32[]{:S(2)}) collective-permute-start(f32[4,136,128]{2,1,0:T(8,128)S(1)} %get-tuple-element.17), channel_id=1, source_target_pairs={{0,256},{8,264},{16,272},{24,280},{32,288},{40,296},{48,304},{56,3... | collective-permute-start | bytes 835592 | tf_op jit(solution)/shard_map/ppermute | solution.py:98
  77.2 8.5 %collective-permute-start.6 = (f32[4,136,128]{2,1,0:T(8,128)S(1)}, f32[4,136,128]{2,1,0:T(8,128)S(1)}, u32[]{:S(2)}, u32[]{:S(2)}) collective-permute-start(f32[4,136,128]{2,1,0:T(8,128)S(1)} %get-tuple-element.17), channel_id=1, source_target_pairs={{0,128},{8,136},{16,144},{24,152},{32,160},{40,168},{48,176},{56,1... | collective-permute-start | bytes 835592 | tf_op jit(solution)/shard_map/ppermute | solution.py:98
  78.5 11.2 %collective-permute-start.8 = (f32[4,136,128]{2,1,0:T(8,128)S(1)}, f32[4,136,128]{2,1,0:T(8,128)S(1)}, u32[]{:S(2)}, u32[]{:S(2)}) collective-permute-start(f32[4,136,128]{2,1,0:T(8,128)S(1)} %get-tuple-element.17), channel_id=1, source_target_pairs={{0,384},{8,392},{16,400},{24,408},{32,416},{40,424},{48,432},{56,4... | collective-permute-start | bytes 835592 | tf_op jit(solution)/shard_map/ppermute | solution.py:98
  95.6 7.2 %collective-permute-start.9 = (f32[4,128,512]{2,1,0:T(8,128)S(1)}, f32[4,128,512]{2,1,0:T(8,128)S(1)}, u32[]{:S(2)}, u32[]{:S(2)}) collective-permute-start(f32[4,128,512]{2,1,0:T(8,128)S(1)} %pad_maximum_fusion), channel_id=1, source_target_pairs={{0,1},{1,0},{2,3},{3,2},{4,5},{5,4},{6,7},{7,6},{8,9},{9,8},{10,11... | collective-permute-start | bytes 3145736 | tf_op jit(solution)/shard_map/ppermute | solution.py:110
  97.6 14.7 %copy-start.4 = (s32[128]{0:T(128)S(1)}, s32[128]{0:T(128)}, u32[]{:S(2)}) copy-start(s32[128]{0:T(128)} %param.14) | copy-start | bytes 1540
  103.1 12.4 %collective-permute-start.10 = (f32[128,512]{1,0:T(8,128)S(1)}, f32[128,512]{1,0:T(8,128)S(1)}, u32[]{:S(2)}, u32[]{:S(2)}) collective-permute-start(f32[128,512]{1,0:T(8,128)S(1)} %get-tuple-element.39), channel_id=1, source_target_pairs={{0,4},{1,5},{2,6},{3,7},{4,0},{5,1},{6,2},{7,3},{8,12},{9,13},{10,... | collective-permute-start | bytes 786440 | tf_op jit(solution)/shard_map/ppermute | solution.py:118
  106.3 12.1 %collective-permute-start.11 = (f32[128,512]{1,0:T(8,128)S(1)}, f32[128,512]{1,0:T(8,128)S(1)}, u32[]{:S(2)}, u32[]{:S(2)}) collective-permute-start(f32[128,512]{1,0:T(8,128)S(1)} %get-tuple-element.41), channel_id=1, source_target_pairs={{0,2},{1,3},{2,4},{3,5},{4,6},{5,7},{6,0},{7,1},{8,10},{9,11},{10,... | collective-permute-start | bytes 786440 | tf_op jit(solution)/shard_map/ppermute | solution.py:118
  110.4 11.3 %collective-permute-start.12 = (f32[128,512]{1,0:T(8,128)S(1)}, f32[128,512]{1,0:T(8,128)S(1)}, u32[]{:S(2)}, u32[]{:S(2)}) collective-permute-start(f32[128,512]{1,0:T(8,128)S(1)} %get-tuple-element.40), channel_id=1, source_target_pairs={{0,6},{1,7},{2,0},{3,1},{4,2},{5,3},{6,4},{7,5},{8,14},{9,15},{10,... | collective-permute-start | bytes 786440 | tf_op jit(solution)/shard_map/ppermute | solution.py:118

commit v9 on v5

--- a/solution.py
+++ b/solution.py
@@ -137,10 +137,14 @@
 
     decays = log_decay.reshape(count, SPAN, heads_here).transpose(0, 2, 1)
     start = jnp.zeros((heads_here, head_size, head_size), jnp.float32)
-    local_memory, blocks = lax.scan(
-        block_step, start, (split(queries), split(keys), split(values), decays)
-    )
-    device_log = jnp.sum(log_decay, axis=0)
+    def step_with_total(state, inputs):
+        new_state, out = block_step(state, inputs)
+        return new_state, (out, jnp.cumsum(inputs[3], axis=1)[:, -1])
+
+    local_memory, (blocks, block_logs) = lax.scan(
+        step_with_total, start, (split(queries), split(keys), split(values), decays)
+    )
+    device_log = jnp.sum(block_logs, axis=0)
     lines, width = seq_n // seq_width, seq_width
     passed = exclusive_scan(pack(device_log, local_memory), "seq", lines, width)
     earlier_memory = passed[:, :head_size, :]

time: 121 us -> 120 us (level)
  no operation moved by 1% of the time
where the time goes in v9:
time: 120 us; the launch traced here: 119 us
  waiting for transfers between devices  70.4 us (59%)
  starting transfers between devices  36.6 us (30%)
  matrix products  4.68 us (4%)
  other arithmetic  3.93 us (3%)
  local copies, waits for them, and re-layouts  2.94 us (2%)
    ppermute x6, waiting for transfers between devices, exclusive_scan(): got = lax.ppermute(send, axis, full)  49.5 us
    ppermute x1, starting transfers between devices, scatter_heads(): mine = keep + lax.ppermute(away, axis, pairs)  13.5 us
    ppermute x3, waiting for transfers between devices, scatter_heads(): out = out + lax.ppermute(send, axis, pairs)  10.4 us
    ppermute x3, starting transfers between devices, scatter_heads(): out = out + lax.ppermute(send, axis, pairs)  9.81 us
    ppermute x6, starting transfers between devices, exclusive_scan(): got = lax.ppermute(send, axis, full)  9.42 us
    ppermute x3, waiting for transfers between devices, exclusive_scan(): got = lax.ppermute(total, axis, pairs)  8.3 us
    ppermute x3, starting transfers between devices, exclusive_scan(): got = lax.ppermute(total, axis, pairs)  3.89 us
    dot_general x1, matrix products, shards(): jnp.dot(normed, out_weight, preferred_element_type=jnp.float32)  2.93 us
  transfers between devices with their start and end apart: 13, of which 10 were waited for; matrix products, arithmetic and copies ran while one was open for 1% of the time, Pallas kernels for 0%

profile of v9, /device:TPU:79, one launch (start us, length us, event | category | flops | bytes accessed | tf_op | source)
XLA Modules:
  0.0 119.2 jit_solution(746547370323540680)
XLA Ops:
  0.0 1.0 reduce_window_sum.24
  1.3 1.0 copy.30
  2.3 0.9 reshape.92
  3.6 3.5 %collective-permute-start = (f32[4,136,128]{2,1,0:T(8,128)S(1)}, f32[4,136,128]{2,1,0:T(8,128)S(1)}, u32[]{:S(2)}, u32[]{:S(2)}) collective-permute-start(f32[4,136,128]{2,1,0:T(8,128)S(1)} %pad_maximum_fusion.1), channel_id=1, source_target_pairs={{0,8},{16,24},{32,40},{48,56},{64,72},{80,88},{96,104},{112,120},{... | collective-permute-start | bytes 835592 | tf_op jit(solution)/shard_map/ppermute | solution.py:86
  7.2 6.2 %collective-permute-done = f32[4,136,128]{2,1,0:T(8,128)S(1)} collective-permute-done((f32[4,136,128]{2,1,0:T(8,128)S(1)}, f32[4,136,128]{2,1,0:T(8,128)S(1)}, u32[]{:S(2)}, u32[]{:S(2)}) %collective-permute-start) | collective-permute-done | bytes 278560 | tf_op jit(solution)/shard_map/ppermute | solution.py:86
  13.6 1.3 %collective-permute-start.1 = (f32[4,136,128]{2,1,0:T(8,128)S(1)}, f32[4,136,128]{2,1,0:T(8,128)S(1)}, u32[]{:S(2)}, u32[]{:S(2)}) collective-permute-start(f32[4,136,128]{2,1,0:T(8,128)S(1)} %get-tuple-element.41), channel_id=1, source_target_pairs={{8,24},{40,56},{72,88},{104,120},{112,96},{80,64},{48,32},{16,0},{... | collective-permute-start | bytes 835592 | tf_op jit(solution)/shard_map/ppermute | solution.py:86
  15.0 4.6 %collective-permute-done.1 = f32[4,136,128]{2,1,0:T(8,128)S(1)} collective-permute-done((f32[4,136,128]{2,1,0:T(8,128)S(1)}, f32[4,136,128]{2,1,0:T(8,128)S(1)}, u32[]{:S(2)}, u32[]{:S(2)}) %collective-permute-start.1) | collective-permute-done | bytes 278560 | tf_op jit(solution)/shard_map/ppermute | solution.py:86
  21.8 1.3 %collective-permute-start.4 = (f32[4,136,128]{2,1,0:T(8,128)S(1)}, f32[4,136,128]{2,1,0:T(8,128)S(1)}, u32[]{:S(2)}, u32[]{:S(2)}) collective-permute-start(f32[4,136,128]{2,1,0:T(8,128)S(1)} %get-tuple-element.23), channel_id=1, source_target_pairs={{24,40},{56,72},{88,104},{96,80},{64,48},{32,16},{152,168},{184,20... | collective-permute-start | bytes 835592 | tf_op jit(solution)/shard_map/ppermute | solution.py:86
  23.2 33.5 %collective-permute-done.4 = f32[4,136,128]{2,1,0:T(8,128)S(1)} collective-permute-done((f32[4,136,128]{2,1,0:T(8,128)S(1)}, f32[4,136,128]{2,1,0:T(8,128)S(1)}, u32[]{:S(2)}, u32[]{:S(2)}) %collective-permute-start.4) | collective-permute-done | bytes 278560 | tf_op jit(solution)/shard_map/ppermute | solution.py:86
  56.9 1.9 %collective-permute-start.5 = (f32[4,136,128]{2,1,0:T(8,128)S(1)}, f32[4,136,128]{2,1,0:T(8,128)S(1)}, u32[]{:S(2)}, u32[]{:S(2)}) collective-permute-start(f32[4,136,128]{2,1,0:T(8,128)S(1)} %add_select_fusion), channel_id=1, source_target_pairs={{8,16},{24,32},{40,48},{56,64},{72,80},{88,96},{104,112},{112,104}... | collective-permute-start | bytes 835592 | tf_op jit(solution)/shard_map/ppermute | solution.py:86
  59.2 5.2 %collective-permute-done.5 = f32[4,136,128]{2,1,0:T(8,128)S(1)} collective-permute-done((f32[4,136,128]{2,1,0:T(8,128)S(1)}, f32[4,136,128]{2,1,0:T(8,128)S(1)}, u32[]{:S(2)}, u32[]{:S(2)}) %collective-permute-start.5) | collective-permute-done | bytes 278560 | tf_op jit(solution)/shard_map/ppermute | solution.py:86
  64.9 1.3 %collective-permute-start.7 = (f32[4,136,128]{2,1,0:T(8,128)S(1)}, f32[4,136,128]{2,1,0:T(8,128)S(1)}, u32[]{:S(2)}, u32[]{:S(2)}) collective-permute-start(f32[4,136,128]{2,1,0:T(8,128)S(1)} %get-tuple-element.21), channel_id=1, source_target_pairs={{0,256},{8,264},{16,272},{24,280},{32,288},{40,296},{48,304},{56,3... | collective-permute-start | bytes 835592 | tf_op jit(solution)/shard_map/ppermute | solution.py:98
  66.9 1.3 %collective-permute-start.6 = (f32[4,136,128]{2,1,0:T(8,128)S(1)}, f32[4,136,128]{2,1,0:T(8,128)S(1)}, u32[]{:S(2)}, u32[]{:S(2)}) collective-permute-start(f32[4,136,128]{2,1,0:T(8,128)S(1)} %get-tuple-element.21), channel_id=1, source_target_pairs={{0,128},{8,136},{16,144},{24,152},{32,160},{40,168},{48,176},{56,1... | collective-permute-start | bytes 835592 | tf_op jit(solution)/shard_map/ppermute | solution.py:98
  68.3 1.3 %collective-permute-start.8 = (f32[4,136,128]{2,1,0:T(8,128)S(1)}, f32[4,136,128]{2,1,0:T(8,128)S(1)}, u32[]{:S(2)}, u32[]{:S(2)}) collective-permute-start(f32[4,136,128]{2,1,0:T(8,128)S(1)} %get-tuple-element.21), channel_id=1, source_target_pairs={{0,384},{8,392},{16,400},{24,408},{32,416},{40,424},{48,432},{56,4... | collective-permute-start | bytes 835592 | tf_op jit(solution)/shard_map/ppermute | solution.py:98
  69.6 4.1 %collective-permute-done.7 = f32[4,136,128]{2,1,0:T(8,128)S(1)} collective-permute-done((f32[4,136,128]{2,1,0:T(8,128)S(1)}, f32[4,136,128]{2,1,0:T(8,128)S(1)}, u32[]{:S(2)}, u32[]{:S(2)}) %collective-permute-start.7) | collective-permute-done | bytes 278560 | tf_op jit(solution)/shard_map/ppermute | solution.py:98
  74.4 3.6 %collective-permute-done.8 = f32[4,136,128]{2,1,0:T(8,128)S(1)} collective-permute-done((f32[4,136,128]{2,1,0:T(8,128)S(1)}, f32[4,136,128]{2,1,0:T(8,128)S(1)}, u32[]{:S(2)}, u32[]{:S(2)}) %collective-permute-start.8) | collective-permute-done | bytes 278560 | tf_op jit(solution)/shard_map/ppermute | solution.py:98
  78.7 2.9 %fusion.52 = f32[128,4096]{1,0:T(8,128)S(1)} fusion(bf16[128,512]{0,1:T(8,128)(2,1)S(1)} %fusion.16, bf16[512,4096]{1,0:T(8,128)(2,1)} %param.13), kind=kOutput, calls=%fused_computation.130 | convolution fusion | flops 536870912 | bytes 6422528 | tf_op jit(solution)/shard_map/dot_general | solution.py:160
  81.9 13.5 %collective-permute-start.9 = (f32[4,128,512]{2,1,0:T(8,128)S(1)}, f32[4,128,512]{2,1,0:T(8,128)S(1)}, u32[]{:S(2)}, u32[]{:S(2)}) collective-permute-start(f32[4,128,512]{2,1,0:T(8,128)S(1)} %pad_maximum_fusion), channel_id=1, source_target_pairs={{0,1},{1,0},{2,3},{3,2},{4,5},{5,4},{6,7},{7,6},{8,9},{9,8},{10,11... | collective-permute-start | bytes 3145736 | tf_op jit(solution)/shard_map/ppermute | solution.py:118
  95.5 2.2 %collective-permute-done.9 = f32[4,128,512]{2,1,0:T(8,128)S(1)} collective-permute-done((f32[4,128,512]{2,1,0:T(8,128)S(1)}, f32[4,128,512]{2,1,0:T(8,128)S(1)}, u32[]{:S(2)}, u32[]{:S(2)}) %collective-permute-start.9) | collective-permute-done | bytes 1048608 | tf_op jit(solution)/shard_map/ppermute | solution.py:118
  98.0 3.2 %collective-permute-start.10 = (f32[128,512]{1,0:T(8,128)S(1)}, f32[128,512]{1,0:T(8,128)S(1)}, u32[]{:S(2)}, u32[]{:S(2)}) collective-permute-start(f32[128,512]{1,0:T(8,128)S(1)} %get-tuple-element.52), channel_id=1, source_target_pairs={{0,2},{1,3},{2,4},{3,5},{4,6},{5,7},{6,0},{7,1},{8,10},{9,11},{10,... | collective-permute-start | bytes 786440 | tf_op jit(solution)/shard_map/ppermute | solution.py:123
  101.2 2.6 %collective-permute-start.11 = (f32[128,512]{1,0:T(8,128)S(1)}, f32[128,512]{1,0:T(8,128)S(1)}, u32[]{:S(2)}, u32[]{:S(2)}) collective-permute-start(f32[128,512]{1,0:T(8,128)S(1)} %get-tuple-element.54), channel_id=1, source_target_pairs={{0,4},{1,5},{2,6},{3,7},{4,0},{5,1},{6,2},{7,3},{8,12},{9,13},{10,... | collective-permute-start | bytes 786440 | tf_op jit(solution)/shard_map/ppermute | solution.py:123
  103.8 4.0 %collective-permute-start.12 = (f32[128,512]{1,0:T(8,128)S(1)}, f32[128,512]{1,0:T(8,128)S(1)}, u32[]{:S(2)}, u32[]{:S(2)}) collective-permute-start(f32[128,512]{1,0:T(8,128)S(1)} %get-tuple-element.53), channel_id=1, source_target_pairs={{0,6},{1,7},{2,0},{3,1},{4,2},{5,3},{6,4},{7,5},{8,14},{9,15},{10,... | collective-permute-start | bytes 786440 | tf_op jit(solution)/shard_map/ppermute | solution.py:123
  108.1 3.8 %collective-permute-done.11 = f32[128,512]{1,0:T(8,128)S(1)} collective-permute-done((f32[128,512]{1,0:T(8,128)S(1)}, f32[128,512]{1,0:T(8,128)S(1)}, u32[]{:S(2)}, u32[]{:S(2)}) %collective-permute-start.11) | collective-permute-done | bytes 262176 | tf_op jit(solution)/shard_map/ppermute | solution.py:123
  111.8 6.6 %collective-permute-done.12 = f32[128,512]{1,0:T(8,128)S(1)} collective-permute-done((f32[128,512]{1,0:T(8,128)S(1)}, f32[128,512]{1,0:T(8,128)S(1)}, u32[]{:S(2)}, u32[]{:S(2)}) %collective-permute-start.12) | collective-permute-done | bytes 262176 | tf_op jit(solution)/shard_map/ppermute | solution.py:123
  (73 shorter events, 7.6 us)
Async XLA Ops:
  0.0 107.8 %copy-start = (bf16[16,512]{1,0:T(8,128)(2,1)S(1)}, bf16[16,512]{1,0:T(8,128)(2,1)}, u32[]{:S(2)}) copy-start(bf16[16,512]{1,0:T(8,128)(2,1)} %param.15) | copy-start | bytes 49156
  3.6 9.8 %collective-permute-start = (f32[4,136,128]{2,1,0:T(8,128)S(1)}, f32[4,136,128]{2,1,0:T(8,128)S(1)}, u32[]{:S(2)}, u32[]{:S(2)}) collective-permute-start(f32[4,136,128]{2,1,0:T(8,128)S(1)} %pad_maximum_fusion.1), channel_id=1, source_target_pairs={{0,8},{16,24},{32,40},{48,56},{64,72},{80,88},{96,104},{112,120},{... | collective-permute-start | bytes 835592 | tf_op jit(solution)/shard_map/ppermute | solution.py:86
  13.6 6.0 %collective-permute-start.1 = (f32[4,136,128]{2,1,0:T(8,128)S(1)}, f32[4,136,128]{2,1,0:T(8,128)S(1)}, u32[]{:S(2)}, u32[]{:S(2)}) collective-permute-start(f32[4,136,128]{2,1,0:T(8,128)S(1)} %get-tuple-element.41), channel_id=1, source_target_pairs={{8,24},{40,56},{72,88},{104,120},{112,96},{80,64},{48,32},{16,0},{... | collective-permute-start | bytes 835592 | tf_op jit(solution)/shard_map/ppermute | solution.py:86
  19.6 3.5 %copy-start.1 = (bf16[128,512]{1,0:T(8,128)(2,1)S(1)}, bf16[128,512]{1,0:T(8,128)(2,1)}, u32[]{:S(2)}) copy-start(bf16[128,512]{1,0:T(8,128)(2,1)} %param.8) | copy-start | bytes 393220
  19.9 0.7 collective-permute-start.2
  20.8 0.7 collective-permute-start.3
  21.8 44.7 %copy-start.2 = (f32[128,4]{0,1:T(4,128)S(1)}, f32[128,4]{0,1:T(4,128)}, u32[]{:S(2)}) copy-start(f32[128,4]{0,1:T(4,128)} %param.11) | copy-start | bytes 6148
  21.8 34.9 %collective-permute-start.4 = (f32[4,136,128]{2,1,0:T(8,128)S(1)}, f32[4,136,128]{2,1,0:T(8,128)S(1)}, u32[]{:S(2)}, u32[]{:S(2)}) collective-permute-start(f32[4,136,128]{2,1,0:T(8,128)S(1)} %get-tuple-element.23), channel_id=1, source_target_pairs={{24,40},{56,72},{88,104},{96,80},{64,48},{32,16},{152,168},{184,20... | collective-permute-start | bytes 835592 | tf_op jit(solution)/shard_map/ppermute | solution.py:86
  56.9 21.6 %copy-start.3 = (f32[512]{0:T(512)S(1)}, f32[512]{0:T(512)}, u32[]{:S(2)}) copy-start(f32[512]{0:T(512)} %param.12) | copy-start | bytes 6148
  56.9 7.6 %collective-permute-start.5 = (f32[4,136,128]{2,1,0:T(8,128)S(1)}, f32[4,136,128]{2,1,0:T(8,128)S(1)}, u32[]{:S(2)}, u32[]{:S(2)}) collective-permute-start(f32[4,136,128]{2,1,0:T(8,128)S(1)} %add_select_fusion), channel_id=1, source_target_pairs={{8,16},{24,32},{40,48},{56,64},{72,80},{88,96},{104,112},{112,104}... | collective-permute-start | bytes 835592 | tf_op jit(solution)/shard_map/ppermute | solution.py:86
  64.9 8.8 %collective-permute-start.7 = (f32[4,136,128]{2,1,0:T(8,128)S(1)}, f32[4,136,128]{2,1,0:T(8,128)S(1)}, u32[]{:S(2)}, u32[]{:S(2)}) collective-permute-start(f32[4,136,128]{2,1,0:T(8,128)S(1)} %get-tuple-element.21), channel_id=1, source_target_pairs={{0,256},{8,264},{16,272},{24,280},{32,288},{40,296},{48,304},{56,3... | collective-permute-start | bytes 835592 | tf_op jit(solution)/shard_map/ppermute | solution.py:98
  66.9 7.3 %collective-permute-start.6 = (f32[4,136,128]{2,1,0:T(8,128)S(1)}, f32[4,136,128]{2,1,0:T(8,128)S(1)}, u32[]{:S(2)}, u32[]{:S(2)}) collective-permute-start(f32[4,136,128]{2,1,0:T(8,128)S(1)} %get-tuple-element.21), channel_id=1, source_target_pairs={{0,128},{8,136},{16,144},{24,152},{32,160},{40,168},{48,176},{56,1... | collective-permute-start | bytes 835592 | tf_op jit(solution)/shard_map/ppermute | solution.py:98
  68.3 9.7 %collective-permute-start.8 = (f32[4,136,128]{2,1,0:T(8,128)S(1)}, f32[4,136,128]{2,1,0:T(8,128)S(1)}, u32[]{:S(2)}, u32[]{:S(2)}) collective-permute-start(f32[4,136,128]{2,1,0:T(8,128)S(1)} %get-tuple-element.21), channel_id=1, source_target_pairs={{0,384},{8,392},{16,400},{24,408},{32,416},{40,424},{48,432},{56,4... | collective-permute-start | bytes 835592 | tf_op jit(solution)/shard_map/ppermute | solution.py:98
  81.8 26.0 %copy-start.4 = (s32[128]{0:T(128)S(1)}, s32[128]{0:T(128)}, u32[]{:S(2)}) copy-start(s32[128]{0:T(128)} %param.14) | copy-start | bytes 1540
  81.9 15.7 %collective-permute-start.9 = (f32[4,128,512]{2,1,0:T(8,128)S(1)}, f32[4,128,512]{2,1,0:T(8,128)S(1)}, u32[]{:S(2)}, u32[]{:S(2)}) collective-permute-start(f32[4,128,512]{2,1,0:T(8,128)S(1)} %pad_maximum_fusion), channel_id=1, source_target_pairs={{0,1},{1,0},{2,3},{3,2},{4,5},{5,4},{6,7},{7,6},{8,9},{9,8},{10,11... | collective-permute-start | bytes 3145736 | tf_op jit(solution)/shard_map/ppermute | solution.py:118
  98.0 10.1 %collective-permute-start.10 = (f32[128,512]{1,0:T(8,128)S(1)}, f32[128,512]{1,0:T(8,128)S(1)}, u32[]{:S(2)}, u32[]{:S(2)}) collective-permute-start(f32[128,512]{1,0:T(8,128)S(1)} %get-tuple-element.52), channel_id=1, source_target_pairs={{0,2},{1,3},{2,4},{3,5},{4,6},{5,7},{6,0},{7,1},{8,10},{9,11},{10,... | collective-permute-start | bytes 786440 | tf_op jit(solution)/shard_map/ppermute | solution.py:123
  101.2 10.6 %collective-permute-start.11 = (f32[128,512]{1,0:T(8,128)S(1)}, f32[128,512]{1,0:T(8,128)S(1)}, u32[]{:S(2)}, u32[]{:S(2)}) collective-permute-start(f32[128,512]{1,0:T(8,128)S(1)} %get-tuple-element.54), channel_id=1, source_target_pairs={{0,4},{1,5},{2,6},{3,7},{4,0},{5,1},{6,2},{7,3},{8,12},{9,13},{10,... | collective-permute-start | bytes 786440 | tf_op jit(solution)/shard_map/ppermute | solution.py:123
  103.8 14.6 %collective-permute-start.12 = (f32[128,512]{1,0:T(8,128)S(1)}, f32[128,512]{1,0:T(8,128)S(1)}, u32[]{:S(2)}, u32[]{:S(2)}) collective-permute-start(f32[128,512]{1,0:T(8,128)S(1)} %get-tuple-element.53), channel_id=1, source_target_pairs={{0,6},{1,7},{2,0},{3,1},{4,2},{5,3},{6,4},{7,5},{8,14},{9,15},{10,... | collective-permute-start | bytes 786440 | tf_op jit(solution)/shard_map/ppermute | solution.py:123

commit v10 on v9

--- a/solution.py
+++ b/solution.py
@@ -32,15 +32,21 @@
 
 def pack(log_total, memory):
     heads, rows, cols = memory.shape
-    extra = jnp.broadcast_to(log_total[:, None, None], (heads, 8, cols))
-    return jnp.concatenate([memory, extra], axis=1)
-
-
-def join(earlier, later):
-    rows = earlier.shape[1] - 8
-    row = lax.broadcasted_iota(jnp.int32, earlier.shape, 1)
-    scale = jnp.where(row < rows, jnp.exp(later[:, rows:rows + 1, :]), 1.0)
-    return scale * earlier + later
+    extra = jnp.broadcast_to(log_total[:, None], (heads, cols))
+    pad = jnp.zeros(((-heads) % 8, cols), memory.dtype)
+    return jnp.concatenate([memory.reshape(heads * rows, cols), extra, pad], axis=0)
+
+
+def unpack(packed, heads, rows):
+    return packed[: heads * rows].reshape(heads, rows, -1)
+
+
+def join(earlier, later, heads, rows):
+    size = heads * rows
+    scale = jnp.exp(later[size:size + heads])[:, None, :]
+    memory = scale * unpack(earlier, heads, rows) + unpack(later, heads, rows)
+    logs = earlier[size:] + later[size:]
+    return jnp.concatenate([memory.reshape(size, -1), logs], axis=0)
 
 
 def member(position, spots):
@@ -74,7 +80,7 @@
     return rounds
 
 
-def exclusive_scan(part, axis, lines, width):
+def exclusive_scan(part, axis, lines, width, heads, rows):
     pos = lax.axis_index(axis) % width
     held = part
     before = jnp.zeros_like(part)
@@ -86,18 +92,18 @@
         got = lax.ppermute(send, axis, full)
         ahead = jnp.where(member(pos, [e[1] for e in entries if e[3]]), got, 0.0)
         behind = jnp.where(member(pos, [e[1] for e in entries if not e[3]]), got, 0.0)
-        held = join(ahead, held)
-        before = join(ahead, before)
-        after = join(after, behind)
-    total = join(before, after)
+        held = join(ahead, held, heads, rows)
+        before = join(ahead, before, heads, rows)
+        after = join(after, behind, heads, rows)
+    total = join(before, after, heads, rows)
     if lines == 1:
         return before
     earlier = None
     for shift in range(lines - 1, 0, -1):
         pairs = [((l - shift) * width + p, l * width + p) for l in range(shift, lines) for p in range(width)]
         got = lax.ppermute(total, axis, pairs)
-        earlier = got if earlier is None else join(earlier, got)
-    return join(earlier, before)
+        earlier = got if earlier is None else join(earlier, got, heads, rows)
+    return join(earlier, before, heads, rows)
 
 
 def scatter_heads(partial, axis, n):
@@ -146,8 +152,8 @@
     )
     device_log = jnp.sum(block_logs, axis=0)
     lines, width = seq_n // seq_width, seq_width
-    passed = exclusive_scan(pack(device_log, local_memory), "seq", lines, width)
-    earlier_memory = passed[:, :head_size, :]
+    passed = exclusive_scan(pack(device_log, local_memory), "seq", lines, width, heads_here, head_size)
+    earlier_memory = unpack(passed, heads_here, head_size)
     running = jnp.cumsum(log_decay, axis=0)
     query_heads = queries.reshape(tok_rows, heads_here, head_size).astype(jnp.float32)
     carried = jnp.exp(running)[:, :, None] * jnp.einsum(

time: 120 us -> 117 us (0.975)
  the two profiles are of different devices: /device:TPU:79 before, /device:TPU:75 now
where the time goes in v10:
time: 117 us
  waiting for transfers between devices  63.5 us (54%)
  starting transfers between devices  38.7 us (33%)
  other arithmetic  5.36 us (5%)
  local copies, waits for them, and re-layouts  4.2 us (4%)
  matrix products  4.15 us (4%)
    ppermute x6, waiting for transfers between devices, exclusive_scan(): got = lax.ppermute(send, axis, full)  45.8 us
    ppermute x1, starting transfers between devices, scatter_heads(): mine = keep + lax.ppermute(away, axis, pairs)  12 us
    ppermute x3, starting transfers between devices, scatter_heads(): out = out + lax.ppermute(send, axis, pairs)  10.7 us
    ppermute x3, waiting for transfers between devices, scatter_heads(): out = out + lax.ppermute(send, axis, pairs)  10.4 us
    ppermute x6, starting transfers between devices, exclusive_scan(): got = lax.ppermute(send, axis, full)  9.41 us
    ppermute x3, starting transfers between devices, exclusive_scan(): got = lax.ppermute(total, axis, pairs)  6.64 us
    ppermute x3, waiting for transfers between devices, exclusive_scan(): got = lax.ppermute(total, axis, pairs)  5.18 us
    reshape x3, local copies, waits for them, and re-layouts, split(): array.reshape(count, SPAN, heads_here, head_size).transpose(0, 2, 1, 3)  2.97 us
  transfers between devices with their start and end apart: 13, of which 8 were waited for; matrix products, arithmetic and copies ran while one was open for 4% of the time, Pallas kernels for 0%

profile of v10, /device:TPU:75, one launch (start us, length us, event | category | flops | bytes accessed | tf_op | source)
XLA Modules:
  0.0 116.9 jit_solution(6177131375845573417)
XLA Ops:
  0.0 1.0 reduce_window_sum.24
  1.3 1.0 copy.30
  2.3 1.0 reshape.189
  3.9 3.5 %collective-permute-start = (f32[520,128]{1,0:T(8,128)S(1)}, f32[520,128]{1,0:T(8,128)S(1)}, u32[]{:S(2)}, u32[]{:S(2)}) collective-permute-start(f32[520,128]{1,0:T(8,128)S(1)} %maximum_maximum_fusion), channel_id=1, source_target_pairs={{0,8},{16,24},{32,40},{48,56},{64,72},{80,88},{96,104},{112,120},{... | collective-permute-start | bytes 798728 | tf_op jit(solution)/shard_map/ppermute | solution.py:92
  7.5 6.0 %collective-permute-done = f32[520,128]{1,0:T(8,128)S(1)} collective-permute-done((f32[520,128]{1,0:T(8,128)S(1)}, f32[520,128]{1,0:T(8,128)S(1)}, u32[]{:S(2)}, u32[]{:S(2)}) %collective-permute-start) | collective-permute-done | bytes 266272 | tf_op jit(solution)/shard_map/ppermute | solution.py:92
  13.7 1.3 %collective-permute-start.1 = (f32[520,128]{1,0:T(8,128)S(1)}, f32[520,128]{1,0:T(8,128)S(1)}, u32[]{:S(2)}, u32[]{:S(2)}) collective-permute-start(f32[520,128]{1,0:T(8,128)S(1)} %maximum_select_fusion), channel_id=1, source_target_pairs={{8,24},{40,56},{72,88},{104,120},{112,96},{80,64},{48,32},{16,0},{... | collective-permute-start | bytes 798728 | tf_op jit(solution)/shard_map/ppermute | solution.py:92
  15.0 4.4 %collective-permute-done.1 = f32[520,128]{1,0:T(8,128)S(1)} collective-permute-done((f32[520,128]{1,0:T(8,128)S(1)}, f32[520,128]{1,0:T(8,128)S(1)}, u32[]{:S(2)}, u32[]{:S(2)}) %collective-permute-start.1) | collective-permute-done | bytes 266272 | tf_op jit(solution)/shard_map/ppermute | solution.py:92
  21.6 1.3 %collective-permute-start.4 = (f32[520,128]{1,0:T(8,128)S(1)}, f32[520,128]{1,0:T(8,128)}, u32[]{:S(2)}, u32[]{:S(2)}) collective-permute-start(f32[520,128]{1,0:T(8,128)S(1)} %maximum_select_fusion.3), channel_id=1, source_target_pairs={{24,40},{56,72},{88,104},{96,80},{64,48},{32,16},{152,168},{184,20... | collective-permute-start | bytes 798728 | tf_op jit(solution)/shard_map/ppermute | solution.py:92
  22.9 33.1 %collective-permute-done.4 = f32[520,128]{1,0:T(8,128)} collective-permute-done((f32[520,128]{1,0:T(8,128)S(1)}, f32[520,128]{1,0:T(8,128)}, u32[]{:S(2)}, u32[]{:S(2)}) %collective-permute-start.4) | collective-permute-done | bytes 266272 | tf_op jit(solution)/shard_map/ppermute | solution.py:92
  56.1 1.0 broadcast_select_fusion.2
  58.0 1.9 %collective-permute-start.5 = (f32[520,128]{1,0:T(8,128)}, f32[520,128]{1,0:T(8,128)S(1)}, u32[]{:S(2)}, u32[]{:S(2)}) collective-permute-start(f32[520,128]{1,0:T(8,128)} %maximum_select_fusion.4), channel_id=1, source_target_pairs={{8,16},{24,32},{40,48},{56,64},{72,80},{88,96},{104,112},{112,104}... | collective-permute-start | bytes 798728 | tf_op jit(solution)/shard_map/ppermute | solution.py:92
  59.9 0.9 reshape.187
  60.9 2.1 %fusion.6 = f32[4,128,128]{1,2,0:T(8,128)} fusion(bf16[4,128,128]{1,2,0:T(8,128)(2,1)} %bitcast.154, f32[4,128]{1,0:T(4,128)S(1)} %reduce_window_sum.24, pred[128,128]{0,1:T(8,128)(4,1)S(1)} %iota_compare_fusion.1, bf16[1,128,4,128]{3,2,1,0:T(4,128)(2,1)} %copy-done.3, bf16[1,128,4,128]{3,2,1,0:T(4,128)(2,1)S(1)} %reshape.187), kind=kOutput, calls=%fused_computation.10 | convolution fusion | flops 33882112 | bytes 673792 | tf_op jit(solution)/shard_map/while/body/eval_jaxpr/hts,hse->hte/dot_general | solution.py:20
  63.0 2.4 %collective-permute-done.5 = f32[520,128]{1,0:T(8,128)S(1)} collective-permute-done((f32[520,128]{1,0:T(8,128)}, f32[520,128]{1,0:T(8,128)S(1)}, u32[]{:S(2)}, u32[]{:S(2)}) %collective-permute-start.5) | collective-permute-done | bytes 266272 | tf_op jit(solution)/shard_map/ppermute | solution.py:92
  65.8 3.8 %collective-permute-start.7 = (f32[520,128]{1,0:T(8,128)S(1)}, f32[520,128]{1,0:T(8,128)S(1)}, u32[]{:S(2)}, u32[]{:S(2)}) collective-permute-start(f32[520,128]{1,0:T(8,128)S(1)} %pad_maximum_fusion.1), channel_id=1, source_target_pairs={{0,256},{8,264},{16,272},{24,280},{32,288},{40,296},{48,304},{56,3... | collective-permute-start | bytes 798728 | tf_op jit(solution)/shard_map/ppermute | solution.py:104
  71.2 2.1 %collective-permute-start.6 = (f32[520,128]{1,0:T(8,128)S(1)}, f32[520,128]{1,0:T(8,128)S(1)}, u32[]{:S(2)}, u32[]{:S(2)}) collective-permute-start(f32[520,128]{1,0:T(8,128)S(1)} %pad_maximum_fusion.1), channel_id=1, source_target_pairs={{0,128},{8,136},{16,144},{24,152},{32,160},{40,168},{48,176},{56,1... | collective-permute-start | bytes 798728 | tf_op jit(solution)/shard_map/ppermute | solution.py:104
  73.3 5.2 %collective-permute-done.6 = f32[520,128]{1,0:T(8,128)S(1)} collective-permute-done((f32[520,128]{1,0:T(8,128)S(1)}, f32[520,128]{1,0:T(8,128)S(1)}, u32[]{:S(2)}, u32[]{:S(2)}) %collective-permute-start.6) | collective-permute-done | bytes 266272 | tf_op jit(solution)/shard_map/ppermute | solution.py:104
  80.3 12.0 %collective-permute-start.9 = (f32[4,128,512]{2,1,0:T(8,128)S(1)}, f32[4,128,512]{2,1,0:T(8,128)S(1)}, u32[]{:S(2)}, u32[]{:S(2)}) collective-permute-start(f32[4,128,512]{2,1,0:T(8,128)S(1)} %pad_maximum_fusion), channel_id=1, source_target_pairs={{0,1},{1,0},{2,3},{3,2},{4,5},{5,4},{6,7},{7,6},{8,9},{9,8},{10,11... | collective-permute-start | bytes 3145736 | tf_op jit(solution)/shard_map/ppermute | solution.py:124
  92.3 2.2 %collective-permute-done.9 = f32[4,128,512]{2,1,0:T(8,128)S(1)} collective-permute-done((f32[4,128,512]{2,1,0:T(8,128)S(1)}, f32[4,128,512]{2,1,0:T(8,128)S(1)}, u32[]{:S(2)}, u32[]{:S(2)}) %collective-permute-start.9) | collective-permute-done | bytes 1048608 | tf_op jit(solution)/shard_map/ppermute | solution.py:124
  94.8 4.1 %collective-permute-start.10 = (f32[128,512]{1,0:T(8,128)S(1)}, f32[128,512]{1,0:T(8,128)S(1)}, u32[]{:S(2)}, u32[]{:S(2)}) collective-permute-start(f32[128,512]{1,0:T(8,128)S(1)} %get-tuple-element.46), channel_id=1, source_target_pairs={{0,2},{1,3},{2,4},{3,5},{4,6},{5,7},{6,0},{7,1},{8,10},{9,11},{10,... | collective-permute-start | bytes 786440 | tf_op jit(solution)/shard_map/ppermute | solution.py:129
  98.9 2.6 %collective-permute-start.11 = (f32[128,512]{1,0:T(8,128)S(1)}, f32[128,512]{1,0:T(8,128)S(1)}, u32[]{:S(2)}, u32[]{:S(2)}) collective-permute-start(f32[128,512]{1,0:T(8,128)S(1)} %get-tuple-element.48), channel_id=1, source_target_pairs={{0,4},{1,5},{2,6},{3,7},{4,0},{5,1},{6,2},{7,3},{8,12},{9,13},{10,... | collective-permute-start | bytes 786440 | tf_op jit(solution)/shard_map/ppermute | solution.py:129
  101.6 4.0 %collective-permute-start.12 = (f32[128,512]{1,0:T(8,128)S(1)}, f32[128,512]{1,0:T(8,128)S(1)}, u32[]{:S(2)}, u32[]{:S(2)}) collective-permute-start(f32[128,512]{1,0:T(8,128)S(1)} %get-tuple-element.47), channel_id=1, source_target_pairs={{0,6},{1,7},{2,0},{3,1},{4,2},{5,3},{6,4},{7,5},{8,14},{9,15},{10,... | collective-permute-start | bytes 786440 | tf_op jit(solution)/shard_map/ppermute | solution.py:129
  105.8 3.8 %collective-permute-done.11 = f32[128,512]{1,0:T(8,128)S(1)} collective-permute-done((f32[128,512]{1,0:T(8,128)S(1)}, f32[128,512]{1,0:T(8,128)S(1)}, u32[]{:S(2)}, u32[]{:S(2)}) %collective-permute-start.11) | collective-permute-done | bytes 262176 | tf_op jit(solution)/shard_map/ppermute | solution.py:129
  109.6 6.6 %collective-permute-done.12 = f32[128,512]{1,0:T(8,128)S(1)} collective-permute-done((f32[128,512]{1,0:T(8,128)S(1)}, f32[128,512]{1,0:T(8,128)S(1)}, u32[]{:S(2)}, u32[]{:S(2)}) %collective-permute-start.12) | collective-permute-done | bytes 262176 | tf_op jit(solution)/shard_map/ppermute | solution.py:129
  (114 shorter events, 8.9 us)
Async XLA Ops:
  0.0 105.5 %copy-start = (bf16[16,512]{1,0:T(8,128)(2,1)S(1)}, bf16[16,512]{1,0:T(8,128)(2,1)}, u32[]{:S(2)}) copy-start(bf16[16,512]{1,0:T(8,128)(2,1)} %param.15) | copy-start | bytes 49156
  2.3 11.2 %copy-start.2 = (bf16[128,512]{0,1:T(8,128)(2,1)}, bf16[128,512]{0,1:T(8,128)(2,1)S(1)}, u32[]{:S(2)}) copy-start(bf16[128,512]{0,1:T(8,128)(2,1)S(1)} %copy.30) | copy-start | bytes 393220
  3.3 10.2 %copy-start.3 = (bf16[1,128,4,128]{3,2,1,0:T(4,128)(2,1)}, bf16[1,128,4,128]{3,2,1,0:T(4,128)(2,1)S(1)}, u32[]{:S(2)}) copy-start(bf16[1,128,4,128]{3,2,1,0:T(4,128)(2,1)S(1)} %reshape.189) | copy-start | bytes 393220
  3.9 9.5 %collective-permute-start = (f32[520,128]{1,0:T(8,128)S(1)}, f32[520,128]{1,0:T(8,128)S(1)}, u32[]{:S(2)}, u32[]{:S(2)}) collective-permute-start(f32[520,128]{1,0:T(8,128)S(1)} %maximum_maximum_fusion), channel_id=1, source_target_pairs={{0,8},{16,24},{32,40},{48,56},{64,72},{80,88},{96,104},{112,120},{... | collective-permute-start | bytes 798728 | tf_op jit(solution)/shard_map/ppermute | solution.py:92
  13.7 5.7 %collective-permute-start.1 = (f32[520,128]{1,0:T(8,128)S(1)}, f32[520,128]{1,0:T(8,128)S(1)}, u32[]{:S(2)}, u32[]{:S(2)}) collective-permute-start(f32[520,128]{1,0:T(8,128)S(1)} %maximum_select_fusion), channel_id=1, source_target_pairs={{8,24},{40,56},{72,88},{104,120},{112,96},{80,64},{48,32},{16,0},{... | collective-permute-start | bytes 798728 | tf_op jit(solution)/shard_map/ppermute | solution.py:92
  19.6 0.7 collective-permute-start.2
  20.6 0.7 collective-permute-start.3
  21.6 34.5 %collective-permute-start.4 = (f32[520,128]{1,0:T(8,128)S(1)}, f32[520,128]{1,0:T(8,128)}, u32[]{:S(2)}, u32[]{:S(2)}) collective-permute-start(f32[520,128]{1,0:T(8,128)S(1)} %maximum_select_fusion.3), channel_id=1, source_target_pairs={{24,40},{56,72},{88,104},{96,80},{64,48},{32,16},{152,168},{184,20... | collective-permute-start | bytes 798728 | tf_op jit(solution)/shard_map/ppermute | solution.py:92
  57.2 12.8 %copy-start.6 = (f32[128,4]{0,1:T(4,128)S(1)}, f32[128,4]{0,1:T(4,128)}, u32[]{:S(2)}) copy-start(f32[128,4]{0,1:T(4,128)} %param.11) | copy-start | bytes 6148
  58.0 7.4 %collective-permute-start.5 = (f32[520,128]{1,0:T(8,128)}, f32[520,128]{1,0:T(8,128)S(1)}, u32[]{:S(2)}, u32[]{:S(2)}) collective-permute-start(f32[520,128]{1,0:T(8,128)} %maximum_select_fusion.4), channel_id=1, source_target_pairs={{8,16},{24,32},{40,48},{56,64},{72,80},{88,96},{104,112},{112,104}... | collective-permute-start | bytes 798728 | tf_op jit(solution)/shard_map/ppermute | solution.py:92
  60.9 17.7 %copy-start.4 = (bf16[128,512]{1,0:T(8,128)(2,1)S(1)}, bf16[128,512]{1,0:T(8,128)(2,1)}, u32[]{:S(2)}) copy-start(bf16[128,512]{1,0:T(8,128)(2,1)} %param.8) | copy-start | bytes 393220
  63.0 6.6 %copy-start.5 = (f32[4,128,128]{1,2,0:T(8,128)S(1)}, f32[4,128,128]{1,2,0:T(8,128)}, u32[]{:S(2)}) copy-start(f32[4,128,128]{1,2,0:T(8,128)} %fusion.6) | copy-start | bytes 786436
  65.4 13.6 %copy-start.7 = (f32[512]{0:T(512)S(1)}, f32[512]{0:T(512)}, u32[]{:S(2)}) copy-start(f32[512]{0:T(512)} %param.12) | copy-start | bytes 6148
  65.8 7.5 %collective-permute-start.7 = (f32[520,128]{1,0:T(8,128)S(1)}, f32[520,128]{1,0:T(8,128)S(1)}, u32[]{:S(2)}, u32[]{:S(2)}) collective-permute-start(f32[520,128]{1,0:T(8,128)S(1)} %pad_maximum_fusion.1), channel_id=1, source_target_pairs={{0,256},{8,264},{16,272},{24,280},{32,288},{40,296},{48,304},{56,3... | collective-permute-start | bytes 798728 | tf_op jit(solution)/shard_map/ppermute | solution.py:104
  70.3 8.8 %copy-start.1 = (bf16[512,4096]{1,0:T(8,128)(2,1)S(1)}, bf16[512,4096]{1,0:T(8,128)(2,1)}, u32[]{:S(2)}) copy-start(bf16[512,4096]{1,0:T(8,128)(2,1)} %param.13) | copy-start | bytes 12582916
  70.3 8.2 %collective-permute-start.8 = (f32[520,128]{1,0:T(8,128)S(1)}, f32[520,128]{1,0:T(8,128)S(1)}, u32[]{:S(2)}, u32[]{:S(2)}) collective-permute-start(f32[520,128]{1,0:T(8,128)S(1)} %pad_maximum_fusion.1), channel_id=1, source_target_pairs={{0,384},{8,392},{16,400},{24,408},{32,416},{40,424},{48,432},{56,4... | collective-permute-start | bytes 798728 | tf_op jit(solution)/shard_map/ppermute | solution.py:104
  71.2 7.3 %collective-permute-start.6 = (f32[520,128]{1,0:T(8,128)S(1)}, f32[520,128]{1,0:T(8,128)S(1)}, u32[]{:S(2)}, u32[]{:S(2)}) collective-permute-start(f32[520,128]{1,0:T(8,128)S(1)} %pad_maximum_fusion.1), channel_id=1, source_target_pairs={{0,128},{8,136},{16,144},{24,152},{32,160},{40,168},{48,176},{56,1... | collective-permute-start | bytes 798728 | tf_op jit(solution)/shard_map/ppermute | solution.py:104
  80.2 25.4 %copy-start.8 = (s32[128]{0:T(128)S(1)}, s32[128]{0:T(128)}, u32[]{:S(2)}) copy-start(s32[128]{0:T(128)} %param.14) | copy-start | bytes 1540
  80.3 14.3 %collective-permute-start.9 = (f32[4,128,512]{2,1,0:T(8,128)S(1)}, f32[4,128,512]{2,1,0:T(8,128)S(1)}, u32[]{:S(2)}, u32[]{:S(2)}) collective-permute-start(f32[4,128,512]{2,1,0:T(8,128)S(1)} %pad_maximum_fusion), channel_id=1, source_target_pairs={{0,1},{1,0},{2,3},{3,2},{4,5},{5,4},{6,7},{7,6},{8,9},{9,8},{10,11... | collective-permute-start | bytes 3145736 | tf_op jit(solution)/shard_map/ppermute | solution.py:124
  94.8 11.0 %collective-permute-start.10 = (f32[128,512]{1,0:T(8,128)S(1)}, f32[128,512]{1,0:T(8,128)S(1)}, u32[]{:S(2)}, u32[]{:S(2)}) collective-permute-start(f32[128,512]{1,0:T(8,128)S(1)} %get-tuple-element.46), channel_id=1, source_target_pairs={{0,2},{1,3},{2,4},{3,5},{4,6},{5,7},{6,0},{7,1},{8,10},{9,11},{10,... | collective-permute-start | bytes 786440 | tf_op jit(solution)/shard_map/ppermute | solution.py:129
  98.9 10.6 %collective-permute-start.11 = (f32[128,512]{1,0:T(8,128)S(1)}, f32[128,512]{1,0:T(8,128)S(1)}, u32[]{:S(2)}, u32[]{:S(2)}) collective-permute-start(f32[128,512]{1,0:T(8,128)S(1)} %get-tuple-element.48), channel_id=1, source_target_pairs={{0,4},{1,5},{2,6},{3,7},{4,0},{5,1},{6,2},{7,3},{8,12},{9,13},{10,... | collective-permute-start | bytes 786440 | tf_op jit(solution)/shard_map/ppermute | solution.py:129
  101.6 14.6 %collective-permute-start.12 = (f32[128,512]{1,0:T(8,128)S(1)}, f32[128,512]{1,0:T(8,128)S(1)}, u32[]{:S(2)}, u32[]{:S(2)}) collective-permute-start(f32[128,512]{1,0:T(8,128)S(1)} %get-tuple-element.47), channel_id=1, source_target_pairs={{0,6},{1,7},{2,0},{3,1},{4,2},{5,3},{6,4},{7,5},{8,14},{9,15},{10,... | collective-permute-start | bytes 786440 | tf_op jit(solution)/shard_map/ppermute | solution.py:129

commit v11 on v10

--- a/solution.py
+++ b/solution.py
@@ -123,7 +123,7 @@
         pairs = [(h, h ^ 1) for h in range(n)]
         mine = keep + lax.ppermute(away, axis, pairs)
         out = lax.dynamic_index_in_dim(mine, chip, 0, False)
-        for shift in range(1, chips):
+        for shift in sorted(range(1, chips), key=lambda s: -min(s, chips - s)):
             send = lax.dynamic_index_in_dim(mine, (chip + shift) % chips, 0, False)
             pairs = [(2 * y + c, 2 * ((y + shift) % chips) + c) for y in range(chips) for c in range(2)]
             out = out + lax.ppermute(send, axis, pairs)

time: 117 us -> 115 us (0.983)
  the two profiles are of different devices: /device:TPU:75 before, /device:TPU:90 now
where the time goes in v11:
time: 115 us; the launch traced here: 114 us
  waiting for transfers between devices  71.7 us (62%)
  starting transfers between devices  27.9 us (24%)
  other arithmetic  5.36 us (5%)
  local copies, waits for them, and re-layouts  4.2 us (4%)
  matrix products  4.14 us (4%)
    ppermute x6, waiting for transfers between devices, exclusive_scan(): got = lax.ppermute(send, axis, full)  54.1 us
    ppermute x6, starting transfers between devices, exclusive_scan(): got = lax.ppermute(send, axis, full)  9.96 us
    ppermute x3, starting transfers between devices, scatter_heads(): out = out + lax.ppermute(send, axis, pairs)  9.15 us
    ppermute x3, waiting for transfers between devices, scatter_heads(): out = out + lax.ppermute(send, axis, pairs)  8.7 us
    ppermute x3, starting transfers between devices, exclusive_scan(): got = lax.ppermute(total, axis, pairs)  6.92 us
    ppermute x3, waiting for transfers between devices, exclusive_scan(): got = lax.ppermute(total, axis, pairs)  6.34 us
    reshape x3, local copies, waits for them, and re-layouts, split(): array.reshape(count, SPAN, heads_here, head_size).transpose(0, 2, 1, 3)  2.97 us
    ppermute x1, waiting for transfers between devices, scatter_heads(): mine = keep + lax.ppermute(away, axis, pairs)  2.55 us
  transfers between devices with their start and end apart: 13, of which 10 were waited for; matrix products, arithmetic and copies ran while one was open for 4% of the time, Pallas kernels for 0%

profile of v11, /device:TPU:90, one launch (start us, length us, event | category | flops | bytes accessed | tf_op | source)
XLA Modules:
  0.0 114.3 jit_solution(3219885004497862432)
XLA Ops:
  0.0 1.0 reduce_window_sum.24
  1.3 1.0 copy.30
  2.3 1.0 reshape.189
  3.9 3.8 %collective-permute-start = (f32[520,128]{1,0:T(8,128)S(1)}, f32[520,128]{1,0:T(8,128)S(1)}, u32[]{:S(2)}, u32[]{:S(2)}) collective-permute-start(f32[520,128]{1,0:T(8,128)S(1)} %maximum_maximum_fusion), channel_id=1, source_target_pairs={{0,8},{16,24},{32,40},{48,56},{64,72},{80,88},{96,104},{112,120},{... | collective-permute-start | bytes 798728 | tf_op jit(solution)/shard_map/ppermute | solution.py:92
  7.7 6.4 %collective-permute-done = f32[520,128]{1,0:T(8,128)S(1)} collective-permute-done((f32[520,128]{1,0:T(8,128)S(1)}, f32[520,128]{1,0:T(8,128)S(1)}, u32[]{:S(2)}, u32[]{:S(2)}) %collective-permute-start) | collective-permute-done | bytes 266272 | tf_op jit(solution)/shard_map/ppermute | solution.py:92
  14.4 1.6 %collective-permute-start.1 = (f32[520,128]{1,0:T(8,128)S(1)}, f32[520,128]{1,0:T(8,128)S(1)}, u32[]{:S(2)}, u32[]{:S(2)}) collective-permute-start(f32[520,128]{1,0:T(8,128)S(1)} %maximum_select_fusion), channel_id=1, source_target_pairs={{8,24},{40,56},{72,88},{104,120},{112,96},{80,64},{48,32},{16,0},{... | collective-permute-start | bytes 798728 | tf_op jit(solution)/shard_map/ppermute | solution.py:92
  16.0 4.9 %collective-permute-done.1 = f32[520,128]{1,0:T(8,128)S(1)} collective-permute-done((f32[520,128]{1,0:T(8,128)S(1)}, f32[520,128]{1,0:T(8,128)S(1)}, u32[]{:S(2)}, u32[]{:S(2)}) %collective-permute-start.1) | collective-permute-done | bytes 266272 | tf_op jit(solution)/shard_map/ppermute | solution.py:92
  23.1 1.3 %collective-permute-start.4 = (f32[520,128]{1,0:T(8,128)S(1)}, f32[520,128]{1,0:T(8,128)}, u32[]{:S(2)}, u32[]{:S(2)}) collective-permute-start(f32[520,128]{1,0:T(8,128)S(1)} %maximum_select_fusion.3), channel_id=1, source_target_pairs={{24,40},{56,72},{88,104},{96,80},{64,48},{32,16},{152,168},{184,20... | collective-permute-start | bytes 798728 | tf_op jit(solution)/shard_map/ppermute | solution.py:92
  24.4 39.3 %collective-permute-done.4 = f32[520,128]{1,0:T(8,128)} collective-permute-done((f32[520,128]{1,0:T(8,128)S(1)}, f32[520,128]{1,0:T(8,128)}, u32[]{:S(2)}, u32[]{:S(2)}) %collective-permute-start.4) | collective-permute-done | bytes 266272 | tf_op jit(solution)/shard_map/ppermute | solution.py:92
  63.8 1.0 broadcast_select_fusion.2
  65.7 1.9 %collective-permute-start.5 = (f32[520,128]{1,0:T(8,128)}, f32[520,128]{1,0:T(8,128)S(1)}, u32[]{:S(2)}, u32[]{:S(2)}) collective-permute-start(f32[520,128]{1,0:T(8,128)} %maximum_select_fusion.4), channel_id=1, source_target_pairs={{8,16},{24,32},{40,48},{56,64},{72,80},{88,96},{104,112},{112,104}... | collective-permute-start | bytes 798728 | tf_op jit(solution)/shard_map/ppermute | solution.py:92
  68.6 2.1 %fusion.6 = f32[4,128,128]{1,2,0:T(8,128)} fusion(bf16[4,128,128]{1,2,0:T(8,128)(2,1)} %bitcast.154, f32[4,128]{1,0:T(4,128)S(1)} %reduce_window_sum.24, pred[128,128]{0,1:T(8,128)(4,1)S(1)} %iota_compare_fusion.1, bf16[1,128,4,128]{3,2,1,0:T(4,128)(2,1)} %copy-done.3, bf16[1,128,4,128]{3,2,1,0:T(4,128)(2,1)S(1)} %reshape.187), kind=kOutput, calls=%fused_computation.10 | convolution fusion | flops 33882112 | bytes 673792 | tf_op jit(solution)/shard_map/while/body/eval_jaxpr/hts,hse->hte/dot_general | solution.py:20
  70.7 3.5 %collective-permute-done.5 = f32[520,128]{1,0:T(8,128)S(1)} collective-permute-done((f32[520,128]{1,0:T(8,128)}, f32[520,128]{1,0:T(8,128)S(1)}, u32[]{:S(2)}, u32[]{:S(2)}) %collective-permute-start.5) | collective-permute-done | bytes 266272 | tf_op jit(solution)/shard_map/ppermute | solution.py:92
  74.6 4.0 %collective-permute-start.7 = (f32[520,128]{1,0:T(8,128)S(1)}, f32[520,128]{1,0:T(8,128)S(1)}, u32[]{:S(2)}, u32[]{:S(2)}) collective-permute-start(f32[520,128]{1,0:T(8,128)S(1)} %pad_maximum_fusion.1), channel_id=1, source_target_pairs={{0,256},{8,264},{16,272},{24,280},{32,288},{40,296},{48,304},{56,3... | collective-permute-start | bytes 798728 | tf_op jit(solution)/shard_map/ppermute | solution.py:104
  80.3 2.1 %collective-permute-start.6 = (f32[520,128]{1,0:T(8,128)S(1)}, f32[520,128]{1,0:T(8,128)S(1)}, u32[]{:S(2)}, u32[]{:S(2)}) collective-permute-start(f32[520,128]{1,0:T(8,128)S(1)} %pad_maximum_fusion.1), channel_id=1, source_target_pairs={{0,128},{8,136},{16,144},{24,152},{32,160},{40,168},{48,176},{56,1... | collective-permute-start | bytes 798728 | tf_op jit(solution)/shard_map/ppermute | solution.py:104
  82.6 6.1 %collective-permute-done.6 = f32[520,128]{1,0:T(8,128)S(1)} collective-permute-done((f32[520,128]{1,0:T(8,128)S(1)}, f32[520,128]{1,0:T(8,128)S(1)}, u32[]{:S(2)}, u32[]{:S(2)}) %collective-permute-start.6) | collective-permute-done | bytes 266272 | tf_op jit(solution)/shard_map/ppermute | solution.py:104
  90.5 1.9 %collective-permute-start.9 = (f32[4,128,512]{2,1,0:T(8,128)S(1)}, f32[4,128,512]{2,1,0:T(8,128)S(1)}, u32[]{:S(2)}, u32[]{:S(2)}) collective-permute-start(f32[4,128,512]{2,1,0:T(8,128)S(1)} %pad_maximum_fusion), channel_id=1, source_target_pairs={{0,1},{1,0},{2,3},{3,2},{4,5},{5,4},{6,7},{7,6},{8,9},{9,8},{10,11... | collective-permute-start | bytes 3145736 | tf_op jit(solution)/shard_map/ppermute | solution.py:124
  92.5 2.6 %collective-permute-done.9 = f32[4,128,512]{2,1,0:T(8,128)S(1)} collective-permute-done((f32[4,128,512]{2,1,0:T(8,128)S(1)}, f32[4,128,512]{2,1,0:T(8,128)S(1)}, u32[]{:S(2)}, u32[]{:S(2)}) %collective-permute-start.9) | collective-permute-done | bytes 1048608 | tf_op jit(solution)/shard_map/ppermute | solution.py:124
  95.4 2.3 %collective-permute-start.10 = (f32[128,512]{1,0:T(8,128)S(1)}, f32[128,512]{1,0:T(8,128)S(1)}, u32[]{:S(2)}, u32[]{:S(2)}) collective-permute-start(f32[128,512]{1,0:T(8,128)S(1)} %get-tuple-element.46), channel_id=1, source_target_pairs={{0,4},{1,5},{2,6},{3,7},{4,0},{5,1},{6,2},{7,3},{8,12},{9,13},{10,... | collective-permute-start | bytes 786440 | tf_op jit(solution)/shard_map/ppermute | solution.py:129
  97.7 5.0 %collective-permute-start.11 = (f32[128,512]{1,0:T(8,128)S(1)}, f32[128,512]{1,0:T(8,128)S(1)}, u32[]{:S(2)}, u32[]{:S(2)}) collective-permute-start(f32[128,512]{1,0:T(8,128)S(1)} %get-tuple-element.48), channel_id=1, source_target_pairs={{0,2},{1,3},{2,4},{3,5},{4,6},{5,7},{6,0},{7,1},{8,10},{9,11},{10,... | collective-permute-start | bytes 786440 | tf_op jit(solution)/shard_map/ppermute | solution.py:129
  102.6 1.9 %collective-permute-start.12 = (f32[128,512]{1,0:T(8,128)S(1)}, f32[128,512]{1,0:T(8,128)S(1)}, u32[]{:S(2)}, u32[]{:S(2)}) collective-permute-start(f32[128,512]{1,0:T(8,128)S(1)} %get-tuple-element.47), channel_id=1, source_target_pairs={{0,6},{1,7},{2,0},{3,1},{4,2},{5,3},{6,4},{7,5},{8,14},{9,15},{10,... | collective-permute-start | bytes 786440 | tf_op jit(solution)/shard_map/ppermute | solution.py:129
  104.8 2.6 %collective-permute-done.10 = f32[128,512]{1,0:T(8,128)S(1)} collective-permute-done((f32[128,512]{1,0:T(8,128)S(1)}, f32[128,512]{1,0:T(8,128)S(1)}, u32[]{:S(2)}, u32[]{:S(2)}) %collective-permute-start.10) | collective-permute-done | bytes 262176 | tf_op jit(solution)/shard_map/ppermute | solution.py:129
  107.5 2.8 %collective-permute-done.11 = f32[128,512]{1,0:T(8,128)S(1)} collective-permute-done((f32[128,512]{1,0:T(8,128)S(1)}, f32[128,512]{1,0:T(8,128)S(1)}, u32[]{:S(2)}, u32[]{:S(2)}) %collective-permute-start.11) | collective-permute-done | bytes 262176 | tf_op jit(solution)/shard_map/ppermute | solution.py:129
  110.3 3.3 %collective-permute-done.12 = f32[128,512]{1,0:T(8,128)S(1)} collective-permute-done((f32[128,512]{1,0:T(8,128)S(1)}, f32[128,512]{1,0:T(8,128)S(1)}, u32[]{:S(2)}, u32[]{:S(2)}) %collective-permute-start.12) | collective-permute-done | bytes 262176 | tf_op jit(solution)/shard_map/ppermute | solution.py:129
  (114 shorter events, 10.0 us)
Async XLA Ops:
  0.0 104.6 %copy-start = (bf16[16,512]{1,0:T(8,128)(2,1)S(1)}, bf16[16,512]{1,0:T(8,128)(2,1)}, u32[]{:S(2)}) copy-start(bf16[16,512]{1,0:T(8,128)(2,1)} %param.15) | copy-start | bytes 49156
  2.3 11.8 %copy-start.2 = (bf16[128,512]{0,1:T(8,128)(2,1)}, bf16[128,512]{0,1:T(8,128)(2,1)S(1)}, u32[]{:S(2)}) copy-start(bf16[128,512]{0,1:T(8,128)(2,1)S(1)} %copy.30) | copy-start | bytes 393220
  3.3 10.8 %copy-start.3 = (bf16[1,128,4,128]{3,2,1,0:T(4,128)(2,1)}, bf16[1,128,4,128]{3,2,1,0:T(4,128)(2,1)S(1)}, u32[]{:S(2)}) copy-start(bf16[1,128,4,128]{3,2,1,0:T(4,128)(2,1)S(1)} %reshape.189) | copy-start | bytes 393220
  3.9 10.2 %collective-permute-start = (f32[520,128]{1,0:T(8,128)S(1)}, f32[520,128]{1,0:T(8,128)S(1)}, u32[]{:S(2)}, u32[]{:S(2)}) collective-permute-start(f32[520,128]{1,0:T(8,128)S(1)} %maximum_maximum_fusion), channel_id=1, source_target_pairs={{0,8},{16,24},{32,40},{48,56},{64,72},{80,88},{96,104},{112,120},{... | collective-permute-start | bytes 798728 | tf_op jit(solution)/shard_map/ppermute | solution.py:92
  14.4 6.5 %collective-permute-start.1 = (f32[520,128]{1,0:T(8,128)S(1)}, f32[520,128]{1,0:T(8,128)S(1)}, u32[]{:S(2)}, u32[]{:S(2)}) collective-permute-start(f32[520,128]{1,0:T(8,128)S(1)} %maximum_select_fusion), channel_id=1, source_target_pairs={{8,24},{40,56},{72,88},{104,120},{112,96},{80,64},{48,32},{16,0},{... | collective-permute-start | bytes 798728 | tf_op jit(solution)/shard_map/ppermute | solution.py:92
  21.2 0.7 collective-permute-start.2
  22.1 0.7 collective-permute-start.3
  23.1 40.6 %collective-permute-start.4 = (f32[520,128]{1,0:T(8,128)S(1)}, f32[520,128]{1,0:T(8,128)}, u32[]{:S(2)}, u32[]{:S(2)}) collective-permute-start(f32[520,128]{1,0:T(8,128)S(1)} %maximum_select_fusion.3), channel_id=1, source_target_pairs={{24,40},{56,72},{88,104},{96,80},{64,48},{32,16},{152,168},{184,20... | collective-permute-start | bytes 798728 | tf_op jit(solution)/shard_map/ppermute | solution.py:92
  64.9 14.2 %copy-start.6 = (f32[128,4]{0,1:T(4,128)S(1)}, f32[128,4]{0,1:T(4,128)}, u32[]{:S(2)}) copy-start(f32[128,4]{0,1:T(4,128)} %param.11) | copy-start | bytes 6148
  65.7 8.5 %collective-permute-start.5 = (f32[520,128]{1,0:T(8,128)}, f32[520,128]{1,0:T(8,128)S(1)}, u32[]{:S(2)}, u32[]{:S(2)}) collective-permute-start(f32[520,128]{1,0:T(8,128)} %maximum_select_fusion.4), channel_id=1, source_target_pairs={{8,16},{24,32},{40,48},{56,64},{72,80},{88,96},{104,112},{112,104}... | collective-permute-start | bytes 798728 | tf_op jit(solution)/shard_map/ppermute | solution.py:92
  68.6 20.3 %copy-start.4 = (bf16[128,512]{1,0:T(8,128)(2,1)S(1)}, bf16[128,512]{1,0:T(8,128)(2,1)}, u32[]{:S(2)}) copy-start(bf16[128,512]{1,0:T(8,128)(2,1)} %param.8) | copy-start | bytes 393220
  70.7 8.0 %copy-start.5 = (f32[4,128,128]{1,2,0:T(8,128)S(1)}, f32[4,128,128]{1,2,0:T(8,128)}, u32[]{:S(2)}) copy-start(f32[4,128,128]{1,2,0:T(8,128)} %fusion.6) | copy-start | bytes 786436
  74.3 15.0 %copy-start.7 = (f32[512]{0:T(512)S(1)}, f32[512]{0:T(512)}, u32[]{:S(2)}) copy-start(f32[512]{0:T(512)} %param.12) | copy-start | bytes 6148
  74.6 8.0 %collective-permute-start.7 = (f32[520,128]{1,0:T(8,128)S(1)}, f32[520,128]{1,0:T(8,128)S(1)}, u32[]{:S(2)}, u32[]{:S(2)}) collective-permute-start(f32[520,128]{1,0:T(8,128)S(1)} %pad_maximum_fusion.1), channel_id=1, source_target_pairs={{0,256},{8,264},{16,272},{24,280},{32,288},{40,296},{48,304},{56,3... | collective-permute-start | bytes 798728 | tf_op jit(solution)/shard_map/ppermute | solution.py:104
  79.5 10.0 %copy-start.1 = (bf16[512,4096]{1,0:T(8,128)(2,1)S(1)}, bf16[512,4096]{1,0:T(8,128)(2,1)}, u32[]{:S(2)}) copy-start(bf16[512,4096]{1,0:T(8,128)(2,1)} %param.13) | copy-start | bytes 12582916
  79.5 9.3 %collective-permute-start.8 = (f32[520,128]{1,0:T(8,128)S(1)}, f32[520,128]{1,0:T(8,128)S(1)}, u32[]{:S(2)}, u32[]{:S(2)}) collective-permute-start(f32[520,128]{1,0:T(8,128)S(1)} %pad_maximum_fusion.1), channel_id=1, source_target_pairs={{0,384},{8,392},{16,400},{24,408},{32,416},{40,424},{48,432},{56,4... | collective-permute-start | bytes 798728 | tf_op jit(solution)/shard_map/ppermute | solution.py:104
  80.3 8.4 %collective-permute-start.6 = (f32[520,128]{1,0:T(8,128)S(1)}, f32[520,128]{1,0:T(8,128)S(1)}, u32[]{:S(2)}, u32[]{:S(2)}) collective-permute-start(f32[520,128]{1,0:T(8,128)S(1)} %pad_maximum_fusion.1), channel_id=1, source_target_pairs={{0,128},{8,136},{16,144},{24,152},{32,160},{40,168},{48,176},{56,1... | collective-permute-start | bytes 798728 | tf_op jit(solution)/shard_map/ppermute | solution.py:104
  90.4 14.1 %copy-start.8 = (s32[128]{0:T(128)S(1)}, s32[128]{0:T(128)}, u32[]{:S(2)}) copy-start(s32[128]{0:T(128)} %param.14) | copy-start | bytes 1540
  90.5 4.6 %collective-permute-start.9 = (f32[4,128,512]{2,1,0:T(8,128)S(1)}, f32[4,128,512]{2,1,0:T(8,128)S(1)}, u32[]{:S(2)}, u32[]{:S(2)}) collective-permute-start(f32[4,128,512]{2,1,0:T(8,128)S(1)} %pad_maximum_fusion), channel_id=1, source_target_pairs={{0,1},{1,0},{2,3},{3,2},{4,5},{5,4},{6,7},{7,6},{8,9},{9,8},{10,11... | collective-permute-start | bytes 3145736 | tf_op jit(solution)/shard_map/ppermute | solution.py:124
  95.4 12.1 %collective-permute-start.10 = (f32[128,512]{1,0:T(8,128)S(1)}, f32[128,512]{1,0:T(8,128)S(1)}, u32[]{:S(2)}, u32[]{:S(2)}) collective-permute-start(f32[128,512]{1,0:T(8,128)S(1)} %get-tuple-element.46), channel_id=1, source_target_pairs={{0,4},{1,5},{2,6},{3,7},{4,0},{5,1},{6,2},{7,3},{8,12},{9,13},{10,... | collective-permute-start | bytes 786440 | tf_op jit(solution)/shard_map/ppermute | solution.py:129
  97.7 12.6 %collective-permute-start.11 = (f32[128,512]{1,0:T(8,128)S(1)}, f32[128,512]{1,0:T(8,128)S(1)}, u32[]{:S(2)}, u32[]{:S(2)}) collective-permute-start(f32[128,512]{1,0:T(8,128)S(1)} %get-tuple-element.48), channel_id=1, source_target_pairs={{0,2},{1,3},{2,4},{3,5},{4,6},{5,7},{6,0},{7,1},{8,10},{9,11},{10,... | collective-permute-start | bytes 786440 | tf_op jit(solution)/shard_map/ppermute | solution.py:129
  102.6 10.9 %collective-permute-start.12 = (f32[128,512]{1,0:T(8,128)S(1)}, f32[128,512]{1,0:T(8,128)S(1)}, u32[]{:S(2)}, u32[]{:S(2)}) collective-permute-start(f32[128,512]{1,0:T(8,128)S(1)} %get-tuple-element.47), channel_id=1, source_target_pairs={{0,6},{1,7},{2,0},{3,1},{4,2},{5,3},{6,4},{7,5},{8,14},{9,15},{10,... | collective-permute-start | bytes 786440 | tf_op jit(solution)/shard_map/ppermute | solution.py:129

commit v12 on v11

--- a/solution.py
+++ b/solution.py
@@ -123,7 +123,7 @@
         pairs = [(h, h ^ 1) for h in range(n)]
         mine = keep + lax.ppermute(away, axis, pairs)
         out = lax.dynamic_index_in_dim(mine, chip, 0, False)
-        for shift in sorted(range(1, chips), key=lambda s: -min(s, chips - s)):
+        for shift in sorted(range(1, chips), key=lambda s: (-min(s, chips - s), -s)):
             send = lax.dynamic_index_in_dim(mine, (chip + shift) % chips, 0, False)
             pairs = [(2 * y + c, 2 * ((y + shift) % chips) + c) for y in range(chips) for c in range(2)]
             out = out + lax.ppermute(send, axis, pairs)

time: 115 us -> 115 us (level)
  the two profiles are of different devices: /device:TPU:90 before, /device:TPU:66 now
where the time goes in v12:
time: 115 us; the launch traced here: 114 us
  waiting for transfers between devices  69.1 us (60%)
  starting transfers between devices  30.6 us (27%)
  other arithmetic  5.36 us (5%)
  local copies, waits for them, and re-layouts  4.2 us (4%)
  matrix products  4.15 us (4%)
    ppermute x6, waiting for transfers between devices, exclusive_scan(): got = lax.ppermute(send, axis, full)  53.2 us
    ppermute x3, starting transfers between devices, scatter_heads(): out = out + lax.ppermute(send, axis, pairs)  11.8 us
    ppermute x6, starting transfers between devices, exclusive_scan(): got = lax.ppermute(send, axis, full)  9.96 us
    ppermute x3, waiting for transfers between devices, scatter_heads(): out = out + lax.ppermute(send, axis, pairs)  6.98 us
    ppermute x3, starting transfers between devices, exclusive_scan(): got = lax.ppermute(total, axis, pairs)  6.92 us
    ppermute x3, waiting for transfers between devices, exclusive_scan(): got = lax.ppermute(total, axis, pairs)  6.34 us
    reshape x3, local copies, waits for them, and re-layouts, split(): array.reshape(count, SPAN, heads_here, head_size).transpose(0, 2, 1, 3)  2.97 us
    ppermute x1, waiting for transfers between devices, scatter_heads(): mine = keep + lax.ppermute(away, axis, pairs)  2.55 us
  transfers between devices with their start and end apart: 13, of which 10 were waited for; matrix products, arithmetic and copies ran while one was open for 4% of the time, Pallas kernels for 0%

profile of v12, /device:TPU:66, one launch (start us, length us, event | category | flops | bytes accessed | tf_op | source)
XLA Modules:
  0.0 114.4 jit_solution(14464532369646747330)
XLA Ops:
  0.0 1.0 reduce_window_sum.24
  1.3 1.0 copy.30
  2.3 1.0 reshape.189
  3.9 3.8 %collective-permute-start = (f32[520,128]{1,0:T(8,128)S(1)}, f32[520,128]{1,0:T(8,128)S(1)}, u32[]{:S(2)}, u32[]{:S(2)}) collective-permute-start(f32[520,128]{1,0:T(8,128)S(1)} %maximum_maximum_fusion), channel_id=1, source_target_pairs={{0,8},{16,24},{32,40},{48,56},{64,72},{80,88},{96,104},{112,120},{... | collective-permute-start | bytes 798728 | tf_op jit(solution)/shard_map/ppermute | solution.py:92
  7.7 6.4 %collective-permute-done = f32[520,128]{1,0:T(8,128)S(1)} collective-permute-done((f32[520,128]{1,0:T(8,128)S(1)}, f32[520,128]{1,0:T(8,128)S(1)}, u32[]{:S(2)}, u32[]{:S(2)}) %collective-permute-start) | collective-permute-done | bytes 266272 | tf_op jit(solution)/shard_map/ppermute | solution.py:92
  14.4 1.6 %collective-permute-start.1 = (f32[520,128]{1,0:T(8,128)S(1)}, f32[520,128]{1,0:T(8,128)S(1)}, u32[]{:S(2)}, u32[]{:S(2)}) collective-permute-start(f32[520,128]{1,0:T(8,128)S(1)} %maximum_select_fusion), channel_id=1, source_target_pairs={{8,24},{40,56},{72,88},{104,120},{112,96},{80,64},{48,32},{16,0},{... | collective-permute-start | bytes 798728 | tf_op jit(solution)/shard_map/ppermute | solution.py:92
  16.0 4.9 %collective-permute-done.1 = f32[520,128]{1,0:T(8,128)S(1)} collective-permute-done((f32[520,128]{1,0:T(8,128)S(1)}, f32[520,128]{1,0:T(8,128)S(1)}, u32[]{:S(2)}, u32[]{:S(2)}) %collective-permute-start.1) | collective-permute-done | bytes 266272 | tf_op jit(solution)/shard_map/ppermute | solution.py:92
  23.1 1.3 %collective-permute-start.4 = (f32[520,128]{1,0:T(8,128)S(1)}, f32[520,128]{1,0:T(8,128)}, u32[]{:S(2)}, u32[]{:S(2)}) collective-permute-start(f32[520,128]{1,0:T(8,128)S(1)} %maximum_select_fusion.3), channel_id=1, source_target_pairs={{24,40},{56,72},{88,104},{96,80},{64,48},{32,16},{152,168},{184,20... | collective-permute-start | bytes 798728 | tf_op jit(solution)/shard_map/ppermute | solution.py:92
  24.4 38.4 %collective-permute-done.4 = f32[520,128]{1,0:T(8,128)} collective-permute-done((f32[520,128]{1,0:T(8,128)S(1)}, f32[520,128]{1,0:T(8,128)}, u32[]{:S(2)}, u32[]{:S(2)}) %collective-permute-start.4) | collective-permute-done | bytes 266272 | tf_op jit(solution)/shard_map/ppermute | solution.py:92
  62.9 1.0 broadcast_select_fusion.2
  64.8 1.9 %collective-permute-start.5 = (f32[520,128]{1,0:T(8,128)}, f32[520,128]{1,0:T(8,128)S(1)}, u32[]{:S(2)}, u32[]{:S(2)}) collective-permute-start(f32[520,128]{1,0:T(8,128)} %maximum_select_fusion.4), channel_id=1, source_target_pairs={{8,16},{24,32},{40,48},{56,64},{72,80},{88,96},{104,112},{112,104}... | collective-permute-start | bytes 798728 | tf_op jit(solution)/shard_map/ppermute | solution.py:92
  66.7 0.9 reshape.187
  67.7 2.1 %fusion.6 = f32[4,128,128]{1,2,0:T(8,128)} fusion(bf16[4,128,128]{1,2,0:T(8,128)(2,1)} %bitcast.154, f32[4,128]{1,0:T(4,128)S(1)} %reduce_window_sum.24, pred[128,128]{0,1:T(8,128)(4,1)S(1)} %iota_compare_fusion.1, bf16[1,128,4,128]{3,2,1,0:T(4,128)(2,1)} %copy-done.3, bf16[1,128,4,128]{3,2,1,0:T(4,128)(2,1)S(1)} %reshape.187), kind=kOutput, calls=%fused_computation.10 | convolution fusion | flops 33882112 | bytes 673792 | tf_op jit(solution)/shard_map/while/body/eval_jaxpr/hts,hse->hte/dot_general | solution.py:20
  69.8 3.5 %collective-permute-done.5 = f32[520,128]{1,0:T(8,128)S(1)} collective-permute-done((f32[520,128]{1,0:T(8,128)}, f32[520,128]{1,0:T(8,128)S(1)}, u32[]{:S(2)}, u32[]{:S(2)}) %collective-permute-start.5) | collective-permute-done | bytes 266272 | tf_op jit(solution)/shard_map/ppermute | solution.py:92
  73.7 4.0 %collective-permute-start.7 = (f32[520,128]{1,0:T(8,128)S(1)}, f32[520,128]{1,0:T(8,128)S(1)}, u32[]{:S(2)}, u32[]{:S(2)}) collective-permute-start(f32[520,128]{1,0:T(8,128)S(1)} %pad_maximum_fusion.1), channel_id=1, source_target_pairs={{0,256},{8,264},{16,272},{24,280},{32,288},{40,296},{48,304},{56,3... | collective-permute-start | bytes 798728 | tf_op jit(solution)/shard_map/ppermute | solution.py:104
  78.6 0.8 collective-permute-start.8
  79.4 2.1 %collective-permute-start.6 = (f32[520,128]{1,0:T(8,128)S(1)}, f32[520,128]{1,0:T(8,128)S(1)}, u32[]{:S(2)}, u32[]{:S(2)}) collective-permute-start(f32[520,128]{1,0:T(8,128)S(1)} %pad_maximum_fusion.1), channel_id=1, source_target_pairs={{0,128},{8,136},{16,144},{24,152},{32,160},{40,168},{48,176},{56,1... | collective-permute-start | bytes 798728 | tf_op jit(solution)/shard_map/ppermute | solution.py:104
  81.7 6.1 %collective-permute-done.6 = f32[520,128]{1,0:T(8,128)S(1)} collective-permute-done((f32[520,128]{1,0:T(8,128)S(1)}, f32[520,128]{1,0:T(8,128)S(1)}, u32[]{:S(2)}, u32[]{:S(2)}) %collective-permute-start.6) | collective-permute-done | bytes 266272 | tf_op jit(solution)/shard_map/ppermute | solution.py:104
  89.6 1.9 %collective-permute-start.9 = (f32[4,128,512]{2,1,0:T(8,128)S(1)}, f32[4,128,512]{2,1,0:T(8,128)S(1)}, u32[]{:S(2)}, u32[]{:S(2)}) collective-permute-start(f32[4,128,512]{2,1,0:T(8,128)S(1)} %pad_maximum_fusion), channel_id=1, source_target_pairs={{0,1},{1,0},{2,3},{3,2},{4,5},{5,4},{6,7},{7,6},{8,9},{9,8},{10,11... | collective-permute-start | bytes 3145736 | tf_op jit(solution)/shard_map/ppermute | solution.py:124
  91.7 2.6 %collective-permute-done.9 = f32[4,128,512]{2,1,0:T(8,128)S(1)} collective-permute-done((f32[4,128,512]{2,1,0:T(8,128)S(1)}, f32[4,128,512]{2,1,0:T(8,128)S(1)}, u32[]{:S(2)}, u32[]{:S(2)}) %collective-permute-start.9) | collective-permute-done | bytes 1048608 | tf_op jit(solution)/shard_map/ppermute | solution.py:124
  94.5 6.0 %collective-permute-start.10 = (f32[128,512]{1,0:T(8,128)S(1)}, f32[128,512]{1,0:T(8,128)S(1)}, u32[]{:S(2)}, u32[]{:S(2)}) collective-permute-start(f32[128,512]{1,0:T(8,128)S(1)} %get-tuple-element.46), channel_id=1, source_target_pairs={{0,4},{1,5},{2,6},{3,7},{4,0},{5,1},{6,2},{7,3},{8,12},{9,13},{10,... | collective-permute-start | bytes 786440 | tf_op jit(solution)/shard_map/ppermute | solution.py:129
  100.5 2.1 %collective-permute-start.11 = (f32[128,512]{1,0:T(8,128)S(1)}, f32[128,512]{1,0:T(8,128)S(1)}, u32[]{:S(2)}, u32[]{:S(2)}) collective-permute-start(f32[128,512]{1,0:T(8,128)S(1)} %get-tuple-element.48), channel_id=1, source_target_pairs={{0,6},{1,7},{2,0},{3,1},{4,2},{5,3},{6,4},{7,5},{8,14},{9,15},{10,... | collective-permute-start | bytes 786440 | tf_op jit(solution)/shard_map/ppermute | solution.py:129
  102.6 3.8 %collective-permute-start.12 = (f32[128,512]{1,0:T(8,128)S(1)}, f32[128,512]{1,0:T(8,128)S(1)}, u32[]{:S(2)}, u32[]{:S(2)}) collective-permute-start(f32[128,512]{1,0:T(8,128)S(1)} %get-tuple-element.47), channel_id=1, source_target_pairs={{0,2},{1,3},{2,4},{3,5},{4,6},{5,7},{6,0},{7,1},{8,10},{9,11},{10,... | collective-permute-start | bytes 786440 | tf_op jit(solution)/shard_map/ppermute | solution.py:129
  107.1 6.0 %collective-permute-done.11 = f32[128,512]{1,0:T(8,128)S(1)} collective-permute-done((f32[128,512]{1,0:T(8,128)S(1)}, f32[128,512]{1,0:T(8,128)S(1)}, u32[]{:S(2)}, u32[]{:S(2)}) %collective-permute-start.11) | collective-permute-done | bytes 262176 | tf_op jit(solution)/shard_map/ppermute | solution.py:129
  (114 shorter events, 9.2 us)
Async XLA Ops:
  0.0 106.4 %copy-start = (bf16[16,512]{1,0:T(8,128)(2,1)S(1)}, bf16[16,512]{1,0:T(8,128)(2,1)}, u32[]{:S(2)}) copy-start(bf16[16,512]{1,0:T(8,128)(2,1)} %param.15) | copy-start | bytes 49156
  2.3 11.8 %copy-start.2 = (bf16[128,512]{0,1:T(8,128)(2,1)}, bf16[128,512]{0,1:T(8,128)(2,1)S(1)}, u32[]{:S(2)}) copy-start(bf16[128,512]{0,1:T(8,128)(2,1)S(1)} %copy.30) | copy-start | bytes 393220
  3.3 10.8 %copy-start.3 = (bf16[1,128,4,128]{3,2,1,0:T(4,128)(2,1)}, bf16[1,128,4,128]{3,2,1,0:T(4,128)(2,1)S(1)}, u32[]{:S(2)}) copy-start(bf16[1,128,4,128]{3,2,1,0:T(4,128)(2,1)S(1)} %reshape.189) | copy-start | bytes 393220
  3.9 10.2 %collective-permute-start = (f32[520,128]{1,0:T(8,128)S(1)}, f32[520,128]{1,0:T(8,128)S(1)}, u32[]{:S(2)}, u32[]{:S(2)}) collective-permute-start(f32[520,128]{1,0:T(8,128)S(1)} %maximum_maximum_fusion), channel_id=1, source_target_pairs={{0,8},{16,24},{32,40},{48,56},{64,72},{80,88},{96,104},{112,120},{... | collective-permute-start | bytes 798728 | tf_op jit(solution)/shard_map/ppermute | solution.py:92
  14.4 6.5 %collective-permute-start.1 = (f32[520,128]{1,0:T(8,128)S(1)}, f32[520,128]{1,0:T(8,128)S(1)}, u32[]{:S(2)}, u32[]{:S(2)}) collective-permute-start(f32[520,128]{1,0:T(8,128)S(1)} %maximum_select_fusion), channel_id=1, source_target_pairs={{8,24},{40,56},{72,88},{104,120},{112,96},{80,64},{48,32},{16,0},{... | collective-permute-start | bytes 798728 | tf_op jit(solution)/shard_map/ppermute | solution.py:92
  21.2 0.7 collective-permute-start.2
  22.1 0.7 collective-permute-start.3
  23.1 39.8 %collective-permute-start.4 = (f32[520,128]{1,0:T(8,128)S(1)}, f32[520,128]{1,0:T(8,128)}, u32[]{:S(2)}, u32[]{:S(2)}) collective-permute-start(f32[520,128]{1,0:T(8,128)S(1)} %maximum_select_fusion.3), channel_id=1, source_target_pairs={{24,40},{56,72},{88,104},{96,80},{64,48},{32,16},{152,168},{184,20... | collective-permute-start | bytes 798728 | tf_op jit(solution)/shard_map/ppermute | solution.py:92
  64.0 14.2 %copy-start.6 = (f32[128,4]{0,1:T(4,128)S(1)}, f32[128,4]{0,1:T(4,128)}, u32[]{:S(2)}) copy-start(f32[128,4]{0,1:T(4,128)} %param.11) | copy-start | bytes 6148
  64.8 8.5 %collective-permute-start.5 = (f32[520,128]{1,0:T(8,128)}, f32[520,128]{1,0:T(8,128)S(1)}, u32[]{:S(2)}, u32[]{:S(2)}) collective-permute-start(f32[520,128]{1,0:T(8,128)} %maximum_select_fusion.4), channel_id=1, source_target_pairs={{8,16},{24,32},{40,48},{56,64},{72,80},{88,96},{104,112},{112,104}... | collective-permute-start | bytes 798728 | tf_op jit(solution)/shard_map/ppermute | solution.py:92
  67.7 20.3 %copy-start.4 = (bf16[128,512]{1,0:T(8,128)(2,1)S(1)}, bf16[128,512]{1,0:T(8,128)(2,1)}, u32[]{:S(2)}) copy-start(bf16[128,512]{1,0:T(8,128)(2,1)} %param.8) | copy-start | bytes 393220
  69.8 8.0 %copy-start.5 = (f32[4,128,128]{1,2,0:T(8,128)S(1)}, f32[4,128,128]{1,2,0:T(8,128)}, u32[]{:S(2)}) copy-start(f32[4,128,128]{1,2,0:T(8,128)} %fusion.6) | copy-start | bytes 786436
  73.4 15.0 %copy-start.7 = (f32[512]{0:T(512)S(1)}, f32[512]{0:T(512)}, u32[]{:S(2)}) copy-start(f32[512]{0:T(512)} %param.12) | copy-start | bytes 6148
  73.7 8.0 %collective-permute-start.7 = (f32[520,128]{1,0:T(8,128)S(1)}, f32[520,128]{1,0:T(8,128)S(1)}, u32[]{:S(2)}, u32[]{:S(2)}) collective-permute-start(f32[520,128]{1,0:T(8,128)S(1)} %pad_maximum_fusion.1), channel_id=1, source_target_pairs={{0,256},{8,264},{16,272},{24,280},{32,288},{40,296},{48,304},{56,3... | collective-permute-start | bytes 798728 | tf_op jit(solution)/shard_map/ppermute | solution.py:104
  78.6 10.0 %copy-start.1 = (bf16[512,4096]{1,0:T(8,128)(2,1)S(1)}, bf16[512,4096]{1,0:T(8,128)(2,1)}, u32[]{:S(2)}) copy-start(bf16[512,4096]{1,0:T(8,128)(2,1)} %param.13) | copy-start | bytes 12582916
  78.6 9.3 %collective-permute-start.8 = (f32[520,128]{1,0:T(8,128)S(1)}, f32[520,128]{1,0:T(8,128)S(1)}, u32[]{:S(2)}, u32[]{:S(2)}) collective-permute-start(f32[520,128]{1,0:T(8,128)S(1)} %pad_maximum_fusion.1), channel_id=1, source_target_pairs={{0,384},{8,392},{16,400},{24,408},{32,416},{40,424},{48,432},{56,4... | collective-permute-start | bytes 798728 | tf_op jit(solution)/shard_map/ppermute | solution.py:104
  79.4 8.4 %collective-permute-start.6 = (f32[520,128]{1,0:T(8,128)S(1)}, f32[520,128]{1,0:T(8,128)S(1)}, u32[]{:S(2)}, u32[]{:S(2)}) collective-permute-start(f32[520,128]{1,0:T(8,128)S(1)} %pad_maximum_fusion.1), channel_id=1, source_target_pairs={{0,128},{8,136},{16,144},{24,152},{32,160},{40,168},{48,176},{56,1... | collective-permute-start | bytes 798728 | tf_op jit(solution)/shard_map/ppermute | solution.py:104
  89.6 16.8 %copy-start.8 = (s32[128]{0:T(128)S(1)}, s32[128]{0:T(128)}, u32[]{:S(2)}) copy-start(s32[128]{0:T(128)} %param.14) | copy-start | bytes 1540
  89.6 4.6 %collective-permute-start.9 = (f32[4,128,512]{2,1,0:T(8,128)S(1)}, f32[4,128,512]{2,1,0:T(8,128)S(1)}, u32[]{:S(2)}, u32[]{:S(2)}) collective-permute-start(f32[4,128,512]{2,1,0:T(8,128)S(1)} %pad_maximum_fusion), channel_id=1, source_target_pairs={{0,1},{1,0},{2,3},{3,2},{4,5},{5,4},{6,7},{7,6},{8,9},{9,8},{10,11... | collective-permute-start | bytes 3145736 | tf_op jit(solution)/shard_map/ppermute | solution.py:124
  94.5 12.6 %collective-permute-start.10 = (f32[128,512]{1,0:T(8,128)S(1)}, f32[128,512]{1,0:T(8,128)S(1)}, u32[]{:S(2)}, u32[]{:S(2)}) collective-permute-start(f32[128,512]{1,0:T(8,128)S(1)} %get-tuple-element.46), channel_id=1, source_target_pairs={{0,4},{1,5},{2,6},{3,7},{4,0},{5,1},{6,2},{7,3},{8,12},{9,13},{10,... | collective-permute-start | bytes 786440 | tf_op jit(solution)/shard_map/ppermute | solution.py:129
  100.5 12.6 %collective-permute-start.11 = (f32[128,512]{1,0:T(8,128)S(1)}, f32[128,512]{1,0:T(8,128)S(1)}, u32[]{:S(2)}, u32[]{:S(2)}) collective-permute-start(f32[128,512]{1,0:T(8,128)S(1)} %get-tuple-element.48), channel_id=1, source_target_pairs={{0,6},{1,7},{2,0},{3,1},{4,2},{5,3},{6,4},{7,5},{8,14},{9,15},{10,... | collective-permute-start | bytes 786440 | tf_op jit(solution)/shard_map/ppermute | solution.py:129
  102.6 11.0 %collective-permute-start.12 = (f32[128,512]{1,0:T(8,128)S(1)}, f32[128,512]{1,0:T(8,128)S(1)}, u32[]{:S(2)}, u32[]{:S(2)}) collective-permute-start(f32[128,512]{1,0:T(8,128)S(1)} %get-tuple-element.47), channel_id=1, source_target_pairs={{0,2},{1,3},{2,4},{3,5},{4,6},{5,7},{6,0},{7,1},{8,10},{9,11},{10,... | collective-permute-start | bytes 786440 | tf_op jit(solution)/shard_map/ppermute | solution.py:129

commit v13 on v12

--- a/solution.py
+++ b/solution.py
@@ -118,13 +118,24 @@
         def block(index):
             return lax.dynamic_slice_in_dim(partial, index * width, width, 1)
 
-        keep = jnp.stack([block(2 * y + core) for y in range(chips)])
-        away = jnp.stack([block(2 * y + 1 - core) for y in range(chips)])
+        shifts = sorted(range(1, chips), key=lambda s: -min(s, chips - s))
         pairs = [(h, h ^ 1) for h in range(n)]
-        mine = keep + lax.ppermute(away, axis, pairs)
-        out = lax.dynamic_index_in_dim(mine, chip, 0, False)
-        for shift in sorted(range(1, chips), key=lambda s: (-min(s, chips - s), -s)):
-            send = lax.dynamic_index_in_dim(mine, (chip + shift) % chips, 0, False)
+        far = shifts[0]
+        near = [s for s in range(chips) if s != far]
+
+        def at(shift, parity):
+            return block(2 * ((chip + shift) % chips) + parity)
+
+        first = at(far, core) + lax.ppermute(at(far, 1 - core), axis, pairs)
+        keep = jnp.stack([at(s, core) for s in near])
+        away = jnp.stack([at(s, 1 - core) for s in near])
+        rest = keep + lax.ppermute(away, axis, pairs)
+        mine = {far: first}
+        for i, s in enumerate(near):
+            mine[s] = rest[i]
+        out = mine[0]
+        for shift in shifts:
+            send = mine[shift]
             pairs = [(2 * y + c, 2 * ((y + shift) % chips) + c) for y in range(chips) for c in range(2)]
             out = out + lax.ppermute(send, axis, pairs)
         return out

time: 115 us -> 116 us (level)
  the two profiles are of different devices: /device:TPU:66 before, /device:TPU:90 now
where the time goes in v13:
time: 116 us; the launch traced here: 115 us
  waiting for transfers between devices  70.8 us (61%)
  starting transfers between devices  30 us (26%)
  other arithmetic  5.53 us (5%)
  matrix products  4.16 us (4%)
  local copies, waits for them, and re-layouts  3.97 us (3%)
    ppermute x6, waiting for transfers between devices, exclusive_scan(): got = lax.ppermute(send, axis, full)  54.1 us
    ppermute x6, starting transfers between devices, exclusive_scan(): got = lax.ppermute(send, axis, full)  9.96 us
    ppermute x3, starting transfers between devices, scatter_heads(): out = out + lax.ppermute(send, axis, pairs)  9.15 us
    ppermute x3, waiting for transfers between devices, scatter_heads(): out = out + lax.ppermute(send, axis, pairs)  8.95 us
    ppermute x3, starting transfers between devices, exclusive_scan(): got = lax.ppermute(total, axis, pairs)  6.92 us
    ppermute x3, waiting for transfers between devices, exclusive_scan(): got = lax.ppermute(total, axis, pairs)  6.34 us
    reshape x3, local copies, waits for them, and re-layouts, split(): array.reshape(count, SPAN, heads_here, head_size).transpose(0, 2, 1, 3)  2.97 us
  transfers between devices with their start and end apart: 14, of which 10 were waited for; matrix products, arithmetic and copies ran while one was open for 4% of the time, Pallas kernels for 0%

profile of v13, /device:TPU:90, one launch (start us, length us, event | category | flops | bytes accessed | tf_op | source)
XLA Modules:
  0.0 115.4 jit_solution(8742495429806843344)
XLA Ops:
  0.0 1.0 reduce_window_sum.24
  1.3 1.0 copy.30
  2.3 1.0 reshape.189
  3.9 3.8 %collective-permute-start = (f32[520,128]{1,0:T(8,128)S(1)}, f32[520,128]{1,0:T(8,128)S(1)}, u32[]{:S(2)}, u32[]{:S(2)}) collective-permute-start(f32[520,128]{1,0:T(8,128)S(1)} %maximum_maximum_fusion), channel_id=1, source_target_pairs={{0,8},{16,24},{32,40},{48,56},{64,72},{80,88},{96,104},{112,120},{... | collective-permute-start | bytes 798728 | tf_op jit(solution)/shard_map/ppermute | solution.py:92
  7.7 6.4 %collective-permute-done = f32[520,128]{1,0:T(8,128)S(1)} collective-permute-done((f32[520,128]{1,0:T(8,128)S(1)}, f32[520,128]{1,0:T(8,128)S(1)}, u32[]{:S(2)}, u32[]{:S(2)}) %collective-permute-start) | collective-permute-done | bytes 266272 | tf_op jit(solution)/shard_map/ppermute | solution.py:92
  14.4 1.6 %collective-permute-start.1 = (f32[520,128]{1,0:T(8,128)S(1)}, f32[520,128]{1,0:T(8,128)S(1)}, u32[]{:S(2)}, u32[]{:S(2)}) collective-permute-start(f32[520,128]{1,0:T(8,128)S(1)} %maximum_select_fusion), channel_id=1, source_target_pairs={{8,24},{40,56},{72,88},{104,120},{112,96},{80,64},{48,32},{16,0},{... | collective-permute-start | bytes 798728 | tf_op jit(solution)/shard_map/ppermute | solution.py:92
  16.0 4.9 %collective-permute-done.1 = f32[520,128]{1,0:T(8,128)S(1)} collective-permute-done((f32[520,128]{1,0:T(8,128)S(1)}, f32[520,128]{1,0:T(8,128)S(1)}, u32[]{:S(2)}, u32[]{:S(2)}) %collective-permute-start.1) | collective-permute-done | bytes 266272 | tf_op jit(solution)/shard_map/ppermute | solution.py:92
  23.1 1.3 %collective-permute-start.4 = (f32[520,128]{1,0:T(8,128)S(1)}, f32[520,128]{1,0:T(8,128)}, u32[]{:S(2)}, u32[]{:S(2)}) collective-permute-start(f32[520,128]{1,0:T(8,128)S(1)} %maximum_select_fusion.3), channel_id=1, source_target_pairs={{24,40},{56,72},{88,104},{96,80},{64,48},{32,16},{152,168},{184,20... | collective-permute-start | bytes 798728 | tf_op jit(solution)/shard_map/ppermute | solution.py:92
  24.4 39.3 %collective-permute-done.4 = f32[520,128]{1,0:T(8,128)} collective-permute-done((f32[520,128]{1,0:T(8,128)S(1)}, f32[520,128]{1,0:T(8,128)}, u32[]{:S(2)}, u32[]{:S(2)}) %collective-permute-start.4) | collective-permute-done | bytes 266272 | tf_op jit(solution)/shard_map/ppermute | solution.py:92
  65.7 1.9 %collective-permute-start.5 = (f32[520,128]{1,0:T(8,128)}, f32[520,128]{1,0:T(8,128)S(1)}, u32[]{:S(2)}, u32[]{:S(2)}) collective-permute-start(f32[520,128]{1,0:T(8,128)} %maximum_select_fusion.4), channel_id=1, source_target_pairs={{8,16},{24,32},{40,48},{56,64},{72,80},{88,96},{104,112},{112,104}... | collective-permute-start | bytes 798728 | tf_op jit(solution)/shard_map/ppermute | solution.py:92
  68.6 2.1 %fusion.6 = f32[4,128,128]{1,2,0:T(8,128)} fusion(bf16[4,128,128]{1,2,0:T(8,128)(2,1)} %bitcast.150, f32[4,128]{1,0:T(4,128)S(1)} %reduce_window_sum.24, pred[128,128]{0,1:T(8,128)(4,1)S(1)} %iota_compare_fusion.1, bf16[1,128,4,128]{3,2,1,0:T(4,128)(2,1)} %copy-done.3, bf16[1,128,4,128]{3,2,1,0:T(4,128)(2,1)S(1)} %reshape.187), kind=kOutput, calls=%fused_computation.10 | convolution fusion | flops 33882112 | bytes 673792 | tf_op jit(solution)/shard_map/while/body/eval_jaxpr/hts,hse->hte/dot_general | solution.py:20
  70.7 3.5 %collective-permute-done.5 = f32[520,128]{1,0:T(8,128)S(1)} collective-permute-done((f32[520,128]{1,0:T(8,128)}, f32[520,128]{1,0:T(8,128)S(1)}, u32[]{:S(2)}, u32[]{:S(2)}) %collective-permute-start.5) | collective-permute-done | bytes 266272 | tf_op jit(solution)/shard_map/ppermute | solution.py:92
  74.6 4.0 %collective-permute-start.7 = (f32[520,128]{1,0:T(8,128)S(1)}, f32[520,128]{1,0:T(8,128)S(1)}, u32[]{:S(2)}, u32[]{:S(2)}) collective-permute-start(f32[520,128]{1,0:T(8,128)S(1)} %pad_maximum_fusion.1), channel_id=1, source_target_pairs={{0,256},{8,264},{16,272},{24,280},{32,288},{40,296},{48,304},{56,3... | collective-permute-start | bytes 798728 | tf_op jit(solution)/shard_map/ppermute | solution.py:104
  80.3 2.1 %collective-permute-start.6 = (f32[520,128]{1,0:T(8,128)S(1)}, f32[520,128]{1,0:T(8,128)S(1)}, u32[]{:S(2)}, u32[]{:S(2)}) collective-permute-start(f32[520,128]{1,0:T(8,128)S(1)} %pad_maximum_fusion.1), channel_id=1, source_target_pairs={{0,128},{8,136},{16,144},{24,152},{32,160},{40,168},{48,176},{56,1... | collective-permute-start | bytes 798728 | tf_op jit(solution)/shard_map/ppermute | solution.py:104
  82.6 6.1 %collective-permute-done.6 = f32[520,128]{1,0:T(8,128)S(1)} collective-permute-done((f32[520,128]{1,0:T(8,128)S(1)}, f32[520,128]{1,0:T(8,128)S(1)}, u32[]{:S(2)}, u32[]{:S(2)}) %collective-permute-start.6) | collective-permute-done | bytes 266272 | tf_op jit(solution)/shard_map/ppermute | solution.py:104
  90.2 1.9 %collective-permute-start.10 = (f32[128,512]{1,0:T(8,128)S(1)}, f32[128,512]{1,0:T(8,128)S(1)}, u32[]{:S(2)}, u32[]{:S(2)}) collective-permute-start(f32[128,512]{1,0:T(8,128)S(1)} %constant_dynamic-slice_fusion), channel_id=1, source_target_pairs={{0,1},{1,0},{2,3},{3,2},{4,5},{5,4},{6,7},{7,6},{8,9},{9,8},{10,11... | collective-permute-start | bytes 786440 | tf_op jit(solution)/shard_map/ppermute | solution.py:129
  92.3 1.4 %collective-permute-done.10 = f32[128,512]{1,0:T(8,128)S(1)} collective-permute-done((f32[128,512]{1,0:T(8,128)S(1)}, f32[128,512]{1,0:T(8,128)S(1)}, u32[]{:S(2)}, u32[]{:S(2)}) %collective-permute-start.10) | collective-permute-done | bytes 262176 | tf_op jit(solution)/shard_map/ppermute | solution.py:129
  94.0 2.0 %collective-permute-start.9 = (f32[3,128,512]{2,1,0:T(8,128)S(1)}, f32[3,128,512]{2,1,0:T(8,128)S(1)}, u32[]{:S(2)}, u32[]{:S(2)}) collective-permute-start(f32[3,128,512]{2,1,0:T(8,128)S(1)} %pad_maximum_fusion), channel_id=1, source_target_pairs={{0,1},{1,0},{2,3},{3,2},{4,5},{5,4},{6,7},{7,6},{8,9},{9,8},{10,11... | collective-permute-start | bytes 2359304 | tf_op jit(solution)/shard_map/ppermute | solution.py:132
  96.0 2.2 %collective-permute-start.11 = (f32[128,512]{1,0:T(8,128)S(1)}, f32[128,512]{1,0:T(8,128)S(1)}, u32[]{:S(2)}, u32[]{:S(2)}) collective-permute-start(f32[128,512]{1,0:T(8,128)S(1)} %get-tuple-element.38), channel_id=1, source_target_pairs={{0,4},{1,5},{2,6},{3,7},{4,0},{5,1},{6,2},{7,3},{8,12},{9,13},{10,... | collective-permute-start | bytes 786440 | tf_op jit(solution)/shard_map/ppermute | solution.py:140
  98.5 5.0 %collective-permute-start.12 = (f32[128,512]{1,0:T(8,128)S(1)}, f32[128,512]{1,0:T(8,128)S(1)}, u32[]{:S(2)}, u32[]{:S(2)}) collective-permute-start(f32[128,512]{1,0:T(8,128)S(1)} %get-tuple-element.45), channel_id=1, source_target_pairs={{0,2},{1,3},{2,4},{3,5},{4,6},{5,7},{6,0},{7,1},{8,10},{9,11},{10,... | collective-permute-start | bytes 786440 | tf_op jit(solution)/shard_map/ppermute | solution.py:140
  103.5 1.9 %collective-permute-start.13 = (f32[128,512]{1,0:T(8,128)S(1)}, f32[128,512]{1,0:T(8,128)S(1)}, u32[]{:S(2)}, u32[]{:S(2)}) collective-permute-start(f32[128,512]{1,0:T(8,128)S(1)} %get-tuple-element.46), channel_id=1, source_target_pairs={{0,6},{1,7},{2,0},{3,1},{4,2},{5,3},{6,4},{7,5},{8,14},{9,15},{10,... | collective-permute-start | bytes 786440 | tf_op jit(solution)/shard_map/ppermute | solution.py:140
  105.7 2.4 %collective-permute-done.11 = f32[128,512]{1,0:T(8,128)S(1)} collective-permute-done((f32[128,512]{1,0:T(8,128)S(1)}, f32[128,512]{1,0:T(8,128)S(1)}, u32[]{:S(2)}, u32[]{:S(2)}) %collective-permute-start.11) | collective-permute-done | bytes 262176 | tf_op jit(solution)/shard_map/ppermute | solution.py:140
  108.1 3.0 %collective-permute-done.12 = f32[128,512]{1,0:T(8,128)S(1)} collective-permute-done((f32[128,512]{1,0:T(8,128)S(1)}, f32[128,512]{1,0:T(8,128)S(1)}, u32[]{:S(2)}, u32[]{:S(2)}) %collective-permute-start.12) | collective-permute-done | bytes 262176 | tf_op jit(solution)/shard_map/ppermute | solution.py:140
  111.1 3.5 %collective-permute-done.13 = f32[128,512]{1,0:T(8,128)S(1)} collective-permute-done((f32[128,512]{1,0:T(8,128)S(1)}, f32[128,512]{1,0:T(8,128)S(1)}, u32[]{:S(2)}, u32[]{:S(2)}) %collective-permute-start.13) | collective-permute-done | bytes 262176 | tf_op jit(solution)/shard_map/ppermute | solution.py:140
  (117 shorter events, 10.9 us)
Async XLA Ops:
  0.0 105.4 %copy-start = (bf16[16,512]{1,0:T(8,128)(2,1)S(1)}, bf16[16,512]{1,0:T(8,128)(2,1)}, u32[]{:S(2)}) copy-start(bf16[16,512]{1,0:T(8,128)(2,1)} %param.15) | copy-start | bytes 49156
  2.3 11.8 %copy-start.2 = (bf16[128,512]{0,1:T(8,128)(2,1)}, bf16[128,512]{0,1:T(8,128)(2,1)S(1)}, u32[]{:S(2)}) copy-start(bf16[128,512]{0,1:T(8,128)(2,1)S(1)} %copy.30) | copy-start | bytes 393220
  3.3 10.8 %copy-start.3 = (bf16[1,128,4,128]{3,2,1,0:T(4,128)(2,1)}, bf16[1,128,4,128]{3,2,1,0:T(4,128)(2,1)S(1)}, u32[]{:S(2)}) copy-start(bf16[1,128,4,128]{3,2,1,0:T(4,128)(2,1)S(1)} %reshape.189) | copy-start | bytes 393220
  3.9 10.2 %collective-permute-start = (f32[520,128]{1,0:T(8,128)S(1)}, f32[520,128]{1,0:T(8,128)S(1)}, u32[]{:S(2)}, u32[]{:S(2)}) collective-permute-start(f32[520,128]{1,0:T(8,128)S(1)} %maximum_maximum_fusion), channel_id=1, source_target_pairs={{0,8},{16,24},{32,40},{48,56},{64,72},{80,88},{96,104},{112,120},{... | collective-permute-start | bytes 798728 | tf_op jit(solution)/shard_map/ppermute | solution.py:92
  14.4 6.5 %collective-permute-start.1 = (f32[520,128]{1,0:T(8,128)S(1)}, f32[520,128]{1,0:T(8,128)S(1)}, u32[]{:S(2)}, u32[]{:S(2)}) collective-permute-start(f32[520,128]{1,0:T(8,128)S(1)} %maximum_select_fusion), channel_id=1, source_target_pairs={{8,24},{40,56},{72,88},{104,120},{112,96},{80,64},{48,32},{16,0},{... | collective-permute-start | bytes 798728 | tf_op jit(solution)/shard_map/ppermute | solution.py:92
  21.2 0.7 collective-permute-start.2
  22.1 0.7 collective-permute-start.3
  23.1 40.6 %collective-permute-start.4 = (f32[520,128]{1,0:T(8,128)S(1)}, f32[520,128]{1,0:T(8,128)}, u32[]{:S(2)}, u32[]{:S(2)}) collective-permute-start(f32[520,128]{1,0:T(8,128)S(1)} %maximum_select_fusion.3), channel_id=1, source_target_pairs={{24,40},{56,72},{88,104},{96,80},{64,48},{32,16},{152,168},{184,20... | collective-permute-start | bytes 798728 | tf_op jit(solution)/shard_map/ppermute | solution.py:92
  64.9 14.2 %copy-start.6 = (f32[128,4]{0,1:T(4,128)S(1)}, f32[128,4]{0,1:T(4,128)}, u32[]{:S(2)}) copy-start(f32[128,4]{0,1:T(4,128)} %param.11) | copy-start | bytes 6148
  65.7 8.5 %collective-permute-start.5 = (f32[520,128]{1,0:T(8,128)}, f32[520,128]{1,0:T(8,128)S(1)}, u32[]{:S(2)}, u32[]{:S(2)}) collective-permute-start(f32[520,128]{1,0:T(8,128)} %maximum_select_fusion.4), channel_id=1, source_target_pairs={{8,16},{24,32},{40,48},{56,64},{72,80},{88,96},{104,112},{112,104}... | collective-permute-start | bytes 798728 | tf_op jit(solution)/shard_map/ppermute | solution.py:92
  68.6 20.3 %copy-start.4 = (bf16[128,512]{1,0:T(8,128)(2,1)S(1)}, bf16[128,512]{1,0:T(8,128)(2,1)}, u32[]{:S(2)}) copy-start(bf16[128,512]{1,0:T(8,128)(2,1)} %param.8) | copy-start | bytes 393220
  70.7 8.0 %copy-start.5 = (f32[4,128,128]{1,2,0:T(8,128)S(1)}, f32[4,128,128]{1,2,0:T(8,128)}, u32[]{:S(2)}) copy-start(f32[4,128,128]{1,2,0:T(8,128)} %fusion.6) | copy-start | bytes 786436
  74.3 15.0 %copy-start.7 = (f32[512]{0:T(512)S(1)}, f32[512]{0:T(512)}, u32[]{:S(2)}) copy-start(f32[512]{0:T(512)} %param.12) | copy-start | bytes 6148
  74.6 8.0 %collective-permute-start.7 = (f32[520,128]{1,0:T(8,128)S(1)}, f32[520,128]{1,0:T(8,128)S(1)}, u32[]{:S(2)}, u32[]{:S(2)}) collective-permute-start(f32[520,128]{1,0:T(8,128)S(1)} %pad_maximum_fusion.1), channel_id=1, source_target_pairs={{0,256},{8,264},{16,272},{24,280},{32,288},{40,296},{48,304},{56,3... | collective-permute-start | bytes 798728 | tf_op jit(solution)/shard_map/ppermute | solution.py:104
  79.5 10.0 %copy-start.1 = (bf16[512,4096]{1,0:T(8,128)(2,1)S(1)}, bf16[512,4096]{1,0:T(8,128)(2,1)}, u32[]{:S(2)}) copy-start(bf16[512,4096]{1,0:T(8,128)(2,1)} %param.13) | copy-start | bytes 12582916
  79.5 9.3 %collective-permute-start.8 = (f32[520,128]{1,0:T(8,128)S(1)}, f32[520,128]{1,0:T(8,128)S(1)}, u32[]{:S(2)}, u32[]{:S(2)}) collective-permute-start(f32[520,128]{1,0:T(8,128)S(1)} %pad_maximum_fusion.1), channel_id=1, source_target_pairs={{0,384},{8,392},{16,400},{24,408},{32,416},{40,424},{48,432},{56,4... | collective-permute-start | bytes 798728 | tf_op jit(solution)/shard_map/ppermute | solution.py:104
  80.3 8.4 %collective-permute-start.6 = (f32[520,128]{1,0:T(8,128)S(1)}, f32[520,128]{1,0:T(8,128)S(1)}, u32[]{:S(2)}, u32[]{:S(2)}) collective-permute-start(f32[520,128]{1,0:T(8,128)S(1)} %pad_maximum_fusion.1), channel_id=1, source_target_pairs={{0,128},{8,136},{16,144},{24,152},{32,160},{40,168},{48,176},{56,1... | collective-permute-start | bytes 798728 | tf_op jit(solution)/shard_map/ppermute | solution.py:104
  90.2 3.4 %collective-permute-start.10 = (f32[128,512]{1,0:T(8,128)S(1)}, f32[128,512]{1,0:T(8,128)S(1)}, u32[]{:S(2)}, u32[]{:S(2)}) collective-permute-start(f32[128,512]{1,0:T(8,128)S(1)} %constant_dynamic-slice_fusion), channel_id=1, source_target_pairs={{0,1},{1,0},{2,3},{3,2},{4,5},{5,4},{6,7},{7,6},{8,9},{9,8},{10,11... | collective-permute-start | bytes 786440 | tf_op jit(solution)/shard_map/ppermute | solution.py:129
  92.3 13.2 %copy-start.8 = (s32[128]{0:T(128)S(1)}, s32[128]{0:T(128)}, u32[]{:S(2)}) copy-start(s32[128]{0:T(128)} %param.14) | copy-start | bytes 1540
  94.0 4.3 %collective-permute-start.9 = (f32[3,128,512]{2,1,0:T(8,128)S(1)}, f32[3,128,512]{2,1,0:T(8,128)S(1)}, u32[]{:S(2)}, u32[]{:S(2)}) collective-permute-start(f32[3,128,512]{2,1,0:T(8,128)S(1)} %pad_maximum_fusion), channel_id=1, source_target_pairs={{0,1},{1,0},{2,3},{3,2},{4,5},{5,4},{6,7},{7,6},{8,9},{9,8},{10,11... | collective-permute-start | bytes 2359304 | tf_op jit(solution)/shard_map/ppermute | solution.py:132
  96.0 12.1 %collective-permute-start.11 = (f32[128,512]{1,0:T(8,128)S(1)}, f32[128,512]{1,0:T(8,128)S(1)}, u32[]{:S(2)}, u32[]{:S(2)}) collective-permute-start(f32[128,512]{1,0:T(8,128)S(1)} %get-tuple-element.38), channel_id=1, source_target_pairs={{0,4},{1,5},{2,6},{3,7},{4,0},{5,1},{6,2},{7,3},{8,12},{9,13},{10,... | collective-permute-start | bytes 786440 | tf_op jit(solution)/shard_map/ppermute | solution.py:140
  98.5 12.6 %collective-permute-start.12 = (f32[128,512]{1,0:T(8,128)S(1)}, f32[128,512]{1,0:T(8,128)S(1)}, u32[]{:S(2)}, u32[]{:S(2)}) collective-permute-start(f32[128,512]{1,0:T(8,128)S(1)} %get-tuple-element.45), channel_id=1, source_target_pairs={{0,2},{1,3},{2,4},{3,5},{4,6},{5,7},{6,0},{7,1},{8,10},{9,11},{10,... | collective-permute-start | bytes 786440 | tf_op jit(solution)/shard_map/ppermute | solution.py:140
  103.5 11.1 %collective-permute-start.13 = (f32[128,512]{1,0:T(8,128)S(1)}, f32[128,512]{1,0:T(8,128)S(1)}, u32[]{:S(2)}, u32[]{:S(2)}) collective-permute-start(f32[128,512]{1,0:T(8,128)S(1)} %get-tuple-element.46), channel_id=1, source_target_pairs={{0,6},{1,7},{2,0},{3,1},{4,2},{5,3},{6,4},{7,5},{8,14},{9,15},{10,... | collective-permute-start | bytes 786440 | tf_op jit(solution)/shard_map/ppermute | solution.py:140
